TPU v7x, 512 devices: a whole 4x8x8 slice. The times are simulated.
512 devices in a mesh: area: 16 (over y, z_lo), tm: 32 (over z_hi, x, core).
Axes of the slice: x: 4, y: 8, z: 8 (z_hi: 4, z_lo: 2; z = z_hi * 2 + z_lo), core: 2. Of those that a mesh axis runs over, the one named last changes fastest.
Arguments:
- angle_start: bfloat16 [16, 2176, 4096], P('area', None, 'tm'), may hold values from -6 to 6
- dispatch_start: bfloat16 [16, 2176, 4096], P('area', None, 'tm'), may hold values from -6 to 6
- demand: bfloat16 [16, 2176, 4096], P('area', None, 'tm'), may hold values from -6 to 6
- price_start: bfloat16 [16, 8, 128, 4096], P('area', None, None, 'tm'), may hold values from -6 to 6
- susceptance: bfloat16 [16, 2176, 2176], P('area'), may hold values from -0.5 to 3.5
- tile_inverse: bfloat16 [16, 34, 64, 64], P('area'), may hold values from -0.1 to 0.3
- cost_slope: float32 [16, 2176], P('area'), may hold values from 0.2 to 2
- ramp_weight: float32 [16, 2176], P('area'), may hold values from 0.1 to 0.4
- partner: int32 [8, 16], replicated, may hold values from 0 to 15, as said below
- boundary: int32 [16, 8, 128], P('area'), may hold values from 0 to 2175
- tie_susceptance: float32 [16, 8, 128], P('area'), may hold values from 0.5 to 2
- tie_penalty: float32 [16, 8, 128], P('area'), may hold values from 0.2 to 1
- store_bus: int32 [16, 128], P('area'), may hold values from 0 to 2175
- store_gain: float32 [16, 128], P('area'), may hold values from 0.5 to 2
- store_output: float32 [16, 128], P('area'), may hold values from 0.5 to 1.5
- retention: float32 [16, 128, 4096], P('area', None, 'tm'), may hold values from 0.45 to 1
Outputs:
- angles: float32 [16, 2176, 4096], P('area', None, 'tm')
- dispatch: bfloat16 [16, 2176, 4096], P('area', None, 'tm')
- prices: float32 [16, 8, 128, 4096], P('area', None, None, 'tm')
- charge_state: float32 [16, 128, 4096], P('area', None, 'tm')
Inputs may be any that keep to these rules, and one draw needn't show every extreme that they name: partner[r, partner[r, a]] = a and partner[r, a] != a; the 8 partners of an area are all different.
All inputs are finite; a program needn't handle non-finite values.
Results may differ from a plain program's by a relative error of at most 0.0061.
Values sent between devices are 32-bit elements; how exact they have to be, the bound alone decides.
No kernel may reach another device: no remote copies, remote signals or barrier semaphores. Data moves between devices by JAX's collectives and lax.ppermute only.
A program may use at most 128 MiB of HBM per device.

v0:
```python
import math

import jax
import jax.numpy as jnp
from jax import lax
from jax.experimental import pallas as pl
from jax.experimental.pallas import tpu as pltpu
from jax.sharding import PartitionSpec as P

ITERS = 2


dispatch_step = 0.5


def padded_2(x, sides, width):
    for axis, dim in sides:
        size, length = (lax.axis_size(axis), x.shape[dim])
        up = [(i, (i + 1) % size) for i in range(size - 1)]
        down = [(j, i) for i, j in up]
        last = lax.slice_in_dim(x, length - width, length, axis=dim)
        leading = lax.slice_in_dim(x, 0, width, axis=dim)
        before = lax.ppermute(last, axis, up)
        after = lax.ppermute(leading, axis, down)
        x = jnp.concatenate([before, x, after], axis=dim)
    return x


def shifted_in(x, lane, step, fill):
    count = x.shape[1]
    ahead = pltpu.roll(x, step, 1)
    behind = pltpu.roll(x, count - step, 1)
    source = pltpu.roll(lane, step, 1)
    moved = jnp.where(source == lane - step, ahead, behind)
    return jnp.where(lane >= step, moved, fill)


def scan_kernel(kept_ref, charge_ref, total_ref, state_ref):
    kept = kept_ref[...]
    state = charge_ref[...]
    lane = lax.broadcasted_iota(jnp.int32, kept.shape, 1)
    step = 1
    while step < kept.shape[1]:
        state = kept * shifted_in(state, lane, step, 0.0) + state
        kept = kept * shifted_in(kept, lane, step, 1.0)
        step *= 2
    total_ref[...] = kept
    state_ref[...] = state


def window_scan(kept, charge):
    shape = jax.ShapeDtypeStruct(kept.shape, jnp.float32)
    return pl.pallas_call(scan_kernel, out_shape=(shape, shape))(kept, charge)


def carried_state(kept_last, state_last, position):
    state_in = jnp.zeros_like(state_last[0])
    for window in range(state_last.shape[0]):
        folded = kept_last[window] * state_in + state_last[window]
        state_in = jnp.where(window < position, folded, state_in)
    return state_in


def local(
    angle_start,
    dispatch_start,
    demand,
    price_start,
    susceptance,
    tile_inverse,
    cost_slope,
    ramp_weight,
    partner,
    boundary,
    tie_susceptance,
    tie_penalty,
    store_bus,
    store_gain,
    store_output,
    retention,
):
    area_count = lax.axis_size("area")
    area_here = lax.axis_index("area")
    position = lax.axis_index("tm")
    partners = jnp.take(partner, area_here, axis=1)
    edge_rows = boundary[0]
    store_rows = store_bus[0]
    matrix = susceptance[0]
    inverses = tile_inverse[0]
    tile_count = inverses.shape[0]
    tile_width = inverses.shape[1]
    bus_count = matrix.shape[0]
    hour_count = retention.shape[2]
    year_hours = hour_count * lax.axis_size("tm")
    kept_local = retention[0]
    angle_now = angle_start[0].astype(jnp.float32)
    dispatch = dispatch_start[0].astype(jnp.float32)
    price_now = price_start[0].astype(jnp.float32)
    demand_local = demand[0].astype(jnp.float32)
    tie_gain = tie_susceptance[0][:, :, None]
    penalty = tie_penalty[0][:, :, None]
    slope = cost_slope[0][:, None]
    ramp_local = ramp_weight[0][:, None]
    gain_local = store_gain[0][:, None]
    output_local = store_output[0][:, None]
    injection = jnp.zeros((bus_count, hour_count), jnp.float32)
    charge_state = jnp.zeros_like(kept_local)
    rounds, lines = edge_rows.shape

    def exchanged(parts):
        flat = jnp.concatenate([part.reshape(rounds, -1) for part in parts], axis=1)
        blank = jnp.zeros((area_count, flat.shape[1]), flat.dtype)
        sent = blank.at[partners].set(flat)
        got = lax.all_to_all(sent, "area", split_axis=0, concat_axis=0, tiled=True)
        got = jnp.take(got, partners, axis=0)
        found, at = [], 0
        for part in parts:
            width = part.size // rounds
            found.append(got[:, at : at + width].reshape(part.shape))
            at += width
        return found

    kept_total = None
    kept_last = None
    price_far = None
    penalty_far = None
    mismatch = None
    for iteration in range(ITERS):
        rounded = angle_now.astype(jnp.bfloat16)
        own_edge = rounded[edge_rows].astype(jnp.float32)
        if iteration == 0:
            far_edge, price_far, penalty_far = exchanged((own_edge, price_now, tie_penalty[0]))
            penalty_far = penalty_far[:, :, None]
        else:
            (far_edge,) = exchanged((own_edge,))
            price_far = price_far - penalty_far * mismatch
        mismatch = own_edge - far_edge
        tie_flow = tie_gain * mismatch + 0.5 * (price_now - price_far)
        spread = jnp.zeros((bus_count, hour_count), jnp.float32).at[edge_rows].add(tie_flow)
        fixed_part = demand_local - dispatch - injection + spread
        balance = jnp.dot(matrix, rounded, preferred_element_type=jnp.float32) + fixed_part
        padded = padded_2(dispatch, (("tm", 1),), 1)
        bend = padded[:, :-2] - 2.0 * dispatch + padded[:, 2:]
        dispatch_next = dispatch + dispatch_step * (balance - slope * dispatch) + ramp_local * bend
        charge = -gain_local * balance[store_rows] / math.sqrt(year_hours)
        kept_total, local_state = window_scan(kept_local, charge)
        if kept_last is None:
            kept_last = lax.all_gather(kept_total[:, -1], "tm", axis=0)
        state_last = lax.all_gather(local_state[:, -1], "tm", axis=0)
        state_in = carried_state(kept_last, state_last, position)
        charge_state = local_state + kept_total * state_in[:, None]
        injection = (
            jnp.zeros((bus_count, hour_count), jnp.float32)
            .at[store_rows]
            .add(output_local * charge_state)
        )
        sweep_rows = balance.astype(jnp.bfloat16).reshape(tile_count, tile_width, hour_count)
        correction = jnp.einsum(
            "tij,tjh->tih", inverses, sweep_rows, preferred_element_type=jnp.float32
        )
        angle_now = angle_now - correction.reshape(bus_count, hour_count)
        price_now = price_now + penalty * mismatch
        dispatch = dispatch_next
    return (
        angle_now[None],
        dispatch.astype(jnp.bfloat16)[None],
        price_now[None],
        charge_state[None],
    )


def solution(mesh):
    in_specs = (
        P("area", None, "tm"),
        P("area", None, "tm"),
        P("area", None, "tm"),
        P("area", None, None, "tm"),
        P("area", None, None),
        P("area", None, None, None),
        P("area", None),
        P("area", None),
        P(),
        P("area", None, None),
        P("area", None, None),
        P("area", None, None),
        P("area", None),
        P("area", None),
        P("area", None),
        P("area", None, "tm"),
    )
    out_specs = (
        P("area", None, "tm"),
        P("area", None, "tm"),
        P("area", None, None, "tm"),
        P("area", None, "tm"),
    )
    return jax.shard_map(local, mesh=mesh, in_specs=in_specs, out_specs=out_specs, check_vma=False)
```

profile of v0, /device:TPU:1, one launch (start us, length us, event | category | flops | bytes accessed | tf_op | source)
XLA Modules:
  0.0 326.8 jit_solution(3788896446341759666)
XLA Ops:
  1.4 4.0 %gather_fusion = bf16[1024,128]{1,0:T(8,128)(2,1)S(1)} fusion(bf16[2176,128]{1,0:T(8,128)(2,1)} %bitcast.127, s32[1024]{0:T(1024)S(1)} %broadcast_clamp_fusion), kind=kCustom, calls=%fused_computation | custom fusion | bytes 528384 | tf_op jit(solution)/shard_map/gather | solution.py:130
  6.5 1.0 pad_maximum_fusion.4
  7.5 2.3 scatter_custom_fusion
  9.9 2.8 all_to_all.16
  12.6 9.7 %all-to-all-start = ((f32[16,1,32896]{2,1,0:T(1,128)}), f32[16,1,32896]{2,1,0:T(1,128)}, u32[]{:S(2)}, u32[]{:S(2)}) async-start(f32[16,1,32896]{2,1,0:T(1,128)} %all_to_all.16), calls=%async_computation | async-start | bytes 4210688 | tf_op jit(solution)/shard_map/all_to_all | solution.py:114
  23.8 4.1 %collective-permute-start = (f32[2176,1]{0,1:T(1,128)S(1)}, f32[2176,1]{0,1:T(1,128)S(1)}, u32[]{:S(2)}, u32[]{:S(2)}) collective-permute-start(f32[2176,1]{0,1:T(1,128)S(1)} %copy.37), channel_id=1, source_target_pairs={{0,1},{1,2},{2,3},{3,4},{4,5},{5,6},{6,7},{7,8},{8,9},{9,10},{10,1... | collective-permute-start | bytes 26120 | tf_op jit(solution)/shard_map/ppermute | solution.py:23
  28.3 1.9 collective-permute-start.1
  30.4 7.4 %fusion.10 = f32[2176,128]{1,0:T(8,128)} fusion(bf16[1,2176,2176]{2,1,0:T(8,128)(2,1)} %param.20, bf16[1,2176,128]{2,1,0:T(8,128)(2,1)S(1)} %copy-done.23, bf16[1,2176,128]{2,1,0:T(8,128)(2,1)S(1)} %copy-done.25, bf16[1,2176,128]{2,1,0:T(8,128)(2,1)S(1)} %copy-done.2), kind=kOutput, calls=%fused_computation.17 | convolution fusion | flops 1213267968 | bytes 12255232 | tf_op jit(solution)/shard_map/dot_general | solution.py:141
  38.8 1.4 copy.38
  40.2 1.4 copy.40
  41.6 28.9 %all-to-all-done = f32[16,1,32896]{2,1,0:T(1,128)} async-done(((f32[16,1,32896]{2,1,0:T(1,128)}), f32[16,1,32896]{2,1,0:T(1,128)}, u32[]{:S(2)}, u32[]{:S(2)}) %all-to-all-start) | async-done | bytes 2105376 | tf_op jit(solution)/shard_map/all_to_all | solution.py:114
  70.5 1.7 copy.82
  72.3 1.8 gather_fusion.1
  74.1 1.4 broadcast_select_fusion
  78.4 6.6 %scatter_fusion = f32[2176,128]{1,0:T(8,128)S(1)} fusion(f32[2176,128]{1,0:T(8,128)S(1)} %copy-done.1, s32[1024]{0:T(1024)S(1)} %fusion.60, f32[1024,128]{1,0:T(8,128)S(1)} %bitcast.140), kind=kCustom, calls=%fused_computation.7 | custom fusion | flops 131072 | bytes 1576960 | tf_op jit(solution)/shard_map/scatter-add | solution.py:139
  85.0 3.9 %fusion.21 = (f32[2176,128]{1,0:T(8,128)S(1)}, bf16[2176,128]{1,0:T(8,128)(2,1)S(1)}) fusion(f32[2176,1]{1,0:T(8,128)} %copy.40, f32[2176,128]{1,0:T(8,128)} %copy-done.3, f32[2176,1]{1,0:T(8,128)} %copy.38, f32[2176,128]{1,0:T(8,128)S(1)} %scatter_fusion, bf16[1,2176,128]{2,1,0:T(8,128)(2,1)} %param.17, f32[2176]{0:T(1024)S(1)} %reduce.3, f32[2176]{0:T(1024)S(1)} %reduce.2), kind=kLoop, calls=%fused_computation.32 | loop fusion | flops 3620864 | bytes 4491264 | tf_op jit(solution)/shard_map/add | solution.py:144
  88.9 1.1 fusion.26
  90.0 1.0 copy-done.4
  91.9 5.2 %gather_fusion.3 = bf16[1024,128]{1,0:T(8,128)(2,1)} fusion(bf16[2176,128]{1,0:T(8,128)(2,1)} %fusion.23, s32[1024]{0:T(1024)S(1)} %broadcast_clamp_fusion), kind=kCustom, calls=%fused_computation.3 | custom fusion | bytes 528384 | tf_op jit(solution)/shard_map/gather | solution.py:130
  97.1 1.8 reshape.1048
  98.9 2.4 scatter_custom_fusion.3
  101.3 3.4 %all_to_all.19 = f32[16,1,16384]{2,1,0:T(1,128)} reshape(f32[16,16384]{1,0:T(8,128)} %scatter_custom_fusion.3) | data formatting | bytes 2097152 | tf_op jit(solution)/shard_map/all_to_all | solution.py:114
  104.6 6.2 %all-to-all-start.1 = ((f32[16,1,16384]{2,1,0:T(1,128)}), f32[16,1,16384]{2,1,0:T(1,128)}, u32[]{:S(2)}, u32[]{:S(2)}) async-start(f32[16,1,16384]{2,1,0:T(1,128)} %all_to_all.19), calls=%async_computation.1 | async-start | bytes 2097152 | tf_op jit(solution)/shard_map/all_to_all | solution.py:114
  112.3 2.3 shard_map.183
  114.5 0.9 slice.372
  115.5 0.9 slice.405
  116.4 1.4 fusion.65
  117.7 1.6 copy.43
  119.3 4.7 %collective-permute-start.2 = (f32[2176,1]{0,1:T(1,128)S(1)}, f32[2176,1]{0,1:T(1,128)S(1)}, u32[]{:S(2)}, u32[]{:S(2)}) collective-permute-start(f32[2176,1]{0,1:T(1,128)S(1)} %copy.43), channel_id=1, source_target_pairs={{0,1},{1,2},{2,3},{3,4},{4,5},{5,6},{6,7},{7,8},{8,9},{9,10},{10,1... | collective-permute-start | bytes 26120 | tf_op jit(solution)/shard_map/ppermute | solution.py:23
  124.4 1.9 collective-permute-start.3
  126.3 57.6 %all-gather = f32[4096,1]{1,0:T(8,128)S(1)} all-gather(f32[128,1]{1,0:T(8,128)S(1)} %slice.372), channel_id=2, replica_groups=mesh['area'=16,'tm'=32] {'tm'}, dimensions={0}, use_global_device_ids=true | all-gather | bytes 16896 | tf_op jit(solution)/shard_map/all_gather | solution.py:148
  183.9 50.0 %all-gather.1 = f32[4096,1]{1,0:T(8,128)S(1)} all-gather(f32[128,1]{1,0:T(8,128)S(1)} %slice.405), channel_id=3, replica_groups=mesh['area'=16,'tm'=32] {'tm'}, dimensions={0}, use_global_device_ids=true | all-gather | bytes 16896 | tf_op jit(solution)/shard_map/all_gather | solution.py:149
  235.7 2.2 scatter_custom_fusion.2
  238.0 7.0 %fusion.7 = f32[2176,128]{1,0:T(8,128)S(1)} fusion(bf16[2176,128]{1,0:T(8,128)(2,1)} %bitcast.136, bf16[1,2176,2176]{2,1,0:T(8,128)(2,1)} %param.20, f32[2176,128]{1,0:T(8,128)} %scatter_custom_fusion.2, f32[2176,128]{1,0:T(8,128)S(1)} %get-tuple-element.124, bf16[1,2176,128]{2,1,0:T(8,128)(2,1)} %param.18), kind=kOutput, calls=%fused_computation.16 | convolution fusion | flops 1213267968 | bytes 13926400 | tf_op jit(solution)/shard_map/dot_general | solution.py:141
  245.9 1.5 copy.44
  247.4 2.1 copy.46
  249.5 2.9 copy.83
  252.4 2.9 gather_fusion.4
  255.3 3.0 fusion.42
  258.4 7.1 %scatter_fusion.1 = f32[2176,128]{1,0:T(8,128)S(1)} fusion(f32[2176,128]{1,0:T(8,128)S(1)} %fusion.7, s32[1024]{0:T(1024)S(1)} %fusion.60, f32[1024,128]{1,0:T(8,128)} %bitcast.139), kind=kCustom, calls=%fused_computation.10 | custom fusion | flops 131072 | bytes 1576960 | tf_op jit(solution)/shard_map/scatter-add | solution.py:139
  266.8 2.3 shard_map.184
  269.1 0.9 slice.443
  270.0 48.0 %all-gather.2 = f32[4096,1]{1,0:T(8,128)S(1)} all-gather(f32[128,1]{1,0:T(8,128)S(1)} %slice.443), channel_id=4, replica_groups=mesh['area'=16,'tm'=32] {'tm'}, dimensions={0}, use_global_device_ids=true | all-gather | bytes 16896 | tf_op jit(solution)/shard_map/all_gather | solution.py:149
  318.0 1.2 fusion.52
  319.7 2.4 fusion.37
  322.3 0.9 copy-done.5
  323.5 1.1 bitcast_subtract_fusion
  325.6 1.2 fusion.43
  (189 shorter events, 15.5 us)
Async XLA Ops:
  0.6 88.3 %copy-start = (bf16[1,34,64,64]{3,2,1,0:T(8,128)(2,1)S(1)}, bf16[1,34,64,64]{3,2,1,0:T(8,128)(2,1)}, u32[]{:S(2)}) copy-start(bf16[1,34,64,64]{3,2,1,0:T(8,128)(2,1)} %param.21) | copy-start | bytes 835588
  1.4 4.2 %copy-start.16 = (bf16[1,8,128,128]{3,2,1,0:T(8,128)(2,1)S(1)}, bf16[1,8,128,128]{3,2,1,0:T(8,128)(2,1)}, u32[]{:S(2)}) copy-start(bf16[1,8,128,128]{3,2,1,0:T(8,128)(2,1)} %param.19) | copy-start | bytes 786436
  12.6 9.8 %copy-start.22 = (bf16[1,2176,128]{2,1,0:T(8,128)(2,1)S(1)}, bf16[1,2176,128]{2,1,0:T(8,128)(2,1)}, u32[]{:S(2)}) copy-start(bf16[1,2176,128]{2,1,0:T(8,128)(2,1)} %param.17) | copy-start | bytes 1671172
  12.6 57.9 %all-to-all-start = ((f32[16,1,32896]{2,1,0:T(1,128)}), f32[16,1,32896]{2,1,0:T(1,128)}, u32[]{:S(2)}, u32[]{:S(2)}) async-start(f32[16,1,32896]{2,1,0:T(1,128)} %all_to_all.16), calls=%async_computation | async-start | bytes 4210688 | tf_op jit(solution)/shard_map/all_to_all | solution.py:114
  23.5 6.8 %copy-start.72 = (s32[1,128]{1,0:T(1,128)S(1)}, s32[1,128]{1,0:T(1,128)}, u32[]{:S(2)}) copy-start(s32[1,128]{1,0:T(1,128)} %param.28) | copy-start | bytes 1540
  23.5 6.8 %copy-start.73 = (f32[1,128]{1,0:T(1,128)S(1)}, f32[1,128]{1,0:T(1,128)}, u32[]{:S(2)}) copy-start(f32[1,128]{1,0:T(1,128)} %param.29) | copy-start | bytes 1540
  23.5 6.9 %copy-start.32 = (s32[1,8,128]{2,1,0:T(8,128)S(1)}, s32[1,8,128]{2,1,0:T(8,128)}, u32[]{:S(2)}) copy-start(s32[1,8,128]{2,1,0:T(8,128)} %param.25) | copy-start | bytes 12292
  23.5 6.9 %copy-start.2 = (bf16[1,2176,128]{2,1,0:T(8,128)(2,1)S(1)}, bf16[1,2176,128]{2,1,0:T(8,128)(2,1)}, u32[]{:S(2)}) copy-start(bf16[1,2176,128]{2,1,0:T(8,128)(2,1)} %param.16) | copy-start | bytes 1671172
  23.8 6.5 %copy-start.23 = (bf16[1,2176,128]{2,1,0:T(8,128)(2,1)S(1)}, bf16[1,2176,128]{2,1,0:T(8,128)(2,1)}, u32[]{:S(2)}) copy-start(bf16[1,2176,128]{2,1,0:T(8,128)(2,1)} %param.17) | copy-start | bytes 1671172
  23.8 6.6 %copy-start.25 = (bf16[1,2176,128]{2,1,0:T(8,128)(2,1)S(1)}, bf16[1,2176,128]{2,1,0:T(8,128)(2,1)}, u32[]{:S(2)}) copy-start(bf16[1,2176,128]{2,1,0:T(8,128)(2,1)} %param.18) | copy-start | bytes 1671172
  23.8 15.0 %collective-permute-start = (f32[2176,1]{0,1:T(1,128)S(1)}, f32[2176,1]{0,1:T(1,128)S(1)}, u32[]{:S(2)}, u32[]{:S(2)}) collective-permute-start(f32[2176,1]{0,1:T(1,128)S(1)} %copy.37), channel_id=1, source_target_pairs={{0,1},{1,2},{2,3},{3,4},{4,5},{5,6},{6,7},{7,8},{8,9},{9,10},{10,1... | collective-permute-start | bytes 26120 | tf_op jit(solution)/shard_map/ppermute | solution.py:23
  28.3 12.0 %collective-permute-start.1 = (f32[2176,1]{0,1:T(1,128)S(1)}, f32[2176,1]{0,1:T(1,128)S(1)}, u32[]{:S(2)}, u32[]{:S(2)}) collective-permute-start(f32[2176,1]{0,1:T(1,128)S(1)} %copy.39), channel_id=1, source_target_pairs={{1,0},{2,1},{3,2},{4,3},{5,4},{6,5},{7,6},{8,7},{9,8},{10,9},{11,1... | collective-permute-start | bytes 26120 | tf_op jit(solution)/shard_map/ppermute | solution.py:24
  30.3 43.8 %copy-start.35 = (pred[8]{0:T(512)(128)(4,1)}, pred[8]{0:T(512)(128)(4,1)S(1)}, u32[]{:S(2)}) copy-start(pred[8]{0:T(512)(128)(4,1)S(1)} %compare_and_fusion) | copy-start | bytes 28
  30.3 7.5 %copy-start.71 = (s32[128]{0:T(128)}, s32[128]{0:T(128)S(1)}, u32[]{:S(2)}) copy-start(s32[128]{0:T(128)S(1)} %fusion.63) | copy-start | bytes 1540
  30.3 81.2 %copy-start.68 = (f32[128]{0:T(128)}, f32[128]{0:T(128)S(1)}, u32[]{:S(2)}) copy-start(f32[128]{0:T(128)S(1)} %negate_bitcast_fusion) | copy-start | bytes 1540
  30.4 7.5 %copy-start.21 = (bf16[1024,128]{1,0:T(8,128)(2,1)S(1)}, bf16[1024,128]{1,0:T(8,128)(2,1)}, u32[]{:S(2)}) copy-start(bf16[1024,128]{1,0:T(8,128)(2,1)} %copy-done.20) | copy-start | bytes 786436
  30.4 8.3 %copy-start.33 = (f32[1,2176]{1,0:T(1,128)S(1)}, f32[1,2176]{1,0:T(1,128)}, u32[]{:S(2)}) copy-start(f32[1,2176]{1,0:T(1,128)} %param.22) | copy-start | bytes 26116
  30.4 8.3 %copy-start.34 = (f32[1,2176]{1,0:T(1,128)S(1)}, f32[1,2176]{1,0:T(1,128)}, u32[]{:S(2)}) copy-start(f32[1,2176]{1,0:T(1,128)} %param.23) | copy-start | bytes 26116
  104.6 144.8 %all-to-all-start.1 = ((f32[16,1,16384]{2,1,0:T(1,128)}), f32[16,1,16384]{2,1,0:T(1,128)}, u32[]{:S(2)}, u32[]{:S(2)}) async-start(f32[16,1,16384]{2,1,0:T(1,128)} %all_to_all.19), calls=%async_computation.1 | async-start | bytes 2097152 | tf_op jit(solution)/shard_map/all_to_all | solution.py:114
  119.3 126.6 %collective-permute-start.2 = (f32[2176,1]{0,1:T(1,128)S(1)}, f32[2176,1]{0,1:T(1,128)S(1)}, u32[]{:S(2)}, u32[]{:S(2)}) collective-permute-start(f32[2176,1]{0,1:T(1,128)S(1)} %copy.43), channel_id=1, source_target_pairs={{0,1},{1,2},{2,3},{3,4},{4,5},{5,6},{6,7},{7,8},{8,9},{9,10},{10,1... | collective-permute-start | bytes 26120 | tf_op jit(solution)/shard_map/ppermute | solution.py:23
  124.4 123.1 %collective-permute-start.3 = (f32[2176,1]{0,1:T(1,128)S(1)}, f32[2176,1]{0,1:T(1,128)}, u32[]{:S(2)}, u32[]{:S(2)}) collective-permute-start(f32[2176,1]{0,1:T(1,128)S(1)} %copy.45), channel_id=1, source_target_pairs={{1,0},{2,1},{3,2},{4,3},{5,4},{6,5},{7,6},{8,7},{9,8},{10,9},{11,1... | collective-permute-start | bytes 26120 | tf_op jit(solution)/shard_map/ppermute | solution.py:24
  183.9 51.1 %copy-start.6 = (f32[4096,1]{1,0:T(8,128)}, f32[4096,1]{1,0:T(8,128)S(1)}, u32[]{:S(2)}) copy-start(f32[4096,1]{1,0:T(8,128)S(1)} %all-gather) | copy-start | bytes 49156
  234.9 3.0 copy-start.37
  235.0 2.9 copy-start.39
  235.0 2.9 copy-start.41
  235.0 2.9 copy-start.43
  235.0 2.9 copy-start.45
  235.0 2.9 copy-start.47
  235.0 2.9 copy-start.49
  235.0 2.9 copy-start.51
  235.0 2.9 copy-start.53
  235.0 2.9 copy-start.55
  235.0 2.9 copy-start.57
  235.1 2.9 copy-start.59
  235.1 2.9 copy-start.61
  235.1 2.9 copy-start.63
  235.5 2.5 copy-start.65
  238.0 7.0 %copy-start.19 = (bf16[1024,128]{1,0:T(8,128)(2,1)S(1)}, bf16[1024,128]{1,0:T(8,128)(2,1)}, u32[]{:S(2)}) copy-start(bf16[1024,128]{1,0:T(8,128)(2,1)} %gather_fusion.3) | copy-start | bytes 786436
  252.4 2.9 slice-start
  252.4 2.9 copy-start.36
  258.4 7.7 %copy-start.69 = (f32[128]{0:T(128)S(1)}, f32[128]{0:T(128)}, u32[]{:S(2)}) copy-start(f32[128]{0:T(128)} %copy-done.68) | copy-start | bytes 1540
  270.0 49.7 %copy-start.14 = (f32[2176,1]{1,0:T(8,128)S(1)}, f32[2176,1]{1,0:T(8,128)}, u32[]{:S(2)}) copy-start(f32[2176,1]{1,0:T(8,128)} %copy.46) | copy-start | bytes 26116
  318.0 1.7 copy-start.13
  323.4 2.2 copy-start.8
  323.4 2.2 copy-start.9
  323.4 2.2 copy-start.10
  323.5 2.2 copy-start.18
  323.5 2.2 copy-start.24
  (33 other events, 40.9 us)
where the time goes:
time: 333 us; the launch traced here: 327 us
  blocking collectives  156 us (47%)
  local copies, waits for them, and re-layouts  53.6 us (16%)
  other arithmetic  37.9 us (11%)
  waiting for transfers between devices  28.9 us (9%)
  starting transfers between devices  28.6 us (9%)
  matrix products  15.8 us (5%)
  Pallas kernels  4.54 us (1%)
    all_gather x2, blocking collectives, local(): state_last = lax.all_gather(local_state[:, -1], 'tm', axis=0)  98 us
    all_gather x1, blocking collectives, local(): kept_last = lax.all_gather(kept_total[:, -1], 'tm', axis=0)  57.6 us
    all_to_all x2, waiting for transfers between devices, exchanged(): got = lax.all_to_all(sent, 'area', split_axis=0, concat_axis=0, tiled=True)  28.9 us
    all_to_all x2, starting transfers between devices, exchanged(): got = lax.all_to_all(sent, 'area', split_axis=0, concat_axis=0, tiled=True)  16 us
    dot_general x2, matrix products, local(): jnp.dot(matrix, rounded, preferred_element_type=jnp.float32) + fixed_part  14.4 us
    scatter-add x2, other arithmetic, local(): jnp.zeros((bus_count, hour_count), jnp.float32).at[edge_rows].add(tie_flow)  13.7 us
    unnamed x151, local copies, waits for them, and re-layouts  9.79 us
    gather x2, local copies, waits for them, and re-layouts, local(): own_edge = rounded[edge_rows].astype(jnp.float32)  9.21 us
  transfers between devices with their start and end apart: 6, of which 1 were waited for; matrix products, arithmetic and copies ran while one was open for 10% of the time, Pallas kernels for 1%

commit v1 on v0

--- a/solution.py
+++ b/solution.py
@@ -121,7 +121,6 @@
         return found
 
     kept_total = None
-    kept_last = None
     price_far = None
     penalty_far = None
     mismatch = None
@@ -144,10 +143,10 @@
         dispatch_next = dispatch + dispatch_step * (balance - slope * dispatch) + ramp_local * bend
         charge = -gain_local * balance[store_rows] / math.sqrt(year_hours)
         kept_total, local_state = window_scan(kept_local, charge)
-        if kept_last is None:
-            kept_last = lax.all_gather(kept_total[:, -1], "tm", axis=0)
-        state_last = lax.all_gather(local_state[:, -1], "tm", axis=0)
-        state_in = carried_state(kept_last, state_last, position)
+        ends = jnp.stack([kept_total[:, -1], local_state[:, -1]])
+        copies = jnp.broadcast_to(ends, (lax.axis_size("tm"),) + ends.shape)
+        ends = lax.all_to_all(copies, "tm", split_axis=0, concat_axis=0, tiled=True)
+        state_in = carried_state(ends[:, 0], ends[:, 1], position)
         charge_state = local_state + kept_total * state_in[:, None]
         injection = (
             jnp.zeros((bus_count, hour_count), jnp.float32)

time: 333 us -> 198 us (0.59); the launches traced: 327 us -> 197 us
  blocking collectives: 156 us -> 0 us
  starting transfers between devices: 28.6 us -> 54.5 us
  local copies, waits for them, and re-layouts: 53.6 us -> 48.7 us
  waiting for transfers between devices: 28.9 us -> 33.8 us
    all_gather x3 -> x0, blocking collectives: 156 us -> none  [the longest x2 98 us: local(): state_last = lax.all_gather(local_state[:, -1], 'tm', axis=0)]
    all_to_all x0 -> x2, starting transfers between devices: none -> 28.8 us  [local(): ends = lax.all_to_all(copies, 'tm', split_axis=0, concat_axis=0, tiled=True)]
    unnamed x151 -> x75, local copies, waits for them, and re-layouts: 9.79 us -> 10.4 us
  transfers between devices with their start and end apart: 6 -> 8, of which waited for: 1 -> 4; matrix products, arithmetic and copies ran while one was open for 10% -> 24% of each run, Pallas kernels for 1% -> 0%
where the time goes in v1:
time: 198 us; the launch traced here: 197 us
  starting transfers between devices  54.5 us (28%)
  local copies, waits for them, and re-layouts  48.7 us (25%)
  other arithmetic  38.2 us (19%)
  waiting for transfers between devices  33.8 us (17%)
  matrix products  15.9 us (8%)
  Pallas kernels  4.55 us (2%)
    all_to_all x2, waiting for transfers between devices, exchanged(): got = lax.all_to_all(sent, 'area', split_axis=0, concat_axis=0, tiled=True)  31.9 us
    all_to_all x2, starting transfers between devices, local(): ends = lax.all_to_all(copies, 'tm', split_axis=0, concat_axis=0, tiled=True)  28.8 us
    dot_general x2, matrix products, local(): jnp.dot(matrix, rounded, preferred_element_type=jnp.float32) + fixed_part  14.5 us
    all_to_all x2, starting transfers between devices, exchanged(): got = lax.all_to_all(sent, 'area', split_axis=0, concat_axis=0, tiled=True)  14.1 us
    scatter-add x2, other arithmetic, local(): jnp.zeros((bus_count, hour_count), jnp.float32).at[edge_rows].add(tie_flow)  13.7 us
    unnamed x75, local copies, waits for them, and re-layouts  10.4 us
    gather x2, local copies, waits for them, and re-layouts, local(): own_edge = rounded[edge_rows].astype(jnp.float32)  7.26 us
    ppermute x2, starting transfers between devices, padded_2(): before = lax.ppermute(last, axis, up)  5.83 us
  transfers between devices with their start and end apart: 8, of which 4 were waited for; matrix products, arithmetic and copies ran while one was open for 24% of the time, Pallas kernels for 0%

profile of v1, /device:TPU:1, one launch (start us, length us, event | category | flops | bytes accessed | tf_op | source)
XLA Modules:
  0.0 196.9 jit_solution(1725684127804843527)
XLA Ops:
  1.4 4.0 %gather_fusion = bf16[1024,128]{1,0:T(8,128)(2,1)S(1)} fusion(bf16[2176,128]{1,0:T(8,128)(2,1)} %bitcast.1253, s32[1024]{0:T(1024)S(1)} %broadcast_clamp_fusion), kind=kCustom, calls=%fused_computation | custom fusion | bytes 528384 | tf_op jit(solution)/shard_map/gather | solution.py:129
  6.5 1.0 pad_maximum_fusion.4
  7.5 2.3 %scatter_custom_fusion = f32[16,32896]{1,0:T(8,128)S(1)} fusion(s32[8]{0:T(128)S(1)} %get-tuple-element.24, f32[8,32896]{1,0:T(8,128)} %pad_maximum_fusion.4, f32[]{:T(128)} %constant.53.clone.1), kind=kCustom, calls=%fused_computation.47 | custom fusion | bytes 2105856 | tf_op jit(solution)/shard_map/scatter | solution.py:113
  9.9 2.8 %all_to_all.22 = f32[16,1,32896]{2,1,0:T(1,128)} reshape(f32[16,32896]{1,0:T(8,128)S(1)} %scatter_custom_fusion) | data formatting | bytes 4210688 | tf_op jit(solution)/shard_map/all_to_all | solution.py:114
  12.6 9.7 %all-to-all-start = ((f32[16,1,32896]{2,1,0:T(1,128)}), f32[16,1,32896]{2,1,0:T(1,128)}, u32[]{:S(2)}, u32[]{:S(2)}) async-start(f32[16,1,32896]{2,1,0:T(1,128)} %all_to_all.22), calls=%async_computation | async-start | bytes 4210688 | tf_op jit(solution)/shard_map/all_to_all | solution.py:114
  23.8 3.8 %collective-permute-start.1 = (f32[2176,1]{0,1:T(1,128)S(1)}, f32[2176,1]{0,1:T(1,128)S(1)}, u32[]{:S(2)}, u32[]{:S(2)}) collective-permute-start(f32[2176,1]{0,1:T(1,128)S(1)} %copy.39), channel_id=1, source_target_pairs={{1,0},{2,1},{3,2},{4,3},{5,4},{6,5},{7,6},{8,7},{9,8},{10,9},{11,1... | collective-permute-start | bytes 26120 | tf_op jit(solution)/shard_map/ppermute | solution.py:24
  28.0 2.3 %collective-permute-start = (f32[2176,1]{0,1:T(1,128)S(1)}, f32[2176,1]{0,1:T(1,128)S(1)}, u32[]{:S(2)}, u32[]{:S(2)}) collective-permute-start(f32[2176,1]{0,1:T(1,128)S(1)} %copy.37), channel_id=1, source_target_pairs={{0,1},{1,2},{2,3},{3,4},{4,5},{5,6},{6,7},{7,8},{8,9},{9,10},{10,1... | collective-permute-start | bytes 26120 | tf_op jit(solution)/shard_map/ppermute | solution.py:23
  30.4 7.4 %fusion.10 = f32[2176,128]{1,0:T(8,128)} fusion(bf16[1,2176,2176]{2,1,0:T(8,128)(2,1)} %param.20, bf16[1,2176,128]{2,1,0:T(8,128)(2,1)S(1)} %copy-done.20, bf16[1,2176,128]{2,1,0:T(8,128)(2,1)S(1)} %copy-done.22, bf16[1,2176,128]{2,1,0:T(8,128)(2,1)S(1)} %copy-done.2), kind=kOutput, calls=%fused_computation.17 | convolution fusion | flops 1213267968 | bytes 12255232 | tf_op jit(solution)/shard_map/dot_general | solution.py:140
  38.8 1.4 copy.38
  40.2 1.4 copy.40
  41.6 29.0 %all-to-all-done = f32[16,1,32896]{2,1,0:T(1,128)} async-done(((f32[16,1,32896]{2,1,0:T(1,128)}), f32[16,1,32896]{2,1,0:T(1,128)}, u32[]{:S(2)}, u32[]{:S(2)}) %all-to-all-start) | async-done | bytes 2105376 | tf_op jit(solution)/shard_map/all_to_all | solution.py:114
  70.6 1.7 copy.82
  72.3 1.8 gather_fusion.1
  74.1 1.4 broadcast_select_fusion
  77.2 1.1 fusion.39
  78.6 6.8 %scatter_fusion = f32[2176,128]{1,0:T(8,128)S(1)} fusion(f32[2176,128]{1,0:T(8,128)S(1)} %copy-done.1, s32[1024]{0:T(1024)S(1)} %fusion.56, f32[1024,128]{1,0:T(8,128)} %bitcast.1266), kind=kCustom, calls=%fused_computation.7 | custom fusion | flops 131072 | bytes 1576960 | tf_op jit(solution)/shard_map/scatter-add | solution.py:138
  86.8 2.3 %shard_map.183 = (f32[128,128]{1,0:T(8,128)}, f32[128,128]{1,0:T(8,128)}) custom-call(f32[128,128]{1,0:T(8,128)} %bitcast.1268, f32[128,128]{1,0:T(8,128)} %multiply_multiply_fusion.1.charge_ref), custom_call_target="tpu_custom_call" | custom-call | tf_op jit(solution)/shard_map/pallas_call | solution.py:53
  89.0 1.0 slice_reduce_fusion.2
  90.7 15.6 %all-to-all-start.1 = ((f32[32,2,128]{2,1,0:T(2,128)}), f32[32,2,128]{2,1,0:T(2,128)S(1)}, u32[]{:S(2)}, u32[]{:S(2)}) async-start(f32[32,2,128]{2,1,0:T(2,128)} %broadcast_in_dim.69), calls=%async_computation.1 | async-start | bytes 65536 | tf_op jit(solution)/shard_map/all_to_all | solution.py:148
  106.3 3.8 %fusion.21 = (f32[2176,128]{1,0:T(8,128)S(1)}, bf16[2176,128]{1,0:T(8,128)(2,1)S(1)}) fusion(f32[2176,1]{1,0:T(8,128)} %copy.40, f32[2176,128]{1,0:T(8,128)} %copy-done.3, f32[2176,1]{1,0:T(8,128)} %copy.38, f32[2176,128]{1,0:T(8,128)S(1)} %scatter_fusion, bf16[1,2176,128]{2,1,0:T(8,128)(2,1)} %param.17, f32[2176]{0:T(1024)S(1)} %reduce.3, f32[2176]{0:T(1024)S(1)} %reduce.2), kind=kLoop, calls=%fused_computation.32 | loop fusion | flops 3620864 | bytes 4491264 | tf_op jit(solution)/shard_map/add | solution.py:143
  110.1 1.1 fusion.26
  111.2 1.0 copy-done.4
  112.4 3.2 %gather_fusion.3 = bf16[1024,128]{1,0:T(8,128)(2,1)S(1)} fusion(bf16[2176,128]{1,0:T(8,128)(2,1)S(1)} %fusion.23, s32[1024]{0:T(1024)S(1)} %broadcast_clamp_fusion), kind=kCustom, calls=%fused_computation.3 | custom fusion | bytes 528384 | tf_op jit(solution)/shard_map/gather | solution.py:129
  117.2 1.6 scatter_custom_fusion.3
  118.8 2.1 %all_to_all.26 = f32[16,1,16384]{2,1,0:T(1,128)} reshape(f32[16,16384]{1,0:T(8,128)S(1)} %scatter_custom_fusion.3) | data formatting | bytes 2097152 | tf_op jit(solution)/shard_map/all_to_all | solution.py:114
  120.9 4.3 %all-to-all-start.2 = ((f32[16,1,16384]{2,1,0:T(1,128)}), f32[16,1,16384]{2,1,0:T(1,128)}, u32[]{:S(2)}, u32[]{:S(2)}) async-start(f32[16,1,16384]{2,1,0:T(1,128)} %all_to_all.26), calls=%async_computation.2 | async-start | bytes 2097152 | tf_op jit(solution)/shard_map/all_to_all | solution.py:114
  125.2 1.3 fusion.187
  126.6 1.6 copy.43
  128.2 3.6 %collective-permute-start.2 = (f32[2176,1]{0,1:T(1,128)S(1)}, f32[2176,1]{0,1:T(1,128)S(1)}, u32[]{:S(2)}, u32[]{:S(2)}) collective-permute-start(f32[2176,1]{0,1:T(1,128)S(1)} %copy.43), channel_id=1, source_target_pairs={{0,1},{1,2},{2,3},{3,4},{4,5},{5,6},{6,7},{7,8},{8,9},{9,10},{10,1... | collective-permute-start | bytes 26120 | tf_op jit(solution)/shard_map/ppermute | solution.py:23
  132.1 1.9 collective-permute-start.3
  134.1 1.8 convert_element_type.138
  135.9 1.4 copy.44
  137.5 1.4 copy.46
  139.0 2.2 %scatter_custom_fusion.2 = f32[2176,128]{1,0:T(8,128)} fusion(s32[128]{0:T(128)S(1)} %fusion.61, f32[]{:T(128)} %constant.53.clone.1, f32[128,128]{1,0:T(8,128)S(1)} %copy-done.26, f32[128,128]{1,0:T(8,128)S(1)} %copy-done.25, f32[128]{0:T(128)S(1)} %broadcast_select_fusion.64, f32[128]{0:T(128)S(1)} %bitcast.1279), kind=kCustom, calls=%fused_computation.60 | custom fusion | flops 65536 | bytes 1246212 | tf_op jit(solution)/shard_map/scatter-add | solution.py:154
  141.2 7.1 %fusion.7 = f32[2176,128]{1,0:T(8,128)S(1)} fusion(bf16[2176,128]{1,0:T(8,128)(2,1)} %bitcast.1262, bf16[1,2176,2176]{2,1,0:T(8,128)(2,1)} %param.20, f32[2176,128]{1,0:T(8,128)} %scatter_custom_fusion.2, f32[2176,128]{1,0:T(8,128)S(1)} %get-tuple-element.29, bf16[1,2176,128]{2,1,0:T(8,128)(2,1)} %param.18), kind=kOutput, calls=%fused_computation.16 | convolution fusion | flops 1213267968 | bytes 13926400 | tf_op jit(solution)/shard_map/dot_general | solution.py:140
  148.3 2.9 %all-to-all-done.2 = f32[16,1,16384]{2,1,0:T(1,128)} async-done(((f32[16,1,16384]{2,1,0:T(1,128)}), f32[16,1,16384]{2,1,0:T(1,128)}, u32[]{:S(2)}, u32[]{:S(2)}) %all-to-all-start.2) | async-done | bytes 1048608 | tf_op jit(solution)/shard_map/all_to_all | solution.py:114
  151.2 2.8 %copy.83 = f32[16,1,16384]{2,0,1:T(8,128)} copy(f32[16,1,16384]{2,1,0:T(1,128)} %all-to-all-done.2) | data formatting | bytes 2097152
  154.0 2.9 %gather_fusion.4 = f32[8,16384]{1,0:T(8,128)} fusion(f32[16,16384]{1,0:T(8,128)} %bitcast.1252, s32[1024]{0:T(1024)S(1)} %pad_clamp_fusion.1), kind=kCustom, calls=%fused_computation.4 | custom fusion | bytes 1048608 | tf_op jit(solution)/shard_map/jit(_take)/gather | solution.py:115
  156.9 3.0 %fusion.42 = f32[8,128,128]{2,1,0:T(8,128)} fusion(bf16[1,8,128,128]{3,2,1,0:T(8,128)(2,1)} %param.19, f32[8,128,128]{2,1,0:T(8,128)} %bitcast.1260, f32[8,128,128]{2,0,1:T(8,128)} %bitcast.1258, f32[8,128,128]{2,0,1:T(8,128)} %copy-done.10, f32[8,128]{1,0:T(8,128)S(1)} %slice-done, f32[8,128]{1,0:T(8,128)S(1)} %bitcast.1271, f32[8,128]{1,0:T(8,128)S(1)} %bitcast.1274, ...), kind=kLoop, calls=%fused_computation.68 | loop fusion | flops 1572864 | bytes 3420168 | tf_op jit(solution)/shard_map/add | solution.py:137
  160.0 6.8 %scatter_fusion.1 = f32[2176,128]{1,0:T(8,128)S(1)} fusion(f32[2176,128]{1,0:T(8,128)S(1)} %fusion.7, s32[1024]{0:T(1024)S(1)} %fusion.56, f32[1024,128]{1,0:T(8,128)} %bitcast.1265), kind=kCustom, calls=%fused_computation.10 | custom fusion | flops 131072 | bytes 1576960 | tf_op jit(solution)/shard_map/scatter-add | solution.py:138
  168.2 2.3 %shard_map.184 = (f32[128,128]{1,0:T(8,128)}, f32[128,128]{1,0:T(8,128)}) custom-call(f32[128,128]{1,0:T(8,128)} %bitcast.1269, f32[128,128]{1,0:T(8,128)} %multiply_multiply_fusion.charge_ref), custom_call_target="tpu_custom_call" | custom-call | tf_op jit(solution)/shard_map/pallas_call | solution.py:53
  170.4 1.0 slice_reduce_fusion
  171.5 1.0 slice_reduce_fusion.1
  173.1 13.2 %all-to-all-start.3 = ((f32[32,2,128]{2,1,0:T(2,128)}), f32[32,2,128]{2,1,0:T(2,128)S(1)}, u32[]{:S(2)}, u32[]{:S(2)}) async-start(f32[32,2,128]{2,1,0:T(2,128)} %broadcast_in_dim.76), calls=%async_computation.3 | async-start | bytes 65536 | tf_op jit(solution)/shard_map/all_to_all | solution.py:148
  186.4 3.6 %fusion.37 = (bf16[1,2176,128]{2,1,0:T(8,128)(2,1)}, bf16[2176,128]{1,0:T(8,128)(2,1)S(1)}) fusion(f32[2176,1]{1,0:T(8,128)} %copy.46, f32[2176,128]{1,0:T(8,128)S(1)} %get-tuple-element.29, f32[2176,1]{1,0:T(8,128)} %copy.44, f32[2176]{0:T(1024)S(1)} %reduce.3, f32[2176,128]{1,0:T(8,128)S(1)} %scatter_fusion.1, f32[2176]{0:T(1024)S(1)} %reduce.2), kind=kLoop, calls=%fused_computation.62 | loop fusion | flops 3620864 | bytes 3377152 | tf_op jit(solution)/shard_map/broadcast_in_dim | solution.py:165
  191.2 1.1 bitcast_subtract_fusion
  193.2 1.2 fusion.43
  194.4 1.7 all-to-all-done.3
  (112 shorter events, 15.6 us)
Async XLA Ops:
  0.6 109.5 %copy-start = (bf16[1,34,64,64]{3,2,1,0:T(8,128)(2,1)S(1)}, bf16[1,34,64,64]{3,2,1,0:T(8,128)(2,1)}, u32[]{:S(2)}) copy-start(bf16[1,34,64,64]{3,2,1,0:T(8,128)(2,1)} %param.21) | copy-start | bytes 835588
  1.4 4.2 %copy-start.13 = (bf16[1,8,128,128]{3,2,1,0:T(8,128)(2,1)S(1)}, bf16[1,8,128,128]{3,2,1,0:T(8,128)(2,1)}, u32[]{:S(2)}) copy-start(bf16[1,8,128,128]{3,2,1,0:T(8,128)(2,1)} %param.19) | copy-start | bytes 786436
  5.5 0.7 copy-start.17
  5.6 0.7 copy-start.32
  5.6 0.9 copy-start.27
  12.6 9.7 %copy-start.19 = (bf16[1,2176,128]{2,1,0:T(8,128)(2,1)S(1)}, bf16[1,2176,128]{2,1,0:T(8,128)(2,1)}, u32[]{:S(2)}) copy-start(bf16[1,2176,128]{2,1,0:T(8,128)(2,1)} %param.17) | copy-start | bytes 1671172
  12.6 57.9 %all-to-all-start = ((f32[16,1,32896]{2,1,0:T(1,128)}), f32[16,1,32896]{2,1,0:T(1,128)}, u32[]{:S(2)}, u32[]{:S(2)}) async-start(f32[16,1,32896]{2,1,0:T(1,128)} %all_to_all.22), calls=%async_computation | async-start | bytes 4210688 | tf_op jit(solution)/shard_map/all_to_all | solution.py:114
  22.5 1.0 copy-start.3
  23.5 6.8 %copy-start.34 = (s32[1,128]{1,0:T(1,128)S(1)}, s32[1,128]{1,0:T(1,128)}, u32[]{:S(2)}) copy-start(s32[1,128]{1,0:T(1,128)} %param.28) | copy-start | bytes 1540
  23.5 6.8 %copy-start.35 = (f32[1,128]{1,0:T(1,128)S(1)}, f32[1,128]{1,0:T(1,128)}, u32[]{:S(2)}) copy-start(f32[1,128]{1,0:T(1,128)} %param.29) | copy-start | bytes 1540
  23.5 6.8 %copy-start.29 = (s32[1,8,128]{2,1,0:T(8,128)S(1)}, s32[1,8,128]{2,1,0:T(8,128)}, u32[]{:S(2)}) copy-start(s32[1,8,128]{2,1,0:T(8,128)} %param.25) | copy-start | bytes 12292
  23.5 6.9 %copy-start.2 = (bf16[1,2176,128]{2,1,0:T(8,128)(2,1)S(1)}, bf16[1,2176,128]{2,1,0:T(8,128)(2,1)}, u32[]{:S(2)}) copy-start(bf16[1,2176,128]{2,1,0:T(8,128)(2,1)} %param.16) | copy-start | bytes 1671172
  23.8 6.5 %copy-start.20 = (bf16[1,2176,128]{2,1,0:T(8,128)(2,1)S(1)}, bf16[1,2176,128]{2,1,0:T(8,128)(2,1)}, u32[]{:S(2)}) copy-start(bf16[1,2176,128]{2,1,0:T(8,128)(2,1)} %param.17) | copy-start | bytes 1671172
  23.8 6.5 %copy-start.22 = (bf16[1,2176,128]{2,1,0:T(8,128)(2,1)S(1)}, bf16[1,2176,128]{2,1,0:T(8,128)(2,1)}, u32[]{:S(2)}) copy-start(bf16[1,2176,128]{2,1,0:T(8,128)(2,1)} %param.18) | copy-start | bytes 1671172
  23.8 16.3 %collective-permute-start.1 = (f32[2176,1]{0,1:T(1,128)S(1)}, f32[2176,1]{0,1:T(1,128)S(1)}, u32[]{:S(2)}, u32[]{:S(2)}) collective-permute-start(f32[2176,1]{0,1:T(1,128)S(1)} %copy.39), channel_id=1, source_target_pairs={{1,0},{2,1},{3,2},{4,3},{5,4},{6,5},{7,6},{8,7},{9,8},{10,9},{11,1... | collective-permute-start | bytes 26120 | tf_op jit(solution)/shard_map/ppermute | solution.py:24
  28.0 10.8 %collective-permute-start = (f32[2176,1]{0,1:T(1,128)S(1)}, f32[2176,1]{0,1:T(1,128)S(1)}, u32[]{:S(2)}, u32[]{:S(2)}) collective-permute-start(f32[2176,1]{0,1:T(1,128)S(1)} %copy.37), channel_id=1, source_target_pairs={{0,1},{1,2},{2,3},{3,4},{4,5},{5,6},{6,7},{7,8},{8,9},{9,10},{10,1... | collective-permute-start | bytes 26120 | tf_op jit(solution)/shard_map/ppermute | solution.py:23
  30.4 7.5 %copy-start.18 = (bf16[1024,128]{1,0:T(8,128)(2,1)S(1)}, bf16[1024,128]{1,0:T(8,128)(2,1)}, u32[]{:S(2)}) copy-start(bf16[1024,128]{1,0:T(8,128)(2,1)} %copy-done.17) | copy-start | bytes 786436
  30.4 8.3 %copy-start.30 = (f32[1,2176]{1,0:T(1,128)S(1)}, f32[1,2176]{1,0:T(1,128)}, u32[]{:S(2)}) copy-start(f32[1,2176]{1,0:T(1,128)} %param.22) | copy-start | bytes 26116
  30.4 8.3 %copy-start.31 = (f32[1,2176]{1,0:T(1,128)S(1)}, f32[1,2176]{1,0:T(1,128)}, u32[]{:S(2)}) copy-start(f32[1,2176]{1,0:T(1,128)} %param.23) | copy-start | bytes 26116
  75.5 1.2 copy-start.12
  75.5 1.4 copy-start.6
  75.5 1.7 copy-start.14
  75.5 1.7 copy-start.28
  76.7 1.6 copy-start.10
  76.7 1.6 copy-start.11
  77.2 1.4 copy-start.1
  90.7 30.2 %all-to-all-start.1 = ((f32[32,2,128]{2,1,0:T(2,128)}), f32[32,2,128]{2,1,0:T(2,128)S(1)}, u32[]{:S(2)}, u32[]{:S(2)}) async-start(f32[32,2,128]{2,1,0:T(2,128)} %broadcast_in_dim.69), calls=%async_computation.1 | async-start | bytes 65536 | tf_op jit(solution)/shard_map/all_to_all | solution.py:148
  111.2 1.0 copy-start.4
  115.6 0.7 copy-start.16
  120.9 30.3 %all-to-all-start.2 = ((f32[16,1,16384]{2,1,0:T(1,128)}), f32[16,1,16384]{2,1,0:T(1,128)}, u32[]{:S(2)}, u32[]{:S(2)}) async-start(f32[16,1,16384]{2,1,0:T(1,128)} %all_to_all.26), calls=%async_computation.2 | async-start | bytes 2097152 | tf_op jit(solution)/shard_map/all_to_all | solution.py:114
  128.2 7.7 %collective-permute-start.2 = (f32[2176,1]{0,1:T(1,128)S(1)}, f32[2176,1]{0,1:T(1,128)S(1)}, u32[]{:S(2)}, u32[]{:S(2)}) collective-permute-start(f32[2176,1]{0,1:T(1,128)S(1)} %copy.43), channel_id=1, source_target_pairs={{0,1},{1,2},{2,3},{3,4},{4,5},{5,6},{6,7},{7,8},{8,9},{9,10},{10,1... | collective-permute-start | bytes 26120 | tf_op jit(solution)/shard_map/ppermute | solution.py:23
  132.1 5.4 %collective-permute-start.3 = (f32[2176,1]{0,1:T(1,128)S(1)}, f32[2176,1]{0,1:T(1,128)S(1)}, u32[]{:S(2)}, u32[]{:S(2)}) collective-permute-start(f32[2176,1]{0,1:T(1,128)S(1)} %copy.45), channel_id=1, source_target_pairs={{1,0},{2,1},{3,2},{4,3},{5,4},{6,5},{7,6},{8,7},{9,8},{10,9},{11,1... | collective-permute-start | bytes 26120 | tf_op jit(solution)/shard_map/ppermute | solution.py:24
  135.9 3.1 %copy-start.25 = (f32[128,128]{1,0:T(8,128)S(1)}, f32[128,128]{1,0:T(8,128)}, u32[]{:S(2)}) copy-start(f32[128,128]{1,0:T(8,128)} %get-tuple-element.9) | copy-start | bytes 196612
  135.9 3.1 %copy-start.26 = (f32[128,128]{1,0:T(8,128)S(1)}, f32[128,128]{1,0:T(8,128)}, u32[]{:S(2)}) copy-start(f32[128,128]{1,0:T(8,128)} %get-tuple-element.8) | copy-start | bytes 196612
  135.9 3.1 %copy-start.33 = (f32[1,128]{1,0:T(1,128)S(1)}, f32[1,128]{1,0:T(1,128)}, u32[]{:S(2)}) copy-start(f32[1,128]{1,0:T(1,128)} %param.30) | copy-start | bytes 1540
  154.0 2.9 %slice-start = ((f32[8,32896]{1,0:T(8,128)}), f32[8,128]{1,0:T(8,128)S(1)}, s32[]{:S(2)}) async-start(f32[8,32896]{1,0:T(8,128)} %copy-done.12), calls=%async_computation.4 | async-start | bytes 8192 | tf_op jit(solution)/shard_map/slice | solution.py:119
  173.1 23.0 %all-to-all-start.3 = ((f32[32,2,128]{2,1,0:T(2,128)}), f32[32,2,128]{2,1,0:T(2,128)S(1)}, u32[]{:S(2)}, u32[]{:S(2)}) async-start(f32[32,2,128]{2,1,0:T(2,128)} %broadcast_in_dim.76), calls=%async_computation.3 | async-start | bytes 65536 | tf_op jit(solution)/shard_map/all_to_all | solution.py:148
  190.0 1.2 copy-start.5
  191.2 1.2 copy-start.7
  191.2 1.5 copy-start.8
  191.2 1.8 copy-start.9
  191.2 1.8 copy-start.15
  191.2 2.0 %copy-start.21 = (f32[1,8,128,128]{3,1,2,0:T(8,128)S(1)}, f32[1,8,128,128]{3,1,2,0:T(8,128)}, u32[]{:S(2)}) copy-start(f32[1,8,128,128]{3,1,2,0:T(8,128)} %get-tuple-element.33) | copy-start | bytes 1572868
  193.2 3.0 %copy-start.23 = (f32[128,128]{1,0:T(8,128)S(1)}, f32[128,128]{1,0:T(8,128)}, u32[]{:S(2)}) copy-start(f32[128,128]{1,0:T(8,128)} %get-tuple-element.11) | copy-start | bytes 196612
  193.2 3.0 %copy-start.24 = (f32[128,128]{1,0:T(8,128)S(1)}, f32[128,128]{1,0:T(8,128)}, u32[]{:S(2)}) copy-start(f32[128,128]{1,0:T(8,128)} %get-tuple-element.10) | copy-start | bytes 196612

commit v2 on v1

--- a/solution.py
+++ b/solution.py
@@ -53,12 +53,21 @@
     return pl.pallas_call(scan_kernel, out_shape=(shape, shape))(kept, charge)
 
 
-def carried_state(kept_last, state_last, position):
-    state_in = jnp.zeros_like(state_last[0])
-    for window in range(state_last.shape[0]):
-        folded = kept_last[window] * state_in + state_last[window]
-        state_in = jnp.where(window < position, folded, state_in)
-    return state_in
+def carried_state(kept_end, state_end, position, count):
+    def passed(ends, step):
+        pairs = [(i, i + step) for i in range(count - step)]
+        got = lax.ppermute(ends, "tm", pairs)
+        have = position >= step
+        return jnp.where(have, got[0], 1.0), jnp.where(have, got[1], 0.0)
+
+    kept, state = passed(jnp.stack([kept_end, state_end]), 1)
+    step = 1
+    while step < count:
+        kept_before, state_before = passed(jnp.stack([kept, state]), step)
+        state = kept * state_before + state
+        kept = kept_before * kept
+        step *= 2
+    return state
 
 
 def local(
@@ -143,10 +152,9 @@
         dispatch_next = dispatch + dispatch_step * (balance - slope * dispatch) + ramp_local * bend
         charge = -gain_local * balance[store_rows] / math.sqrt(year_hours)
         kept_total, local_state = window_scan(kept_local, charge)
-        ends = jnp.stack([kept_total[:, -1], local_state[:, -1]])
-        copies = jnp.broadcast_to(ends, (lax.axis_size("tm"),) + ends.shape)
-        ends = lax.all_to_all(copies, "tm", split_axis=0, concat_axis=0, tiled=True)
-        state_in = carried_state(ends[:, 0], ends[:, 1], position)
+        state_in = carried_state(
+            kept_total[:, -1], local_state[:, -1], position, lax.axis_size("tm")
+        )
         charge_state = local_state + kept_total * state_in[:, None]
         injection = (
             jnp.zeros((bus_count, hour_count), jnp.float32)

time: 198 us -> 253 us (1.28)
  the two profiles are of different devices: /device:TPU:1 before, /device:TPU:8 now
where the time goes in v2:
time: 253 us; the launch traced here: 252 us
  starting transfers between devices  110 us (43%)
  local copies, waits for them, and re-layouts  47.1 us (19%)
  other arithmetic  38.8 us (15%)
  waiting for transfers between devices  33.8 us (13%)
  matrix products  15.9 us (6%)
  Pallas kernels  4.54 us (2%)
    ppermute x12, starting transfers between devices, passed(): got = lax.ppermute(ends, 'tm', pairs)  83.4 us
    all_to_all x2, waiting for transfers between devices, exchanged(): got = lax.all_to_all(sent, 'area', split_axis=0, concat_axis=0, tiled=True)  29.7 us
    all_to_all x2, starting transfers between devices, exchanged(): got = lax.all_to_all(sent, 'area', split_axis=0, concat_axis=0, tiled=True)  16.9 us
    dot_general x2, matrix products, local(): jnp.dot(matrix, rounded, preferred_element_type=jnp.float32) + fixed_part  14.5 us
    scatter-add x2, other arithmetic, local(): jnp.zeros((bus_count, hour_count), jnp.float32).at[edge_rows].add(tie_flow)  13.7 us
    unnamed x111, local copies, waits for them, and re-layouts  8.19 us
    gather x2, local copies, waits for them, and re-layouts, local(): own_edge = rounded[edge_rows].astype(jnp.float32)  7.25 us
    ppermute x2, starting transfers between devices, padded_2(): before = lax.ppermute(last, axis, up)  6.91 us
  transfers between devices with their start and end apart: 18, of which 6 were waited for; matrix products, arithmetic and copies ran while one was open for 19% of the time, Pallas kernels for 0%

profile of v2, /device:TPU:8, one launch (start us, length us, event | category | flops | bytes accessed | tf_op | source)
XLA Modules:
  0.0 251.7 jit_solution(17576865580759958573)
XLA Ops:
  2.0 4.0 %gather_fusion = bf16[1024,128]{1,0:T(8,128)(2,1)S(1)} fusion(bf16[2176,128]{1,0:T(8,128)(2,1)} %bitcast.137, s32[1024]{0:T(1024)S(1)} %broadcast_clamp_fusion), kind=kCustom, calls=%fused_computation | custom fusion | bytes 528384 | tf_op jit(solution)/shard_map/gather | solution.py:138
  8.1 2.3 scatter_custom_fusion
  10.5 2.8 %all_to_all.16 = f32[16,1,32896]{2,1,0:T(1,128)} reshape(f32[16,32896]{1,0:T(8,128)S(1)} %scatter_custom_fusion) | data formatting | bytes 4210688 | tf_op jit(solution)/shard_map/all_to_all | solution.py:123
  13.3 10.1 %all-to-all-start = ((f32[16,1,32896]{2,1,0:T(1,128)}), f32[16,1,32896]{2,1,0:T(1,128)}, u32[]{:S(2)}, u32[]{:S(2)}) async-start(f32[16,1,32896]{2,1,0:T(1,128)} %all_to_all.16), calls=%async_computation | async-start | bytes 4210688 | tf_op jit(solution)/shard_map/all_to_all | solution.py:123
  24.9 1.4 collective-permute-start.1
  26.6 3.0 %collective-permute-start = (f32[2176,1]{0,1:T(1,128)S(1)}, f32[2176,1]{0,1:T(1,128)S(1)}, u32[]{:S(2)}, u32[]{:S(2)}) collective-permute-start(f32[2176,1]{0,1:T(1,128)S(1)} %copy.37), channel_id=1, source_target_pairs={{0,1},{1,2},{2,3},{3,4},{4,5},{5,6},{6,7},{7,8},{8,9},{9,10},{10,1... | collective-permute-start | bytes 26120 | tf_op jit(solution)/shard_map/ppermute | solution.py:23
  29.9 7.4 %fusion.10 = f32[2176,128]{1,0:T(8,128)} fusion(bf16[1,2176,2176]{2,1,0:T(8,128)(2,1)} %param.20, bf16[1,2176,128]{2,1,0:T(8,128)(2,1)S(1)} %copy-done.19, bf16[1,2176,128]{2,1,0:T(8,128)(2,1)S(1)} %copy-done.21, bf16[1,2176,128]{2,1,0:T(8,128)(2,1)S(1)} %copy-done.2), kind=kOutput, calls=%fused_computation.17 | convolution fusion | flops 1213267968 | bytes 12255232 | tf_op jit(solution)/shard_map/dot_general | solution.py:149
  38.3 1.4 copy.38
  39.7 1.4 copy.40
  41.1 29.7 %all-to-all-done = f32[16,1,32896]{2,1,0:T(1,128)} async-done(((f32[16,1,32896]{2,1,0:T(1,128)}), f32[16,1,32896]{2,1,0:T(1,128)}, u32[]{:S(2)}, u32[]{:S(2)}) %all-to-all-start) | async-done | bytes 2105376 | tf_op jit(solution)/shard_map/all_to_all | solution.py:123
  70.8 1.7 copy.82
  72.5 1.8 gather_fusion.1
  74.4 1.4 broadcast_select_fusion
  78.8 6.8 %scatter_fusion = f32[2176,128]{1,0:T(8,128)S(1)} fusion(f32[2176,128]{1,0:T(8,128)S(1)} %copy-done.1, s32[1024]{0:T(1024)S(1)} %fusion.56, f32[1024,128]{1,0:T(8,128)} %bitcast.150), kind=kCustom, calls=%fused_computation.7 | custom fusion | flops 131072 | bytes 1576960 | tf_op jit(solution)/shard_map/scatter-add | solution.py:147
  87.0 2.3 shard_map.183
  90.3 1.5 collective-permute-start.2
  91.8 3.8 %fusion.21 = (f32[2176,128]{1,0:T(8,128)S(1)}, bf16[2176,128]{1,0:T(8,128)(2,1)S(1)}) fusion(f32[2176,1]{1,0:T(8,128)} %copy.40, f32[2176,128]{1,0:T(8,128)} %copy-done.3, f32[2176,1]{1,0:T(8,128)} %copy.38, f32[2176,128]{1,0:T(8,128)S(1)} %scatter_fusion, bf16[1,2176,128]{2,1,0:T(8,128)(2,1)} %param.17, f32[2176]{0:T(1024)S(1)} %reduce.3, f32[2176]{0:T(1024)S(1)} %reduce.2), kind=kLoop, calls=%fused_computation.32 | loop fusion | flops 3620864 | bytes 4491264 | tf_op jit(solution)/shard_map/add | solution.py:152
  95.7 4.5 %collective-permute-start.3 = (f32[2,128]{1,0:T(2,128)S(1)}, f32[2,128]{1,0:T(2,128)S(1)}, u32[]{:S(2)}, u32[]{:S(2)}) collective-permute-start(f32[2,128]{1,0:T(2,128)S(1)} %pad_maximum_fusion.6), channel_id=1, source_target_pairs={{0,1},{1,2},{2,3},{3,4},{4,5},{5,6},{6,7},{7,8},{8,9},{9,10},{10,1... | collective-permute-start | bytes 3080 | tf_op jit(solution)/shard_map/ppermute | solution.py:59
  102.0 4.2 %collective-permute-start.4 = (f32[2,128]{1,0:T(2,128)}, f32[2,128]{1,0:T(2,128)}, u32[]{:S(2)}, u32[]{:S(2)}) collective-permute-start(f32[2,128]{1,0:T(2,128)} %pad_maximum_fusion.7), channel_id=1, source_target_pairs={{0,2},{1,3},{2,4},{3,5},{4,6},{5,7},{6,8},{7,9},{8,10},{9,11},{10,... | collective-permute-start | bytes 3080 | tf_op jit(solution)/shard_map/ppermute | solution.py:59
  106.9 3.2 %gather_fusion.3 = bf16[1024,128]{1,0:T(8,128)(2,1)S(1)} fusion(bf16[2176,128]{1,0:T(8,128)(2,1)S(1)} %fusion.23, s32[1024]{0:T(1024)S(1)} %copy-done.32), kind=kCustom, calls=%fused_computation.3 | custom fusion | bytes 528384 | tf_op jit(solution)/shard_map/gather | solution.py:138
  111.0 1.6 scatter_custom_fusion.3
  112.7 2.1 all_to_all.19
  114.8 6.8 %all-to-all-start.1 = ((f32[16,1,16384]{2,1,0:T(1,128)}), f32[16,1,16384]{2,1,0:T(1,128)}, u32[]{:S(2)}, u32[]{:S(2)}) async-start(f32[16,1,16384]{2,1,0:T(1,128)} %all_to_all.19), calls=%async_computation.1 | async-start | bytes 2097152 | tf_op jit(solution)/shard_map/all_to_all | solution.py:123
  122.3 6.4 %collective-permute-start.5 = (f32[2,128]{1,0:T(2,128)S(1)}, f32[2,128]{1,0:T(2,128)S(1)}, u32[]{:S(2)}, u32[]{:S(2)}) collective-permute-start(f32[2,128]{1,0:T(2,128)S(1)} %pad_maximum_fusion.8), channel_id=1, source_target_pairs={{0,4},{1,5},{2,6},{3,7},{4,8},{5,9},{6,10},{7,11},{8,12},{9,13},{1... | collective-permute-start | bytes 3080 | tf_op jit(solution)/shard_map/ppermute | solution.py:59
  128.8 1.3 collective-permute-done.5
  130.1 9.9 %collective-permute-start.6 = (f32[2,128]{1,0:T(2,128)S(1)}, f32[2,128]{1,0:T(2,128)S(1)}, u32[]{:S(2)}, u32[]{:S(2)}) collective-permute-start(f32[2,128]{1,0:T(2,128)S(1)} %pad_maximum_fusion.9), channel_id=1, source_target_pairs={{0,8},{1,9},{2,10},{3,11},{4,12},{5,13},{6,14},{7,15},{8,16},{9,17... | collective-permute-start | bytes 3080 | tf_op jit(solution)/shard_map/ppermute | solution.py:59
  141.3 13.8 %collective-permute-start.7 = (f32[2,128]{1,0:T(2,128)S(1)}, f32[2,128]{1,0:T(2,128)S(1)}, u32[]{:S(2)}, u32[]{:S(2)}) collective-permute-start(f32[2,128]{1,0:T(2,128)S(1)} %pad_maximum_fusion.10), channel_id=1, source_target_pairs={{0,16},{1,17},{2,18},{3,19},{4,20},{5,21},{6,22},{7,23},{8,24},{9,... | collective-permute-start | bytes 3080 | tf_op jit(solution)/shard_map/ppermute | solution.py:59
  156.5 2.2 scatter_custom_fusion.2
  158.7 7.0 %fusion.7 = f32[2176,128]{1,0:T(8,128)S(1)} fusion(bf16[2176,128]{1,0:T(8,128)(2,1)} %bitcast.146, bf16[1,2176,2176]{2,1,0:T(8,128)(2,1)} %param.20, f32[2176,128]{1,0:T(8,128)} %scatter_custom_fusion.2, f32[2176,128]{1,0:T(8,128)S(1)} %get-tuple-element.29, bf16[1,2176,128]{2,1,0:T(8,128)(2,1)} %param.18), kind=kOutput, calls=%fused_computation.16 | convolution fusion | flops 1213267968 | bytes 13926400 | tf_op jit(solution)/shard_map/dot_general | solution.py:149
  165.8 2.8 %copy.83 = f32[16,1,16384]{2,0,1:T(8,128)} copy(f32[16,1,16384]{2,1,0:T(1,128)} %all-to-all-done.1) | data formatting | bytes 2097152
  168.6 3.1 %gather_fusion.4 = f32[8,16384]{1,0:T(8,128)} fusion(f32[16,16384]{1,0:T(8,128)} %bitcast.136, s32[1024]{0:T(1024)} %copy-done.38), kind=kCustom, calls=%fused_computation.4 | custom fusion | bytes 1048608 | tf_op jit(solution)/shard_map/jit(_take)/gather | solution.py:124
  171.7 3.0 %fusion.42 = f32[8,128,128]{2,1,0:T(8,128)} fusion(bf16[1,8,128,128]{3,2,1,0:T(8,128)(2,1)} %param.19, f32[8,128,128]{2,1,0:T(8,128)} %bitcast.144, f32[8,128,128]{2,0,1:T(8,128)} %bitcast.142, f32[8,128,128]{2,0,1:T(8,128)} %copy-done.10, f32[8,128]{1,0:T(8,128)S(1)} %slice-done, f32[8,128]{1,0:T(8,128)S(1)} %bitcast.155, f32[8,128]{1,0:T(8,128)S(1)} %bitcast.158, ...), kind=kLoop, calls=%fused_computation.68 | loop fusion | flops 1572864 | bytes 3420168 | tf_op jit(solution)/shard_map/add | solution.py:146
  174.7 6.8 %scatter_fusion.1 = f32[2176,128]{1,0:T(8,128)S(1)} fusion(f32[2176,128]{1,0:T(8,128)S(1)} %fusion.7, s32[1024]{0:T(1024)S(1)} %copy-done.30, f32[1024,128]{1,0:T(8,128)} %bitcast.149), kind=kCustom, calls=%fused_computation.10 | custom fusion | flops 131072 | bytes 1576960 | tf_op jit(solution)/shard_map/scatter-add | solution.py:147
  183.1 2.3 shard_map.184
  187.4 1.3 collective-permute-start.10
  188.7 1.7 fusion.91
  190.4 1.6 copy.43
  192.0 1.6 copy.45
  193.6 1.3 collective-permute-start.9
  194.9 3.9 %collective-permute-start.8 = (f32[2176,1]{0,1:T(1,128)S(1)}, f32[2176,1]{0,1:T(1,128)S(1)}, u32[]{:S(2)}, u32[]{:S(2)}) collective-permute-start(f32[2176,1]{0,1:T(1,128)S(1)} %copy.43), channel_id=1, source_target_pairs={{0,1},{1,2},{2,3},{3,4},{4,5},{5,6},{6,7},{7,8},{8,9},{9,10},{10,1... | collective-permute-start | bytes 26120 | tf_op jit(solution)/shard_map/ppermute | solution.py:23
  198.8 3.9 %collective-permute-start.11 = (f32[2,128]{1,0:T(2,128)S(1)}, f32[2,128]{1,0:T(2,128)S(1)}, u32[]{:S(2)}, u32[]{:S(2)}) collective-permute-start(f32[2,128]{1,0:T(2,128)S(1)} %pad_maximum_fusion.12), channel_id=1, source_target_pairs={{0,1},{1,2},{2,3},{3,4},{4,5},{5,6},{6,7},{7,8},{8,9},{9,10},{10,1... | collective-permute-start | bytes 3080 | tf_op jit(solution)/shard_map/ppermute | solution.py:59
  202.7 1.4 copy.44
  204.1 1.4 copy.46
  205.6 2.7 %collective-permute-start.12 = (f32[2,128]{1,0:T(2,128)S(1)}, f32[2,128]{1,0:T(2,128)S(1)}, u32[]{:S(2)}, u32[]{:S(2)}) collective-permute-start(f32[2,128]{1,0:T(2,128)S(1)} %pad_maximum_fusion.13), channel_id=1, source_target_pairs={{0,2},{1,3},{2,4},{3,5},{4,6},{5,7},{6,8},{7,9},{8,10},{9,11},{10,... | collective-permute-start | bytes 3080 | tf_op jit(solution)/shard_map/ppermute | solution.py:59
  208.2 3.6 %fusion.37 = (bf16[1,2176,128]{2,1,0:T(8,128)(2,1)}, bf16[2176,128]{1,0:T(8,128)(2,1)S(1)}) fusion(f32[2176,1]{1,0:T(8,128)} %copy.46, f32[2176,128]{1,0:T(8,128)S(1)} %get-tuple-element.29, f32[2176,1]{1,0:T(8,128)} %copy.44, f32[2176]{0:T(1024)S(1)} %copy-done.27, f32[2176,128]{1,0:T(8,128)S(1)} %scatter_fusion.1, f32[2176]{0:T(1024)S(1)} %reduce.2), kind=kLoop, calls=%fused_computation.62 | loop fusion | flops 3620864 | bytes 3377152 | tf_op jit(solution)/shard_map/broadcast_in_dim | solution.py:173
  211.8 6.5 %collective-permute-start.13 = (f32[2,128]{1,0:T(2,128)S(1)}, f32[2,128]{1,0:T(2,128)S(1)}, u32[]{:S(2)}, u32[]{:S(2)}) collective-permute-start(f32[2,128]{1,0:T(2,128)S(1)} %pad_maximum_fusion.14), channel_id=1, source_target_pairs={{0,4},{1,5},{2,6},{3,7},{4,8},{5,9},{6,10},{7,11},{8,12},{9,13},{1... | collective-permute-start | bytes 3080 | tf_op jit(solution)/shard_map/ppermute | solution.py:59
  219.7 11.2 %collective-permute-start.14 = (f32[2,128]{1,0:T(2,128)S(1)}, f32[2,128]{1,0:T(2,128)S(1)}, u32[]{:S(2)}, u32[]{:S(2)}) collective-permute-start(f32[2,128]{1,0:T(2,128)S(1)} %pad_maximum_fusion.15), channel_id=1, source_target_pairs={{0,8},{1,9},{2,10},{3,11},{4,12},{5,13},{6,14},{7,15},{8,16},{9,17... | collective-permute-start | bytes 3080 | tf_op jit(solution)/shard_map/ppermute | solution.py:59
  232.2 17.5 %collective-permute-start.15 = (f32[2,128]{1,0:T(2,128)S(1)}, f32[2,128]{1,0:T(2,128)S(1)}, u32[]{:S(2)}, u32[]{:S(2)}) collective-permute-start(f32[2,128]{1,0:T(2,128)S(1)} %pad_maximum_fusion.16), channel_id=1, source_target_pairs={{0,16},{1,17},{2,18},{3,19},{4,20},{5,21},{6,22},{7,23},{8,24},{9,... | collective-permute-start | bytes 3080 | tf_op jit(solution)/shard_map/ppermute | solution.py:59
  (186 shorter events, 26.4 us)
Async XLA Ops:
  0.6 99.6 %copy-start = (bf16[1,34,64,64]{3,2,1,0:T(8,128)(2,1)S(1)}, bf16[1,34,64,64]{3,2,1,0:T(8,128)(2,1)}, u32[]{:S(2)}) copy-start(bf16[1,34,64,64]{3,2,1,0:T(8,128)(2,1)} %param.21) | copy-start | bytes 835588
  7.1 22.6 %copy-start.49 = (s32[8]{0:T(128)}, s32[8]{0:T(128)S(1)}, u32[]{:S(2)}) copy-start(s32[8]{0:T(128)S(1)} %get-tuple-element.24) | copy-start | bytes 100
  13.3 10.1 %copy-start.18 = (bf16[1,2176,128]{2,1,0:T(8,128)(2,1)S(1)}, bf16[1,2176,128]{2,1,0:T(8,128)(2,1)}, u32[]{:S(2)}) copy-start(bf16[1,2176,128]{2,1,0:T(8,128)(2,1)} %param.17) | copy-start | bytes 1671172
  13.3 57.5 %all-to-all-start = ((f32[16,1,32896]{2,1,0:T(1,128)}), f32[16,1,32896]{2,1,0:T(1,128)}, u32[]{:S(2)}, u32[]{:S(2)}) async-start(f32[16,1,32896]{2,1,0:T(1,128)} %all_to_all.16), calls=%async_computation | async-start | bytes 4210688 | tf_op jit(solution)/shard_map/all_to_all | solution.py:123
  24.5 5.3 %copy-start.52 = (s32[1,128]{1,0:T(1,128)S(1)}, s32[1,128]{1,0:T(1,128)}, u32[]{:S(2)}) copy-start(s32[1,128]{1,0:T(1,128)} %param.28) | copy-start | bytes 1540
  24.5 5.3 %copy-start.53 = (f32[1,128]{1,0:T(1,128)S(1)}, f32[1,128]{1,0:T(1,128)}, u32[]{:S(2)}) copy-start(f32[1,128]{1,0:T(1,128)} %param.29) | copy-start | bytes 1540
  24.5 5.3 %copy-start.35 = (s32[1,8,128]{2,1,0:T(8,128)S(1)}, s32[1,8,128]{2,1,0:T(8,128)}, u32[]{:S(2)}) copy-start(s32[1,8,128]{2,1,0:T(8,128)} %param.25) | copy-start | bytes 12292
  24.5 5.3 %copy-start.2 = (bf16[1,2176,128]{2,1,0:T(8,128)(2,1)S(1)}, bf16[1,2176,128]{2,1,0:T(8,128)(2,1)}, u32[]{:S(2)}) copy-start(bf16[1,2176,128]{2,1,0:T(8,128)(2,1)} %param.16) | copy-start | bytes 1671172
  24.9 14.9 %collective-permute-start.1 = (f32[2176,1]{0,1:T(1,128)S(1)}, f32[2176,1]{0,1:T(1,128)S(1)}, u32[]{:S(2)}, u32[]{:S(2)}) collective-permute-start(f32[2176,1]{0,1:T(1,128)S(1)} %copy.39), channel_id=1, source_target_pairs={{1,0},{2,1},{3,2},{4,3},{5,4},{6,5},{7,6},{8,7},{9,8},{10,9},{11,1... | collective-permute-start | bytes 26120 | tf_op jit(solution)/shard_map/ppermute | solution.py:24
  26.6 11.7 %collective-permute-start = (f32[2176,1]{0,1:T(1,128)S(1)}, f32[2176,1]{0,1:T(1,128)S(1)}, u32[]{:S(2)}, u32[]{:S(2)}) collective-permute-start(f32[2176,1]{0,1:T(1,128)S(1)} %copy.37), channel_id=1, source_target_pairs={{0,1},{1,2},{2,3},{3,4},{4,5},{5,6},{6,7},{7,8},{8,9},{9,10},{10,1... | collective-permute-start | bytes 26120 | tf_op jit(solution)/shard_map/ppermute | solution.py:23
  29.7 42.8 %copy-start.38 = (s32[1024]{0:T(1024)}, s32[1024]{0:T(1024)S(1)}, u32[]{:S(2)}) copy-start(s32[1024]{0:T(1024)S(1)} %pad_clamp_fusion.1) | copy-start | bytes 12292
  29.8 44.6 %copy-start.40 = (pred[8]{0:T(512)(128)(4,1)}, pred[8]{0:T(512)(128)(4,1)S(1)}, u32[]{:S(2)}) copy-start(pred[8]{0:T(512)(128)(4,1)S(1)} %compare_and_fusion) | copy-start | bytes 28
  29.8 7.6 %copy-start.51 = (s32[128]{0:T(128)}, s32[128]{0:T(128)S(1)}, u32[]{:S(2)}) copy-start(s32[128]{0:T(128)S(1)} %fusion.87) | copy-start | bytes 1540
  29.8 56.5 %copy-start.47 = (f32[128]{0:T(128)}, f32[128]{0:T(128)S(1)}, u32[]{:S(2)}) copy-start(f32[128]{0:T(128)S(1)} %negate_bitcast_fusion) | copy-start | bytes 1540
  29.9 48.6 %copy-start.29 = (s32[1024]{0:T(1024)}, s32[1024]{0:T(1024)S(1)}, u32[]{:S(2)}) copy-start(s32[1024]{0:T(1024)S(1)} %fusion.56) | copy-start | bytes 12292
  29.9 7.5 %copy-start.17 = (bf16[1024,128]{1,0:T(8,128)(2,1)S(1)}, bf16[1024,128]{1,0:T(8,128)(2,1)}, u32[]{:S(2)}) copy-start(bf16[1024,128]{1,0:T(8,128)(2,1)} %copy-done.16) | copy-start | bytes 786436
  29.9 8.3 %copy-start.36 = (f32[1,2176]{1,0:T(1,128)S(1)}, f32[1,2176]{1,0:T(1,128)}, u32[]{:S(2)}) copy-start(f32[1,2176]{1,0:T(1,128)} %param.22) | copy-start | bytes 26116
  29.9 8.4 %copy-start.37 = (f32[1,2176]{1,0:T(1,128)S(1)}, f32[1,2176]{1,0:T(1,128)}, u32[]{:S(2)}) copy-start(f32[1,2176]{1,0:T(1,128)} %param.23) | copy-start | bytes 26116
  37.4 48.2 %copy-start.39 = (s32[1024]{0:T(1024)}, s32[1024]{0:T(1024)S(1)}, u32[]{:S(2)}) copy-start(s32[1024]{0:T(1024)S(1)} %pad_clamp_fusion) | copy-start | bytes 12292
  38.3 53.5 %copy-start.26 = (f32[2176]{0:T(1024)}, f32[2176]{0:T(1024)S(1)}, u32[]{:S(2)}) copy-start(f32[2176]{0:T(1024)S(1)} %reduce.3) | copy-start | bytes 26116
  90.3 5.3 %collective-permute-start.2 = (f32[2,128]{1,0:T(2,128)S(1)}, f32[2,128]{1,0:T(2,128)S(1)}, u32[]{:S(2)}, u32[]{:S(2)}) collective-permute-start(f32[2,128]{1,0:T(2,128)S(1)} %pad_maximum_fusion.5), channel_id=1, source_target_pairs={{0,1},{1,2},{2,3},{3,4},{4,5},{5,6},{6,7},{7,8},{8,9},{9,10},{10,1... | collective-permute-start | bytes 3080 | tf_op jit(solution)/shard_map/ppermute | solution.py:59
  95.7 5.6 %collective-permute-start.3 = (f32[2,128]{1,0:T(2,128)S(1)}, f32[2,128]{1,0:T(2,128)S(1)}, u32[]{:S(2)}, u32[]{:S(2)}) collective-permute-start(f32[2,128]{1,0:T(2,128)S(1)} %pad_maximum_fusion.6), channel_id=1, source_target_pairs={{0,1},{1,2},{2,3},{3,4},{4,5},{5,6},{6,7},{7,8},{8,9},{9,10},{10,1... | collective-permute-start | bytes 3080 | tf_op jit(solution)/shard_map/ppermute | solution.py:59
  102.0 19.5 %collective-permute-start.4 = (f32[2,128]{1,0:T(2,128)}, f32[2,128]{1,0:T(2,128)}, u32[]{:S(2)}, u32[]{:S(2)}) collective-permute-start(f32[2,128]{1,0:T(2,128)} %pad_maximum_fusion.7), channel_id=1, source_target_pairs={{0,2},{1,3},{2,4},{3,5},{4,6},{5,7},{6,8},{7,9},{8,10},{9,11},{10,... | collective-permute-start | bytes 3080 | tf_op jit(solution)/shard_map/ppermute | solution.py:59
  114.7 6.8 %copy-start.43 = (f32[1,128]{1,0:T(1,128)S(1)}, f32[1,128]{1,0:T(1,128)}, u32[]{:S(2)}) copy-start(f32[1,128]{1,0:T(1,128)} %copy-done.42) | copy-start | bytes 1540
  114.8 6.8 %copy-start.45 = (f32[1,128]{1,0:T(1,128)S(1)}, f32[1,128]{1,0:T(1,128)}, u32[]{:S(2)}) copy-start(f32[1,128]{1,0:T(1,128)} %copy-done.44) | copy-start | bytes 1540
  114.8 41.7 %copy-start.24 = (f32[128,128]{1,0:T(8,128)S(1)}, f32[128,128]{1,0:T(8,128)}, u32[]{:S(2)}) copy-start(f32[128,128]{1,0:T(8,128)} %get-tuple-element.9) | copy-start | bytes 196612
  114.8 41.7 %copy-start.25 = (f32[128,128]{1,0:T(8,128)S(1)}, f32[128,128]{1,0:T(8,128)}, u32[]{:S(2)}) copy-start(f32[128,128]{1,0:T(8,128)} %get-tuple-element.8) | copy-start | bytes 196612
  114.8 41.7 %copy-start.50 = (f32[1,128]{1,0:T(1,128)S(1)}, f32[1,128]{1,0:T(1,128)}, u32[]{:S(2)}) copy-start(f32[1,128]{1,0:T(1,128)} %param.30) | copy-start | bytes 1540
  114.8 51.0 %all-to-all-start.1 = ((f32[16,1,16384]{2,1,0:T(1,128)}), f32[16,1,16384]{2,1,0:T(1,128)}, u32[]{:S(2)}, u32[]{:S(2)}) async-start(f32[16,1,16384]{2,1,0:T(1,128)} %all_to_all.19), calls=%async_computation.1 | async-start | bytes 2097152 | tf_op jit(solution)/shard_map/all_to_all | solution.py:123
  122.3 7.7 %collective-permute-start.5 = (f32[2,128]{1,0:T(2,128)S(1)}, f32[2,128]{1,0:T(2,128)S(1)}, u32[]{:S(2)}, u32[]{:S(2)}) collective-permute-start(f32[2,128]{1,0:T(2,128)S(1)} %pad_maximum_fusion.8), channel_id=1, source_target_pairs={{0,4},{1,5},{2,6},{3,7},{4,8},{5,9},{6,10},{7,11},{8,12},{9,13},{1... | collective-permute-start | bytes 3080 | tf_op jit(solution)/shard_map/ppermute | solution.py:59
  130.1 11.2 %collective-permute-start.6 = (f32[2,128]{1,0:T(2,128)S(1)}, f32[2,128]{1,0:T(2,128)S(1)}, u32[]{:S(2)}, u32[]{:S(2)}) collective-permute-start(f32[2,128]{1,0:T(2,128)S(1)} %pad_maximum_fusion.9), channel_id=1, source_target_pairs={{0,8},{1,9},{2,10},{3,11},{4,12},{5,13},{6,14},{7,15},{8,16},{9,17... | collective-permute-start | bytes 3080 | tf_op jit(solution)/shard_map/ppermute | solution.py:59
  141.3 15.1 %collective-permute-start.7 = (f32[2,128]{1,0:T(2,128)S(1)}, f32[2,128]{1,0:T(2,128)S(1)}, u32[]{:S(2)}, u32[]{:S(2)}) collective-permute-start(f32[2,128]{1,0:T(2,128)S(1)} %pad_maximum_fusion.10), channel_id=1, source_target_pairs={{0,16},{1,17},{2,18},{3,19},{4,20},{5,21},{6,22},{7,23},{8,24},{9,... | collective-permute-start | bytes 3080 | tf_op jit(solution)/shard_map/ppermute | solution.py:59
  174.7 7.6 %copy-start.48 = (f32[128]{0:T(128)S(1)}, f32[128]{0:T(128)}, u32[]{:S(2)}) copy-start(f32[128]{0:T(128)} %copy-done.47) | copy-start | bytes 1540
  187.4 11.4 %collective-permute-start.10 = (f32[2,128]{1,0:T(2,128)S(1)}, f32[2,128]{1,0:T(2,128)S(1)}, u32[]{:S(2)}, u32[]{:S(2)}) collective-permute-start(f32[2,128]{1,0:T(2,128)S(1)} %pad_maximum_fusion.11), channel_id=1, source_target_pairs={{0,1},{1,2},{2,3},{3,4},{4,5},{5,6},{6,7},{7,8},{8,9},{9,10},{10,1... | collective-permute-start | bytes 3080 | tf_op jit(solution)/shard_map/ppermute | solution.py:59
  193.6 10.5 %collective-permute-start.9 = (f32[2176,1]{0,1:T(1,128)S(1)}, f32[2176,1]{0,1:T(1,128)S(1)}, u32[]{:S(2)}, u32[]{:S(2)}) collective-permute-start(f32[2176,1]{0,1:T(1,128)S(1)} %copy.45), channel_id=1, source_target_pairs={{1,0},{2,1},{3,2},{4,3},{5,4},{6,5},{7,6},{8,7},{9,8},{10,9},{11,1... | collective-permute-start | bytes 26120 | tf_op jit(solution)/shard_map/ppermute | solution.py:24
  194.9 7.8 %collective-permute-start.8 = (f32[2176,1]{0,1:T(1,128)S(1)}, f32[2176,1]{0,1:T(1,128)S(1)}, u32[]{:S(2)}, u32[]{:S(2)}) collective-permute-start(f32[2176,1]{0,1:T(1,128)S(1)} %copy.43), channel_id=1, source_target_pairs={{0,1},{1,2},{2,3},{3,4},{4,5},{5,6},{6,7},{7,8},{8,9},{9,10},{10,1... | collective-permute-start | bytes 26120 | tf_op jit(solution)/shard_map/ppermute | solution.py:23
  198.8 9.4 %copy-start.27 = (f32[2176]{0:T(1024)S(1)}, f32[2176]{0:T(1024)}, u32[]{:S(2)}) copy-start(f32[2176]{0:T(1024)} %copy-done.26) | copy-start | bytes 26116
  198.8 6.7 %collective-permute-start.11 = (f32[2,128]{1,0:T(2,128)S(1)}, f32[2,128]{1,0:T(2,128)S(1)}, u32[]{:S(2)}, u32[]{:S(2)}) collective-permute-start(f32[2,128]{1,0:T(2,128)S(1)} %pad_maximum_fusion.12), channel_id=1, source_target_pairs={{0,1},{1,2},{2,3},{3,4},{4,5},{5,6},{6,7},{7,8},{8,9},{9,10},{10,1... | collective-permute-start | bytes 3080 | tf_op jit(solution)/shard_map/ppermute | solution.py:59
  205.6 6.2 %collective-permute-start.12 = (f32[2,128]{1,0:T(2,128)S(1)}, f32[2,128]{1,0:T(2,128)S(1)}, u32[]{:S(2)}, u32[]{:S(2)}) collective-permute-start(f32[2,128]{1,0:T(2,128)S(1)} %pad_maximum_fusion.13), channel_id=1, source_target_pairs={{0,2},{1,3},{2,4},{3,5},{4,6},{5,7},{6,8},{7,9},{8,10},{9,11},{10,... | collective-permute-start | bytes 3080 | tf_op jit(solution)/shard_map/ppermute | solution.py:59
  211.8 7.8 %collective-permute-start.13 = (f32[2,128]{1,0:T(2,128)S(1)}, f32[2,128]{1,0:T(2,128)S(1)}, u32[]{:S(2)}, u32[]{:S(2)}) collective-permute-start(f32[2,128]{1,0:T(2,128)S(1)} %pad_maximum_fusion.14), channel_id=1, source_target_pairs={{0,4},{1,5},{2,6},{3,7},{4,8},{5,9},{6,10},{7,11},{8,12},{9,13},{1... | collective-permute-start | bytes 3080 | tf_op jit(solution)/shard_map/ppermute | solution.py:59
  218.4 12.5 %copy-start.5 = (f32[34,128,64]{1,2,0:T(8,128)S(1)}, f32[34,128,64]{1,2,0:T(8,128)}, u32[]{:S(2)}) copy-start(f32[34,128,64]{1,2,0:T(8,128)} %copy-done.4) | copy-start | bytes 3342340
  219.7 30.0 %copy-start.7 = (f32[1024,128]{1,0:T(8,128)S(1)}, f32[1024,128]{1,0:T(8,128)}, u32[]{:S(2)}) copy-start(f32[1024,128]{1,0:T(8,128)} %convert_element_type.137) | copy-start | bytes 1572868
  219.7 30.0 %copy-start.8 = (f32[8,16384]{1,0:T(8,128)S(1)}, f32[8,16384]{1,0:T(8,128)}, u32[]{:S(2)}) copy-start(f32[8,16384]{1,0:T(8,128)} %gather_fusion.4) | copy-start | bytes 1572868
  219.7 30.0 %copy-start.9 = (f32[1024,128]{1,0:T(8,128)S(1)}, f32[1024,128]{1,0:T(8,128)}, u32[]{:S(2)}) copy-start(f32[1024,128]{1,0:T(8,128)} %convert_element_type.138) | copy-start | bytes 1572868
  219.7 30.0 %copy-start.15 = (bf16[1,8,128,128]{3,2,1,0:T(8,128)(2,1)S(1)}, bf16[1,8,128,128]{3,2,1,0:T(8,128)(2,1)}, u32[]{:S(2)}) copy-start(bf16[1,8,128,128]{3,2,1,0:T(8,128)(2,1)} %param.19) | copy-start | bytes 786436
  219.7 30.0 %copy-start.20 = (f32[1,8,128,128]{3,1,2,0:T(8,128)S(1)}, f32[1,8,128,128]{3,1,2,0:T(8,128)}, u32[]{:S(2)}) copy-start(f32[1,8,128,128]{3,1,2,0:T(8,128)} %get-tuple-element.33) | copy-start | bytes 1572868
  219.7 12.5 %collective-permute-start.14 = (f32[2,128]{1,0:T(2,128)S(1)}, f32[2,128]{1,0:T(2,128)S(1)}, u32[]{:S(2)}, u32[]{:S(2)}) collective-permute-start(f32[2,128]{1,0:T(2,128)S(1)} %pad_maximum_fusion.15), channel_id=1, source_target_pairs={{0,8},{1,9},{2,10},{3,11},{4,12},{5,13},{6,14},{7,15},{8,16},{9,17... | collective-permute-start | bytes 3080 | tf_op jit(solution)/shard_map/ppermute | solution.py:59
  232.2 18.8 %collective-permute-start.15 = (f32[2,128]{1,0:T(2,128)S(1)}, f32[2,128]{1,0:T(2,128)S(1)}, u32[]{:S(2)}, u32[]{:S(2)}) collective-permute-start(f32[2,128]{1,0:T(2,128)S(1)} %pad_maximum_fusion.16), channel_id=1, source_target_pairs={{0,16},{1,17},{2,18},{3,19},{4,20},{5,21},{6,22},{7,23},{8,24},{9,... | collective-permute-start | bytes 3080 | tf_op jit(solution)/shard_map/ppermute | solution.py:59
  (25 other events, 58.7 us)

commit v3 on v1

--- a/solution.py
+++ b/solution.py
@@ -107,16 +107,21 @@
     charge_state = jnp.zeros_like(kept_local)
     rounds, lines = edge_rows.shape
 
-    def exchanged(parts):
-        flat = jnp.concatenate([part.reshape(rounds, -1) for part in parts], axis=1)
-        blank = jnp.zeros((area_count, flat.shape[1]), flat.dtype)
-        sent = blank.at[partners].set(flat)
+    slot_ids = jnp.arange(area_count, dtype=jnp.int32)
+    round_ids = jnp.arange(rounds, dtype=jnp.int32)
+    round_of = jnp.sum(jnp.where(partners[:, None] == slot_ids[None, :], round_ids[:, None], 0), axis=0)
+    slot_rows = jnp.take(edge_rows, round_of, axis=0)
+
+    def exchanged(parts, shapes):
+        lanes = 128
+        sent = jnp.concatenate([part.reshape(area_count, -1, lanes) for part in parts], axis=1)
+        sent = jnp.pad(sent, ((0, 0), (0, -sent.shape[1] % 8), (0, 0)))
         got = lax.all_to_all(sent, "area", split_axis=0, concat_axis=0, tiled=True)
-        got = jnp.take(got, partners, axis=0)
+        got = jnp.take(got, partners, axis=0).reshape(rounds, -1)
         found, at = [], 0
-        for part in parts:
-            width = part.size // rounds
-            found.append(got[:, at : at + width].reshape(part.shape))
+        for shape in shapes:
+            width = math.prod(shape[1:])
+            found.append(got[:, at : at + width].reshape(shape))
             at += width
         return found
 
@@ -127,11 +132,16 @@
     for iteration in range(ITERS):
         rounded = angle_now.astype(jnp.bfloat16)
         own_edge = rounded[edge_rows].astype(jnp.float32)
+        edge_out = rounded[slot_rows].astype(jnp.float32)
         if iteration == 0:
-            far_edge, price_far, penalty_far = exchanged((own_edge, price_now, tie_penalty[0]))
+            far_edge, price_far, penalty_far = exchanged(
+                (edge_out, jnp.take(price_now, round_of, axis=0),
+                 jnp.take(tie_penalty[0], round_of, axis=0)),
+                (own_edge.shape, price_now.shape, tie_penalty[0].shape),
+            )
             penalty_far = penalty_far[:, :, None]
         else:
-            (far_edge,) = exchanged((own_edge,))
+            (far_edge,) = exchanged((edge_out,), (own_edge.shape,))
             price_far = price_far - penalty_far * mismatch
         mismatch = own_edge - far_edge
         tie_flow = tie_gain * mismatch + 0.5 * (price_now - price_far)

time: 198 us -> 196 us (0.990)
  waiting for transfers between devices: 33.8 us -> 30.5 us
  local copies, waits for them, and re-layouts: 48.7 us -> 51.6 us
    gather x2 -> x7, local copies, waits for them, and re-layouts: 4.77 us -> 21.8 us  [the longest x2 12.9 us: local(): edge_out = rounded[slot_rows].astype(jnp.float32)]
    all_to_all x2 -> x0, local copies, waits for them, and re-layouts: 4.84 us -> none  [exchanged(): got = lax.all_to_all(sent, 'area', split_axis=0, concat_axis=0, tiled=True)]
    unnamed x75 -> x59, local copies, waits for them, and re-layouts: 10.4 us -> 6.25 us
    scatter x2 -> x0, local copies, waits for them, and re-layouts: 3.97 us -> none  [exchanged(): sent = blank.at[partners].set(flat)]
    all_to_all x2, waiting for transfers between devices: 31.9 us -> 28.8 us  [exchanged(): got = lax.all_to_all(sent, 'area', split_axis=0, concat_axis=0, tiled=True)]
  transfers between devices with their start and end apart: 8 -> 8, of which waited for: 4 -> 2; matrix products, arithmetic and copies ran while one was open for 24% -> 27% of each run, Pallas kernels for 0% -> 0%
where the time goes in v3:
time: 196 us; the launch traced here: 195 us
  starting transfers between devices  53.4 us (27%)
  local copies, waits for them, and re-layouts  51.6 us (26%)
  other arithmetic  38.6 us (20%)
  waiting for transfers between devices  30.5 us (16%)
  matrix products  15.1 us (8%)
  Pallas kernels  4.54 us (2%)
    all_to_all x2, waiting for transfers between devices, exchanged(): got = lax.all_to_all(sent, 'area', split_axis=0, concat_axis=0, tiled=True)  28.8 us
    all_to_all x2, starting transfers between devices, local(): ends = lax.all_to_all(copies, 'tm', split_axis=0, concat_axis=0, tiled=True)  27.8 us
    all_to_all x2, starting transfers between devices, exchanged(): got = lax.all_to_all(sent, 'area', split_axis=0, concat_axis=0, tiled=True)  14.1 us
    dot_general x2, matrix products, local(): jnp.dot(matrix, rounded, preferred_element_type=jnp.float32) + fixed_part  13.7 us
    scatter-add x2, other arithmetic, local(): jnp.zeros((bus_count, hour_count), jnp.float32).at[edge_rows].add(tie_flow)  13.7 us
    gather x2, local copies, waits for them, and re-layouts, local(): edge_out = rounded[slot_rows].astype(jnp.float32)  12.9 us
    gather x2, local copies, waits for them, and re-layouts, local(): own_edge = rounded[edge_rows].astype(jnp.float32)  6.42 us
    unnamed x59, local copies, waits for them, and re-layouts  6.25 us
  transfers between devices with their start and end apart: 8, of which 2 were waited for; matrix products, arithmetic and copies ran while one was open for 27% of the time, Pallas kernels for 0%

profile of v3, /device:TPU:1, one launch (start us, length us, event | category | flops | bytes accessed | tf_op | source)
XLA Modules:
  0.0 195.1 jit_solution(17895426053662613561)
XLA Ops:
  0.7 1.0 fusion.51
  1.7 1.2 gather_fusion.4
  3.0 1.2 gather_fusion.1
  4.4 6.7 %gather_fusion.2 = bf16[2048,128]{1,0:T(8,128)(2,1)S(1)} fusion(bf16[2176,128]{1,0:T(8,128)(2,1)} %bitcast.1281, s32[2048]{0:T(1024)S(1)} %fusion.49), kind=kCustom, calls=%fused_computation.2 | custom fusion | bytes 1056768 | tf_op jit(solution)/shard_map/gather | solution.py:135
  12.9 1.5 select_maximum_fusion
  14.4 9.7 %all-to-all-start = ((f32[16,264,128]{2,1,0:T(8,128)}), f32[16,264,128]{2,1,0:T(8,128)}, u32[]{:S(2)}, u32[]{:S(2)}) async-start(f32[16,264,128]{2,1,0:T(8,128)} %select_maximum_fusion), calls=%async_computation | async-start | bytes 4325376 | tf_op jit(solution)/shard_map/all_to_all | solution.py:119
  25.6 3.6 %collective-permute-start.1 = (f32[2176,1]{0,1:T(1,128)S(1)}, f32[2176,1]{0,1:T(1,128)S(1)}, u32[]{:S(2)}, u32[]{:S(2)}) collective-permute-start(f32[2176,1]{0,1:T(1,128)S(1)} %copy.38), channel_id=1, source_target_pairs={{1,0},{2,1},{3,2},{4,3},{5,4},{6,5},{7,6},{8,7},{9,8},{10,9},{11,1... | collective-permute-start | bytes 26120 | tf_op jit(solution)/shard_map/ppermute | solution.py:24
  29.6 2.3 %collective-permute-start = (f32[2176,1]{0,1:T(1,128)S(1)}, f32[2176,1]{0,1:T(1,128)S(1)}, u32[]{:S(2)}, u32[]{:S(2)}) collective-permute-start(f32[2176,1]{0,1:T(1,128)S(1)} %copy.36), channel_id=1, source_target_pairs={{0,1},{1,2},{2,3},{3,4},{4,5},{5,6},{6,7},{7,8},{8,9},{9,10},{10,1... | collective-permute-start | bytes 26120 | tf_op jit(solution)/shard_map/ppermute | solution.py:23
  32.0 6.6 %fusion.10 = f32[2176,128]{1,0:T(8,128)S(1)} fusion(bf16[1,2176,2176]{2,1,0:T(8,128)(2,1)} %param.20, bf16[1,2176,128]{2,1,0:T(8,128)(2,1)} %param.17, bf16[1,2176,128]{2,1,0:T(8,128)(2,1)} %param.18, bf16[1,2176,128]{2,1,0:T(8,128)(2,1)S(1)} %copy-done.1), kind=kOutput, calls=%fused_computation.20 | convolution fusion | flops 1213267968 | bytes 12255232 | tf_op jit(solution)/shard_map/dot_general | solution.py:150
  38.7 3.2 %gather_fusion = bf16[1024,128]{1,0:T(8,128)(2,1)S(1)} fusion(bf16[2176,128]{1,0:T(8,128)(2,1)S(1)} %bitcast.1282, s32[1024]{0:T(1024)S(1)} %broadcast_clamp_fusion), kind=kCustom, calls=%fused_computation | custom fusion | bytes 528384 | tf_op jit(solution)/shard_map/gather | solution.py:134
  42.0 1.4 copy.37
  43.4 1.4 copy.39
  44.8 28.8 %all-to-all-done = f32[16,264,128]{2,1,0:T(8,128)} async-done(((f32[16,264,128]{2,1,0:T(8,128)}), f32[16,264,128]{2,1,0:T(8,128)}, u32[]{:S(2)}, u32[]{:S(2)}) %all-to-all-start) | async-done | bytes 2162720 | tf_op jit(solution)/shard_map/all_to_all | solution.py:119
  73.5 3.2 %gather_fusion.5 = f32[8,264,128]{2,1,0:T(8,128)} fusion(f32[16,264,128]{2,1,0:T(8,128)} %all-to-all-done, s32[1024]{0:T(1024)S(1)} %pad_clamp_fusion.1), kind=kCustom, calls=%fused_computation.5 | custom fusion | bytes 2162720 | tf_op jit(solution)/shard_map/jit(_take)/gather | solution.py:120
  76.8 1.5 bitcast_select_fusion
  78.3 1.0 copy-done.12
  80.2 1.1 fusion.37
  81.3 6.8 %scatter_fusion = f32[2176,128]{1,0:T(8,128)S(1)} fusion(f32[2176,128]{1,0:T(8,128)S(1)} %fusion.10, s32[1024]{0:T(1024)S(1)} %fusion.50, f32[1024,128]{1,0:T(8,128)} %bitcast.1296), kind=kCustom, calls=%fused_computation.11 | custom fusion | flops 131072 | bytes 1576960 | tf_op jit(solution)/shard_map/scatter-add | solution.py:148
  89.5 2.3 %shard_map.183 = (f32[128,128]{1,0:T(8,128)}, f32[128,128]{1,0:T(8,128)}) custom-call(f32[128,128]{1,0:T(8,128)} %bitcast.1301, f32[128,128]{1,0:T(8,128)} %multiply_multiply_fusion.1.charge_ref), custom_call_target="tpu_custom_call" | custom-call | tf_op jit(solution)/shard_map/pallas_call | solution.py:53
  91.8 1.0 slice_reduce_fusion.2
  93.4 15.5 %all-to-all-start.1 = ((f32[32,2,128]{2,1,0:T(2,128)}), f32[32,2,128]{2,1,0:T(2,128)S(1)}, u32[]{:S(2)}, u32[]{:S(2)}) async-start(f32[32,2,128]{2,1,0:T(2,128)} %broadcast_in_dim.115), calls=%async_computation.1 | async-start | bytes 65536 | tf_op jit(solution)/shard_map/all_to_all | solution.py:158
  108.9 3.7 %fusion.21 = (f32[2176,128]{1,0:T(8,128)S(1)}, bf16[2176,128]{1,0:T(8,128)(2,1)S(1)}) fusion(f32[2176,1]{1,0:T(8,128)} %copy.39, f32[2176,128]{1,0:T(8,128)} %copy-done.2, f32[2176,1]{1,0:T(8,128)} %copy.37, f32[2176,128]{1,0:T(8,128)S(1)} %scatter_fusion, bf16[1,2176,128]{2,1,0:T(8,128)(2,1)} %param.17, f32[2176]{0:T(1024)S(1)} %reduce.3, f32[2176]{0:T(1024)S(1)} %reduce.2), kind=kLoop, calls=%fused_computation.37 | loop fusion | flops 3620864 | bytes 4491264 | tf_op jit(solution)/shard_map/add | solution.py:153
  112.7 1.1 fusion.26
  113.8 1.0 copy-done.3
  114.9 6.2 %gather_fusion.8 = bf16[2048,128]{1,0:T(8,128)(2,1)S(1)} fusion(bf16[2176,128]{1,0:T(8,128)(2,1)S(1)} %fusion.23, s32[2048]{0:T(1024)S(1)} %fusion.49), kind=kCustom, calls=%fused_computation.8 | custom fusion | bytes 1056768 | tf_op jit(solution)/shard_map/gather | solution.py:135
  121.1 1.1 convert.9
  122.2 4.3 %all-to-all-start.2 = ((f32[16,128,128]{2,1,0:T(8,128)}), f32[16,128,128]{2,1,0:T(8,128)}, u32[]{:S(2)}, u32[]{:S(2)}) async-start(f32[16,128,128]{2,1,0:T(8,128)} %convert.9), calls=%async_computation.2 | async-start | bytes 2097152 | tf_op jit(solution)/shard_map/all_to_all | solution.py:119
  126.5 1.7 fusion.182
  128.3 1.6 copy.40
  129.8 3.6 %collective-permute-start.2 = (f32[2176,1]{0,1:T(1,128)S(1)}, f32[2176,1]{0,1:T(1,128)S(1)}, u32[]{:S(2)}, u32[]{:S(2)}) collective-permute-start(f32[2176,1]{0,1:T(1,128)S(1)} %copy.40), channel_id=1, source_target_pairs={{0,1},{1,2},{2,3},{3,4},{4,5},{5,6},{6,7},{7,8},{8,9},{9,10},{10,1... | collective-permute-start | bytes 26120 | tf_op jit(solution)/shard_map/ppermute | solution.py:23
  133.4 1.6 copy.42
  135.0 2.1 %collective-permute-start.3 = (f32[2176,1]{0,1:T(1,128)S(1)}, f32[2176,1]{0,1:T(1,128)S(1)}, u32[]{:S(2)}, u32[]{:S(2)}) collective-permute-start(f32[2176,1]{0,1:T(1,128)S(1)} %copy.42), channel_id=1, source_target_pairs={{1,0},{2,1},{3,2},{4,3},{5,4},{6,5},{7,6},{8,7},{9,8},{10,9},{11,1... | collective-permute-start | bytes 26120 | tf_op jit(solution)/shard_map/ppermute | solution.py:24
  137.2 3.2 %gather_fusion.7 = bf16[1024,128]{1,0:T(8,128)(2,1)S(1)} fusion(bf16[2176,128]{1,0:T(8,128)(2,1)S(1)} %fusion.23, s32[1024]{0:T(1024)S(1)} %broadcast_clamp_fusion), kind=kCustom, calls=%fused_computation.7 | custom fusion | bytes 528384 | tf_op jit(solution)/shard_map/gather | solution.py:134
  141.2 1.4 copy.41
  142.6 1.4 copy.43
  144.2 2.1 %scatter_custom_fusion.1 = f32[2176,128]{1,0:T(8,128)} fusion(s32[128]{0:T(128)S(1)} %fusion.56, f32[]{:T(128)} %constant.60.clone.1, f32[128,128]{1,0:T(8,128)S(1)} %copy-done.22, f32[128,128]{1,0:T(8,128)S(1)} %copy-done.21, f32[128]{0:T(128)S(1)} %broadcast_select_fusion.64, f32[128]{0:T(128)S(1)} %bitcast.1310), kind=kCustom, calls=%fused_computation.59 | custom fusion | flops 65536 | bytes 1246212 | tf_op jit(solution)/shard_map/scatter-add | solution.py:164
  146.3 7.1 %fusion.7 = f32[2176,128]{1,0:T(8,128)S(1)} fusion(bf16[2176,128]{1,0:T(8,128)(2,1)} %bitcast.1290, bf16[1,2176,2176]{2,1,0:T(8,128)(2,1)} %param.20, f32[2176,128]{1,0:T(8,128)} %scatter_custom_fusion.1, f32[2176,128]{1,0:T(8,128)S(1)} %get-tuple-element.29, bf16[1,2176,128]{2,1,0:T(8,128)(2,1)} %param.18), kind=kOutput, calls=%fused_computation.19 | convolution fusion | flops 1213267968 | bytes 13926400 | tf_op jit(solution)/shard_map/dot_general | solution.py:150
  153.4 2.6 %gather_fusion.9 = f32[8,128,128]{2,1,0:T(8,128)} fusion(f32[16,128,128]{2,1,0:T(8,128)} %all-to-all-done.2, s32[1024]{0:T(1024)S(1)} %pad_clamp_fusion.1), kind=kCustom, calls=%fused_computation.9 | custom fusion | bytes 1048608 | tf_op jit(solution)/shard_map/jit(_take)/gather | solution.py:120
  156.0 3.0 %fusion.40 = f32[8,128,128]{2,1,0:T(8,128)} fusion(f32[8,128,128]{2,1,0:T(8,128)} %bitcast.1287, f32[8,128,128]{2,1,0:T(8,128)} %gather_fusion.9, f32[1,8,128,128]{3,1,2,0:T(8,128)} %copy-done.11, bf16[1,8,128,128]{3,2,1,0:T(8,128)(2,1)} %param.19, f32[8,128]{1,0:T(8,128)S(1)} %slice-done, f32[8,128]{1,0:T(8,128)S(1)} %bitcast.1298, ...), kind=kLoop, calls=%fused_computation.71 | loop fusion | flops 1572864 | bytes 3420168 | tf_op jit(solution)/shard_map/add | solution.py:147
  159.1 6.8 %scatter_fusion.1 = f32[2176,128]{1,0:T(8,128)S(1)} fusion(f32[2176,128]{1,0:T(8,128)S(1)} %fusion.7, s32[1024]{0:T(1024)S(1)} %fusion.50, f32[1024,128]{1,0:T(8,128)} %bitcast.1295), kind=kCustom, calls=%fused_computation.13 | custom fusion | flops 131072 | bytes 1576960 | tf_op jit(solution)/shard_map/scatter-add | solution.py:148
  167.3 2.3 %shard_map.184 = (f32[128,128]{1,0:T(8,128)}, f32[128,128]{1,0:T(8,128)}) custom-call(f32[128,128]{1,0:T(8,128)} %bitcast.1302, f32[128,128]{1,0:T(8,128)} %multiply_multiply_fusion.charge_ref), custom_call_target="tpu_custom_call" | custom-call | tf_op jit(solution)/shard_map/pallas_call | solution.py:53
  169.5 1.0 slice_reduce_fusion
  170.6 1.0 slice_reduce_fusion.1
  172.2 12.3 %all-to-all-start.3 = ((f32[32,2,128]{2,1,0:T(2,128)}), f32[32,2,128]{2,1,0:T(2,128)S(1)}, u32[]{:S(2)}, u32[]{:S(2)}) async-start(f32[32,2,128]{2,1,0:T(2,128)} %broadcast_in_dim.121), calls=%async_computation.3 | async-start | bytes 65536 | tf_op jit(solution)/shard_map/all_to_all | solution.py:158
  184.5 3.6 %fusion.33 = (bf16[1,2176,128]{2,1,0:T(8,128)(2,1)}, bf16[2176,128]{1,0:T(8,128)(2,1)S(1)}) fusion(f32[2176,1]{1,0:T(8,128)} %copy.43, f32[2176,128]{1,0:T(8,128)S(1)} %get-tuple-element.29, f32[2176,1]{1,0:T(8,128)} %copy.41, f32[2176]{0:T(1024)S(1)} %reduce.3, f32[2176,128]{1,0:T(8,128)S(1)} %scatter_fusion.1, f32[2176]{0:T(1024)S(1)} %reduce.2), kind=kLoop, calls=%fused_computation.61 | loop fusion | flops 3620864 | bytes 3377152 | tf_op jit(solution)/shard_map/broadcast_in_dim | solution.py:175
  189.4 1.1 bitcast_subtract_fusion
  191.4 1.1 fusion.34
  192.5 1.8 all-to-all-done.3
  (103 shorter events, 12.8 us)
Async XLA Ops:
  0.6 112.0 %copy-start = (bf16[1,34,64,64]{3,2,1,0:T(8,128)(2,1)S(1)}, bf16[1,34,64,64]{3,2,1,0:T(8,128)(2,1)}, u32[]{:S(2)}) copy-start(bf16[1,34,64,64]{3,2,1,0:T(8,128)(2,1)} %param.21) | copy-start | bytes 835588
  11.1 1.0 copy-start.13
  14.4 9.8 %copy-start.16 = (bf16[1,2176,128]{2,1,0:T(8,128)(2,1)S(1)}, bf16[1,2176,128]{2,1,0:T(8,128)(2,1)}, u32[]{:S(2)}) copy-start(bf16[1,2176,128]{2,1,0:T(8,128)(2,1)} %param.17) | copy-start | bytes 1671172
  14.4 59.2 %all-to-all-start = ((f32[16,264,128]{2,1,0:T(8,128)}), f32[16,264,128]{2,1,0:T(8,128)}, u32[]{:S(2)}, u32[]{:S(2)}) async-start(f32[16,264,128]{2,1,0:T(8,128)} %select_maximum_fusion), calls=%async_computation | async-start | bytes 4325376 | tf_op jit(solution)/shard_map/all_to_all | solution.py:119
  24.2 1.0 copy-start.2
  25.2 6.7 %copy-start.27 = (s32[1,128]{1,0:T(1,128)S(1)}, s32[1,128]{1,0:T(1,128)}, u32[]{:S(2)}) copy-start(s32[1,128]{1,0:T(1,128)} %param.28) | copy-start | bytes 1540
  25.2 6.7 %copy-start.28 = (f32[1,128]{1,0:T(1,128)S(1)}, f32[1,128]{1,0:T(1,128)}, u32[]{:S(2)}) copy-start(f32[1,128]{1,0:T(1,128)} %param.29) | copy-start | bytes 1540
  25.2 6.7 %copy-start.18 = (s32[1,8,128]{2,1,0:T(8,128)S(1)}, s32[1,8,128]{2,1,0:T(8,128)}, u32[]{:S(2)}) copy-start(s32[1,8,128]{2,1,0:T(8,128)} %param.25) | copy-start | bytes 12292
  25.2 6.7 %copy-start.1 = (bf16[1,2176,128]{2,1,0:T(8,128)(2,1)S(1)}, bf16[1,2176,128]{2,1,0:T(8,128)(2,1)}, u32[]{:S(2)}) copy-start(bf16[1,2176,128]{2,1,0:T(8,128)(2,1)} %param.16) | copy-start | bytes 1671172
  25.6 17.8 %collective-permute-start.1 = (f32[2176,1]{0,1:T(1,128)S(1)}, f32[2176,1]{0,1:T(1,128)S(1)}, u32[]{:S(2)}, u32[]{:S(2)}) collective-permute-start(f32[2176,1]{0,1:T(1,128)S(1)} %copy.38), channel_id=1, source_target_pairs={{1,0},{2,1},{3,2},{4,3},{5,4},{6,5},{7,6},{8,7},{9,8},{10,9},{11,1... | collective-permute-start | bytes 26120 | tf_op jit(solution)/shard_map/ppermute | solution.py:24
  29.6 12.4 %collective-permute-start = (f32[2176,1]{0,1:T(1,128)S(1)}, f32[2176,1]{0,1:T(1,128)S(1)}, u32[]{:S(2)}, u32[]{:S(2)}) collective-permute-start(f32[2176,1]{0,1:T(1,128)S(1)} %copy.36), channel_id=1, source_target_pairs={{0,1},{1,2},{2,3},{3,4},{4,5},{5,6},{6,7},{7,8},{8,9},{9,10},{10,1... | collective-permute-start | bytes 26120 | tf_op jit(solution)/shard_map/ppermute | solution.py:23
  32.0 6.6 %copy-start.24 = (f32[1,2176]{1,0:T(1,128)S(1)}, f32[1,2176]{1,0:T(1,128)}, u32[]{:S(2)}) copy-start(f32[1,2176]{1,0:T(1,128)} %param.22) | copy-start | bytes 26116
  32.0 6.7 %copy-start.25 = (f32[1,2176]{1,0:T(1,128)S(1)}, f32[1,2176]{1,0:T(1,128)}, u32[]{:S(2)}) copy-start(f32[1,2176]{1,0:T(1,128)} %param.23) | copy-start | bytes 26116
  41.9 37.4 %copy-start.5 = (f32[1024,128]{1,0:T(8,128)}, f32[1024,128]{1,0:T(8,128)S(1)}, u32[]{:S(2)}) copy-start(f32[1024,128]{1,0:T(8,128)S(1)} %convert_element_type.120) | copy-start | bytes 1572868
  78.3 1.0 copy-start.12
  79.3 0.9 copy-start.14
  79.3 1.0 copy-start.23
  79.3 1.9 copy-start.7
  79.3 1.9 copy-start.11
  93.4 28.8 %all-to-all-start.1 = ((f32[32,2,128]{2,1,0:T(2,128)}), f32[32,2,128]{2,1,0:T(2,128)S(1)}, u32[]{:S(2)}, u32[]{:S(2)}) async-start(f32[32,2,128]{2,1,0:T(2,128)} %broadcast_in_dim.115), calls=%async_computation.1 | async-start | bytes 65536 | tf_op jit(solution)/shard_map/all_to_all | solution.py:158
  113.8 1.0 copy-start.3
  122.2 31.2 %all-to-all-start.2 = ((f32[16,128,128]{2,1,0:T(8,128)}), f32[16,128,128]{2,1,0:T(8,128)}, u32[]{:S(2)}, u32[]{:S(2)}) async-start(f32[16,128,128]{2,1,0:T(8,128)} %convert.9), calls=%async_computation.2 | async-start | bytes 2097152 | tf_op jit(solution)/shard_map/all_to_all | solution.py:119
  129.8 11.4 %collective-permute-start.2 = (f32[2176,1]{0,1:T(1,128)S(1)}, f32[2176,1]{0,1:T(1,128)S(1)}, u32[]{:S(2)}, u32[]{:S(2)}) collective-permute-start(f32[2176,1]{0,1:T(1,128)S(1)} %copy.40), channel_id=1, source_target_pairs={{0,1},{1,2},{2,3},{3,4},{4,5},{5,6},{6,7},{7,8},{8,9},{9,10},{10,1... | collective-permute-start | bytes 26120 | tf_op jit(solution)/shard_map/ppermute | solution.py:23
  135.0 7.7 %collective-permute-start.3 = (f32[2176,1]{0,1:T(1,128)S(1)}, f32[2176,1]{0,1:T(1,128)S(1)}, u32[]{:S(2)}, u32[]{:S(2)}) collective-permute-start(f32[2176,1]{0,1:T(1,128)S(1)} %copy.42), channel_id=1, source_target_pairs={{1,0},{2,1},{3,2},{4,3},{5,4},{6,5},{7,6},{8,7},{9,8},{10,9},{11,1... | collective-permute-start | bytes 26120 | tf_op jit(solution)/shard_map/ppermute | solution.py:24
  141.2 2.9 %copy-start.21 = (f32[128,128]{1,0:T(8,128)S(1)}, f32[128,128]{1,0:T(8,128)}, u32[]{:S(2)}) copy-start(f32[128,128]{1,0:T(8,128)} %get-tuple-element.9) | copy-start | bytes 196612
  141.2 2.9 %copy-start.22 = (f32[128,128]{1,0:T(8,128)S(1)}, f32[128,128]{1,0:T(8,128)}, u32[]{:S(2)}) copy-start(f32[128,128]{1,0:T(8,128)} %get-tuple-element.8) | copy-start | bytes 196612
  141.2 2.9 %copy-start.26 = (f32[1,128]{1,0:T(1,128)S(1)}, f32[1,128]{1,0:T(1,128)}, u32[]{:S(2)}) copy-start(f32[1,128]{1,0:T(1,128)} %param.30) | copy-start | bytes 1540
  146.3 9.7 %slice-start = ((f32[8,33792]{1,0:T(8,128)}), f32[8,128]{1,0:T(8,128)S(1)}, s32[]{:S(2)}) async-start(f32[8,33792]{1,0:T(8,128)} %copy-done.12), calls=%async_computation.4 | async-start | bytes 8192 | tf_op jit(solution)/shard_map/slice | solution.py:124
  146.3 9.7 %copy-start.17 = (f32[1,8,128]{2,1,0:T(8,128)S(1)}, f32[1,8,128]{2,1,0:T(8,128)}, u32[]{:S(2)}) copy-start(f32[1,8,128]{2,1,0:T(8,128)} %param.27) | copy-start | bytes 12292
  172.2 22.0 %all-to-all-start.3 = ((f32[32,2,128]{2,1,0:T(2,128)}), f32[32,2,128]{2,1,0:T(2,128)S(1)}, u32[]{:S(2)}, u32[]{:S(2)}) async-start(f32[32,2,128]{2,1,0:T(2,128)} %broadcast_in_dim.121), calls=%async_computation.3 | async-start | bytes 65536 | tf_op jit(solution)/shard_map/all_to_all | solution.py:158
  188.1 1.2 copy-start.4
  189.4 1.2 copy-start.6
  189.4 1.5 copy-start.8
  189.4 1.8 copy-start.9
  189.4 1.9 copy-start.10
  189.4 2.0 %copy-start.15 = (bf16[1,8,128,128]{3,2,1,0:T(8,128)(2,1)S(1)}, bf16[1,8,128,128]{3,2,1,0:T(8,128)(2,1)}, u32[]{:S(2)}) copy-start(bf16[1,8,128,128]{3,2,1,0:T(8,128)(2,1)} %param.19) | copy-start | bytes 786436
  191.4 3.0 %copy-start.19 = (f32[128,128]{1,0:T(8,128)S(1)}, f32[128,128]{1,0:T(8,128)}, u32[]{:S(2)}) copy-start(f32[128,128]{1,0:T(8,128)} %get-tuple-element.11) | copy-start | bytes 196612
  191.4 3.0 %copy-start.20 = (f32[128,128]{1,0:T(8,128)S(1)}, f32[128,128]{1,0:T(8,128)}, u32[]{:S(2)}) copy-start(f32[128,128]{1,0:T(8,128)} %get-tuple-element.10) | copy-start | bytes 196612

commit v4 on v3

--- a/solution.py
+++ b/solution.py
@@ -110,7 +110,6 @@
     slot_ids = jnp.arange(area_count, dtype=jnp.int32)
     round_ids = jnp.arange(rounds, dtype=jnp.int32)
     round_of = jnp.sum(jnp.where(partners[:, None] == slot_ids[None, :], round_ids[:, None], 0), axis=0)
-    slot_rows = jnp.take(edge_rows, round_of, axis=0)
 
     def exchanged(parts, shapes):
         lanes = 128
@@ -131,8 +130,8 @@
     mismatch = None
     for iteration in range(ITERS):
         rounded = angle_now.astype(jnp.bfloat16)
-        own_edge = rounded[edge_rows].astype(jnp.float32)
-        edge_out = rounded[slot_rows].astype(jnp.float32)
+        own_edge = lax.optimization_barrier(rounded[edge_rows].astype(jnp.float32))
+        edge_out = jnp.take(own_edge, round_of, axis=0)
         if iteration == 0:
             far_edge, price_far, penalty_far = exchanged(
                 (edge_out, jnp.take(price_now, round_of, axis=0),

time: 196 us -> 194 us (0.990)
  local copies, waits for them, and re-layouts: 51.6 us -> 39.2 us
  waiting for transfers between devices: 30.5 us -> 39.4 us
    gather x5 -> x4, local copies, waits for them, and re-layouts: 20.6 us -> 10.4 us  [the longest x2 7.25 us: local(): own_edge = lax.optimization_barrier(rounded[edge_rows].astype(jnp.float32))]
    all_to_all x2, waiting for transfers between devices: 28.8 us -> 33.9 us  [exchanged(): got = lax.all_to_all(sent, 'area', split_axis=0, concat_axis=0, tiled=True)]
    select_n x2 -> x3, other arithmetic: 0.14 us -> 3.86 us  [local(): edge_out = jnp.take(own_edge, round_of, axis=0)]
    broadcast_in_dim x0 -> x1, other arithmetic: none -> 3.2 us  [local(): price_now[None]]
    add x2 -> x1, other arithmetic: 4.08 us -> 1.05 us  [local(): tie_flow = tie_gain * mismatch + 0.5 * (price_now - price_far)]
    unnamed x59 -> x51, local copies, waits for them, and re-layouts: 6.25 us -> 3.92 us
    convert_element_type x4 -> x2, other arithmetic: 2.07 us -> 0.07 us  [local(): own_edge = lax.optimization_barrier(rounded[edge_rows].astype(jnp.float32))]
    all_to_all x2, waiting for transfers between devices: 1.76 us -> 3.75 us  [local(): ends = lax.all_to_all(copies, 'tm', split_axis=0, concat_axis=0, tiled=True)]
  transfers between devices with their start and end apart: 8 -> 8, of which waited for: 2 -> 4; matrix products, arithmetic and copies ran while one was open for 27% -> 24% of each run, Pallas kernels for 0% -> 0%
where the time goes in v4:
time: 194 us; the launch traced here: 193 us
  starting transfers between devices  53.8 us (28%)
  other arithmetic  40 us (21%)
  waiting for transfers between devices  39.4 us (20%)
  local copies, waits for them, and re-layouts  39.2 us (20%)
  matrix products  15.1 us (8%)
  Pallas kernels  4.55 us (2%)
    all_to_all x2, waiting for transfers between devices, exchanged(): got = lax.all_to_all(sent, 'area', split_axis=0, concat_axis=0, tiled=True)  33.9 us
    all_to_all x2, starting transfers between devices, local(): ends = lax.all_to_all(copies, 'tm', split_axis=0, concat_axis=0, tiled=True)  28.2 us
    all_to_all x2, starting transfers between devices, exchanged(): got = lax.all_to_all(sent, 'area', split_axis=0, concat_axis=0, tiled=True)  14.1 us
    dot_general x2, matrix products, local(): jnp.dot(matrix, rounded, preferred_element_type=jnp.float32) + fixed_part  13.7 us
    scatter-add x2, other arithmetic, local(): jnp.zeros((bus_count, hour_count), jnp.float32).at[edge_rows].add(tie_flow)  13.7 us
    gather x2, local copies, waits for them, and re-layouts, local(): own_edge = lax.optimization_barrier(rounded[edge_rows].astype(jnp.float32))  7.25 us
    ppermute x2, starting transfers between devices, padded_2(): before = lax.ppermute(last, axis, up)  5.84 us
    gather x2, local copies, waits for them, and re-layouts, exchanged(): got = jnp.take(got, partners, axis=0).reshape(rounds, -1)  5.8 us
  transfers between devices with their start and end apart: 8, of which 4 were waited for; matrix products, arithmetic and copies ran while one was open for 24% of the time, Pallas kernels for 0%

profile of v4, /device:TPU:1, one launch (start us, length us, event | category | flops | bytes accessed | tf_op | source)
XLA Modules:
  0.0 193.3 jit_solution(17603514514907705450)
XLA Ops:
  0.7 1.0 fusion.45
  2.5 4.0 %gather_fusion = bf16[1024,128]{1,0:T(8,128)(2,1)S(1)} fusion(bf16[2176,128]{1,0:T(8,128)(2,1)} %bitcast.1256, s32[1024]{0:T(1024)S(1)} %broadcast_clamp_fusion), kind=kCustom, calls=%fused_computation.3 | custom fusion | bytes 528384 | tf_op jit(solution)/shard_map/gather | solution.py:133
  7.3 1.6 gather_fusion.7
  9.5 1.5 broadcast_select_fusion.2
  11.0 1.5 select_maximum_fusion
  12.5 9.7 %all-to-all-start = ((f32[16,264,128]{2,1,0:T(8,128)}), f32[16,264,128]{2,1,0:T(8,128)}, u32[]{:S(2)}, u32[]{:S(2)}) async-start(f32[16,264,128]{2,1,0:T(8,128)} %select_maximum_fusion), calls=%async_computation | async-start | bytes 4325376 | tf_op jit(solution)/shard_map/all_to_all | solution.py:118
  22.3 1.3 fusion.177
  23.7 1.6 copy.38
  25.3 3.6 %collective-permute-start.1 = (f32[2176,1]{0,1:T(1,128)S(1)}, f32[2176,1]{0,1:T(1,128)S(1)}, u32[]{:S(2)}, u32[]{:S(2)}) collective-permute-start(f32[2176,1]{0,1:T(1,128)S(1)} %copy.38), channel_id=1, source_target_pairs={{1,0},{2,1},{3,2},{4,3},{5,4},{6,5},{7,6},{8,7},{9,8},{10,9},{11,1... | collective-permute-start | bytes 26120 | tf_op jit(solution)/shard_map/ppermute | solution.py:24
  29.3 2.3 %collective-permute-start = (f32[2176,1]{0,1:T(1,128)S(1)}, f32[2176,1]{0,1:T(1,128)S(1)}, u32[]{:S(2)}, u32[]{:S(2)}) collective-permute-start(f32[2176,1]{0,1:T(1,128)S(1)} %copy.36), channel_id=1, source_target_pairs={{0,1},{1,2},{2,3},{3,4},{4,5},{5,6},{6,7},{7,8},{8,9},{9,10},{10,1... | collective-permute-start | bytes 26120 | tf_op jit(solution)/shard_map/ppermute | solution.py:23
  31.7 6.6 %fusion.10 = f32[2176,128]{1,0:T(8,128)S(1)} fusion(bf16[1,2176,2176]{2,1,0:T(8,128)(2,1)} %param.22, bf16[1,2176,128]{2,1,0:T(8,128)(2,1)} %param.19, bf16[1,2176,128]{2,1,0:T(8,128)(2,1)} %param.20, bf16[1,2176,128]{2,1,0:T(8,128)(2,1)S(1)} %copy-done.1), kind=kOutput, calls=%fused_computation.19 | convolution fusion | flops 1213267968 | bytes 12255232 | tf_op jit(solution)/shard_map/dot_general | solution.py:149
  38.4 1.4 copy.37
  39.8 1.4 copy.39
  41.2 30.4 %all-to-all-done = f32[16,264,128]{2,1,0:T(8,128)} async-done(((f32[16,264,128]{2,1,0:T(8,128)}), f32[16,264,128]{2,1,0:T(8,128)}, u32[]{:S(2)}, u32[]{:S(2)}) %all-to-all-start) | async-done | bytes 2162720 | tf_op jit(solution)/shard_map/all_to_all | solution.py:118
  71.6 3.2 %gather_fusion.2 = f32[8,264,128]{2,1,0:T(8,128)} fusion(f32[16,264,128]{2,1,0:T(8,128)} %all-to-all-done, s32[1024]{0:T(1024)S(1)} %pad_clamp_fusion.1), kind=kCustom, calls=%fused_computation.5 | custom fusion | bytes 2162720 | tf_op jit(solution)/shard_map/jit(_take)/gather | solution.py:119
  74.9 1.5 bitcast_select_fusion
  78.3 1.1 fusion.35
  79.4 6.8 %scatter_fusion = f32[2176,128]{1,0:T(8,128)S(1)} fusion(f32[2176,128]{1,0:T(8,128)S(1)} %fusion.10, s32[1024]{0:T(1024)S(1)} %fusion.44, f32[1024,128]{1,0:T(8,128)} %bitcast.1263), kind=kCustom, calls=%fused_computation.10 | custom fusion | flops 131072 | bytes 1576960 | tf_op jit(solution)/shard_map/scatter-add | solution.py:147
  87.6 2.3 %shard_map.183 = (f32[128,128]{1,0:T(8,128)}, f32[128,128]{1,0:T(8,128)}) custom-call(f32[128,128]{1,0:T(8,128)} %bitcast.1268, f32[128,128]{1,0:T(8,128)} %multiply_multiply_fusion.1.charge_ref), custom_call_target="tpu_custom_call" | custom-call | tf_op jit(solution)/shard_map/pallas_call | solution.py:53
  89.8 1.0 slice_reduce_fusion.2
  91.5 15.5 %all-to-all-start.1 = ((f32[32,2,128]{2,1,0:T(2,128)}), f32[32,2,128]{2,1,0:T(2,128)S(1)}, u32[]{:S(2)}, u32[]{:S(2)}) async-start(f32[32,2,128]{2,1,0:T(2,128)} %broadcast_in_dim.96), calls=%async_computation.1 | async-start | bytes 65536 | tf_op jit(solution)/shard_map/all_to_all | solution.py:157
  107.0 3.8 %fusion.21 = (f32[2176,128]{1,0:T(8,128)S(1)}, bf16[2176,128]{1,0:T(8,128)(2,1)S(1)}) fusion(f32[2176,1]{1,0:T(8,128)} %copy.39, f32[2176,128]{1,0:T(8,128)} %copy-done.2, f32[2176,1]{1,0:T(8,128)} %copy.37, f32[2176,128]{1,0:T(8,128)S(1)} %scatter_fusion, bf16[1,2176,128]{2,1,0:T(8,128)(2,1)} %param.19, f32[2176]{0:T(1024)S(1)} %reduce.3, f32[2176]{0:T(1024)S(1)} %reduce.2), kind=kLoop, calls=%fused_computation.36 | loop fusion | flops 3620864 | bytes 4491264 | tf_op jit(solution)/shard_map/add | solution.py:152
  110.8 1.1 fusion.26
  111.9 1.0 copy-done.4
  113.0 3.2 %gather_fusion.4 = bf16[1024,128]{1,0:T(8,128)(2,1)S(1)} fusion(bf16[2176,128]{1,0:T(8,128)(2,1)S(1)} %fusion.23, s32[1024]{0:T(1024)S(1)} %broadcast_clamp_fusion), kind=kCustom, calls=%fused_computation.7 | custom fusion | bytes 528384 | tf_op jit(solution)/shard_map/gather | solution.py:133
  116.3 1.6 gather_fusion.9
  117.9 2.4 %broadcast_select_fusion = f32[16,128,128]{2,1,0:T(8,128)} fusion(f32[16,128,128]{2,1,0:T(8,128)} %gather_fusion.9, pred[16]{0:T(512)(128)(4,1)S(1)} %compare_and_fusion), kind=kLoop, calls=%fused_computation.69 | loop fusion | flops 262144 | bytes 2097168 | tf_op jit(solution)/shard_map/jit(_take)/select_n | solution.py:134
  120.2 4.3 %all-to-all-start.2 = ((f32[16,128,128]{2,1,0:T(8,128)}), f32[16,128,128]{2,1,0:T(8,128)}, u32[]{:S(2)}, u32[]{:S(2)}) async-start(f32[16,128,128]{2,1,0:T(8,128)} %broadcast_select_fusion), calls=%async_computation.2 | async-start | bytes 2097152 | tf_op jit(solution)/shard_map/all_to_all | solution.py:118
  124.6 1.3 fusion.176
  125.9 1.6 copy.40
  127.5 3.6 %collective-permute-start.2 = (f32[2176,1]{0,1:T(1,128)S(1)}, f32[2176,1]{0,1:T(1,128)S(1)}, u32[]{:S(2)}, u32[]{:S(2)}) collective-permute-start(f32[2176,1]{0,1:T(1,128)S(1)} %copy.40), channel_id=1, source_target_pairs={{0,1},{1,2},{2,3},{3,4},{4,5},{5,6},{6,7},{7,8},{8,9},{9,10},{10,1... | collective-permute-start | bytes 26120 | tf_op jit(solution)/shard_map/ppermute | solution.py:23
  131.4 2.1 %collective-permute-start.3 = (f32[2176,1]{0,1:T(1,128)S(1)}, f32[2176,1]{0,1:T(1,128)S(1)}, u32[]{:S(2)}, u32[]{:S(2)}) collective-permute-start(f32[2176,1]{0,1:T(1,128)S(1)} %copy.42), channel_id=1, source_target_pairs={{1,0},{2,1},{3,2},{4,3},{5,4},{6,5},{7,6},{8,7},{9,8},{10,9},{11,1... | collective-permute-start | bytes 26120 | tf_op jit(solution)/shard_map/ppermute | solution.py:24
  133.7 1.4 copy.41
  135.1 1.8 collective-permute-done.3
  136.8 1.4 copy.43
  138.3 2.1 %scatter_custom_fusion.1 = f32[2176,128]{1,0:T(8,128)} fusion(s32[128]{0:T(128)S(1)} %fusion.50, f32[]{:T(128)} %constant.40.clone.1, f32[128,128]{1,0:T(8,128)S(1)} %copy-done.17, f32[128,128]{1,0:T(8,128)S(1)} %copy-done.16, f32[128]{0:T(128)S(1)} %broadcast_select_fusion.66, f32[128]{0:T(128)S(1)} %bitcast.1277), kind=kCustom, calls=%fused_computation.56 | custom fusion | flops 65536 | bytes 1246212 | tf_op jit(solution)/shard_map/scatter-add | solution.py:163
  140.5 7.1 %fusion.7 = f32[2176,128]{1,0:T(8,128)S(1)} fusion(bf16[2176,128]{1,0:T(8,128)(2,1)} %bitcast.1259, bf16[1,2176,2176]{2,1,0:T(8,128)(2,1)} %param.22, f32[2176,128]{1,0:T(8,128)} %scatter_custom_fusion.1, f32[2176,128]{1,0:T(8,128)S(1)} %get-tuple-element.32, bf16[1,2176,128]{2,1,0:T(8,128)(2,1)} %param.20), kind=kOutput, calls=%fused_computation.18 | convolution fusion | flops 1213267968 | bytes 13926400 | tf_op jit(solution)/shard_map/dot_general | solution.py:149
  147.6 3.5 %all-to-all-done.2 = f32[16,128,128]{2,1,0:T(8,128)} async-done(((f32[16,128,128]{2,1,0:T(8,128)}), f32[16,128,128]{2,1,0:T(8,128)}, u32[]{:S(2)}, u32[]{:S(2)}) %all-to-all-start.2) | async-done | bytes 1048608 | tf_op jit(solution)/shard_map/all_to_all | solution.py:118
  151.1 2.6 %gather_fusion.5 = f32[8,128,128]{2,1,0:T(8,128)} fusion(f32[16,128,128]{2,1,0:T(8,128)} %all-to-all-done.2, s32[1024]{0:T(1024)S(1)} %pad_clamp_fusion.1), kind=kCustom, calls=%fused_computation.8 | custom fusion | bytes 1048608 | tf_op jit(solution)/shard_map/jit(_take)/gather | solution.py:119
  153.7 3.2 %add_bitcast_fusion = (f32[1,8,128,128]{3,2,1,0:T(8,128)}, f32[8,128,128]{2,1,0:T(8,128)}) fusion(bf16[1,8,128,128]{3,2,1,0:T(8,128)(2,1)} %param.21, f32[8,128]{1,0:T(8,128)S(1)} %bitcast.1265, f32[8,128,128]{2,1,0:T(8,128)} %copy-done.6, f32[8,128,128]{2,1,0:T(8,128)} %gather_fusion.5, pred[8]{0:T(512)(128)(4,1)S(1)} %compare_and_fusion.1, ...), kind=kLoop, calls=%fused_computation.72 | loop fusion | flops 1835008 | bytes 3944456 | tf_op jit(solution)/shard_map/broadcast_in_dim | solution.py:175
  156.9 6.8 %scatter_fusion.1 = f32[2176,128]{1,0:T(8,128)S(1)} fusion(f32[2176,128]{1,0:T(8,128)S(1)} %fusion.7, s32[1024]{0:T(1024)S(1)} %fusion.44, f32[1024,128]{1,0:T(8,128)} %bitcast.1262), kind=kCustom, calls=%fused_computation.12 | custom fusion | flops 131072 | bytes 1576960 | tf_op jit(solution)/shard_map/scatter-add | solution.py:147
  165.1 2.3 %shard_map.184 = (f32[128,128]{1,0:T(8,128)}, f32[128,128]{1,0:T(8,128)}) custom-call(f32[128,128]{1,0:T(8,128)} %bitcast.1269, f32[128,128]{1,0:T(8,128)} %multiply_multiply_fusion.charge_ref), custom_call_target="tpu_custom_call" | custom-call | tf_op jit(solution)/shard_map/pallas_call | solution.py:53
  167.3 1.0 slice_reduce_fusion
  168.4 1.0 slice_reduce_fusion.1
  170.0 12.7 %all-to-all-start.3 = ((f32[32,2,128]{2,1,0:T(2,128)}), f32[32,2,128]{2,1,0:T(2,128)S(1)}, u32[]{:S(2)}, u32[]{:S(2)}) async-start(f32[32,2,128]{2,1,0:T(2,128)} %broadcast_in_dim.101), calls=%async_computation.3 | async-start | bytes 65536 | tf_op jit(solution)/shard_map/all_to_all | solution.py:157
  182.7 3.6 %fusion.33 = (bf16[1,2176,128]{2,1,0:T(8,128)(2,1)}, bf16[2176,128]{1,0:T(8,128)(2,1)S(1)}) fusion(f32[2176,1]{1,0:T(8,128)} %copy.43, f32[2176,128]{1,0:T(8,128)S(1)} %get-tuple-element.32, f32[2176,1]{1,0:T(8,128)} %copy.41, f32[2176]{0:T(1024)S(1)} %reduce.3, f32[2176,128]{1,0:T(8,128)S(1)} %scatter_fusion.1, f32[2176]{0:T(1024)S(1)} %reduce.2), kind=kLoop, calls=%fused_computation.58 | loop fusion | flops 3620864 | bytes 3377152 | tf_op jit(solution)/shard_map/broadcast_in_dim | solution.py:174
  187.6 1.1 bitcast_subtract_fusion
  188.7 3.7 %all-to-all-done.3 = f32[32,2,128]{2,1,0:T(2,128)S(1)} async-done(((f32[32,2,128]{2,1,0:T(2,128)}), f32[32,2,128]{2,1,0:T(2,128)S(1)}, u32[]{:S(2)}, u32[]{:S(2)}) %all-to-all-start.3) | async-done | bytes 32800 | tf_op jit(solution)/shard_map/all_to_all | solution.py:157
  (93 shorter events, 11.3 us)
Async XLA Ops:
  0.6 110.1 %copy-start = (bf16[1,34,64,64]{3,2,1,0:T(8,128)(2,1)S(1)}, bf16[1,34,64,64]{3,2,1,0:T(8,128)(2,1)}, u32[]{:S(2)}) copy-start(bf16[1,34,64,64]{3,2,1,0:T(8,128)(2,1)} %param.23) | copy-start | bytes 835588
  2.5 4.1 %copy-start.10 = (bf16[1,8,128,128]{3,2,1,0:T(8,128)(2,1)S(1)}, bf16[1,8,128,128]{3,2,1,0:T(8,128)(2,1)}, u32[]{:S(2)}) copy-start(bf16[1,8,128,128]{3,2,1,0:T(8,128)(2,1)} %param.21) | copy-start | bytes 786436
  6.6 70.9 %copy-start.3 = (f32[8,128,128]{2,1,0:T(8,128)}, f32[8,128,128]{2,1,0:T(8,128)S(1)}, u32[]{:S(2)}) copy-start(f32[8,128,128]{2,1,0:T(8,128)S(1)} %convert.7) | copy-start | bytes 1572868
  7.2 1.6 copy-start.13
  12.5 9.8 %copy-start.12 = (bf16[1,2176,128]{2,1,0:T(8,128)(2,1)S(1)}, bf16[1,2176,128]{2,1,0:T(8,128)(2,1)}, u32[]{:S(2)}) copy-start(bf16[1,2176,128]{2,1,0:T(8,128)(2,1)} %param.19) | copy-start | bytes 1671172
  12.5 59.2 %all-to-all-start = ((f32[16,264,128]{2,1,0:T(8,128)}), f32[16,264,128]{2,1,0:T(8,128)}, u32[]{:S(2)}, u32[]{:S(2)}) async-start(f32[16,264,128]{2,1,0:T(8,128)} %select_maximum_fusion), calls=%async_computation | async-start | bytes 4325376 | tf_op jit(solution)/shard_map/all_to_all | solution.py:118
  22.3 1.4 copy-start.2
  23.7 8.0 %copy-start.23 = (s32[1,128]{1,0:T(1,128)S(1)}, s32[1,128]{1,0:T(1,128)}, u32[]{:S(2)}) copy-start(s32[1,128]{1,0:T(1,128)} %param.30) | copy-start | bytes 1540
  23.7 8.0 %copy-start.24 = (f32[1,128]{1,0:T(1,128)S(1)}, f32[1,128]{1,0:T(1,128)}, u32[]{:S(2)}) copy-start(f32[1,128]{1,0:T(1,128)} %param.31) | copy-start | bytes 1540
  23.7 8.0 %copy-start.19 = (s32[1,8,128]{2,1,0:T(8,128)S(1)}, s32[1,8,128]{2,1,0:T(8,128)}, u32[]{:S(2)}) copy-start(s32[1,8,128]{2,1,0:T(8,128)} %param.27) | copy-start | bytes 12292
  23.7 8.0 %copy-start.1 = (bf16[1,2176,128]{2,1,0:T(8,128)(2,1)S(1)}, bf16[1,2176,128]{2,1,0:T(8,128)(2,1)}, u32[]{:S(2)}) copy-start(bf16[1,2176,128]{2,1,0:T(8,128)(2,1)} %param.18) | copy-start | bytes 1671172
  25.3 14.5 %collective-permute-start.1 = (f32[2176,1]{0,1:T(1,128)S(1)}, f32[2176,1]{0,1:T(1,128)S(1)}, u32[]{:S(2)}, u32[]{:S(2)}) collective-permute-start(f32[2176,1]{0,1:T(1,128)S(1)} %copy.38), channel_id=1, source_target_pairs={{1,0},{2,1},{3,2},{4,3},{5,4},{6,5},{7,6},{8,7},{9,8},{10,9},{11,1... | collective-permute-start | bytes 26120 | tf_op jit(solution)/shard_map/ppermute | solution.py:24
  29.3 9.1 %collective-permute-start = (f32[2176,1]{0,1:T(1,128)S(1)}, f32[2176,1]{0,1:T(1,128)S(1)}, u32[]{:S(2)}, u32[]{:S(2)}) collective-permute-start(f32[2176,1]{0,1:T(1,128)S(1)} %copy.36), channel_id=1, source_target_pairs={{0,1},{1,2},{2,3},{3,4},{4,5},{5,6},{6,7},{7,8},{8,9},{9,10},{10,1... | collective-permute-start | bytes 26120 | tf_op jit(solution)/shard_map/ppermute | solution.py:23
  31.7 6.6 %copy-start.20 = (f32[1,2176]{1,0:T(1,128)S(1)}, f32[1,2176]{1,0:T(1,128)}, u32[]{:S(2)}) copy-start(f32[1,2176]{1,0:T(1,128)} %param.24) | copy-start | bytes 26116
  31.7 6.7 %copy-start.21 = (f32[1,2176]{1,0:T(1,128)S(1)}, f32[1,2176]{1,0:T(1,128)}, u32[]{:S(2)}) copy-start(f32[1,2176]{1,0:T(1,128)} %param.25) | copy-start | bytes 26116
  76.4 1.0 copy-start.9
  77.3 0.9 copy-start.11
  77.3 1.0 copy-start.18
  77.4 1.9 %copy-start.7 = (f32[1,8,128,128]{3,1,2,0:T(8,128)}, f32[1,8,128,128]{3,1,2,0:T(8,128)S(1)}, u32[]{:S(2)}) copy-start(f32[1,8,128,128]{3,1,2,0:T(8,128)S(1)} %get-tuple-element.36) | copy-start | bytes 1572868
  77.4 1.9 copy-start.8
  91.5 28.7 %all-to-all-start.1 = ((f32[32,2,128]{2,1,0:T(2,128)}), f32[32,2,128]{2,1,0:T(2,128)S(1)}, u32[]{:S(2)}, u32[]{:S(2)}) async-start(f32[32,2,128]{2,1,0:T(2,128)} %broadcast_in_dim.96), calls=%async_computation.1 | async-start | bytes 65536 | tf_op jit(solution)/shard_map/all_to_all | solution.py:157
  111.9 1.0 copy-start.4
  116.3 4.0 %copy-start.6 = (f32[8,128,128]{2,1,0:T(8,128)}, f32[8,128,128]{2,1,0:T(8,128)S(1)}, u32[]{:S(2)}) copy-start(f32[8,128,128]{2,1,0:T(8,128)S(1)} %convert.8) | copy-start | bytes 1572868
  120.2 30.8 %all-to-all-start.2 = ((f32[16,128,128]{2,1,0:T(8,128)}), f32[16,128,128]{2,1,0:T(8,128)}, u32[]{:S(2)}, u32[]{:S(2)}) async-start(f32[16,128,128]{2,1,0:T(8,128)} %broadcast_select_fusion), calls=%async_computation.2 | async-start | bytes 2097152 | tf_op jit(solution)/shard_map/all_to_all | solution.py:118
  127.5 6.1 %collective-permute-start.2 = (f32[2176,1]{0,1:T(1,128)S(1)}, f32[2176,1]{0,1:T(1,128)S(1)}, u32[]{:S(2)}, u32[]{:S(2)}) collective-permute-start(f32[2176,1]{0,1:T(1,128)S(1)} %copy.40), channel_id=1, source_target_pairs={{0,1},{1,2},{2,3},{3,4},{4,5},{5,6},{6,7},{7,8},{8,9},{9,10},{10,1... | collective-permute-start | bytes 26120 | tf_op jit(solution)/shard_map/ppermute | solution.py:23
  131.4 5.4 %collective-permute-start.3 = (f32[2176,1]{0,1:T(1,128)S(1)}, f32[2176,1]{0,1:T(1,128)S(1)}, u32[]{:S(2)}, u32[]{:S(2)}) collective-permute-start(f32[2176,1]{0,1:T(1,128)S(1)} %copy.42), channel_id=1, source_target_pairs={{1,0},{2,1},{3,2},{4,3},{5,4},{6,5},{7,6},{8,7},{9,8},{10,9},{11,1... | collective-permute-start | bytes 26120 | tf_op jit(solution)/shard_map/ppermute | solution.py:24
  133.6 4.7 %copy-start.16 = (f32[128,128]{1,0:T(8,128)S(1)}, f32[128,128]{1,0:T(8,128)}, u32[]{:S(2)}) copy-start(f32[128,128]{1,0:T(8,128)} %get-tuple-element.10) | copy-start | bytes 196612
  133.6 4.7 %copy-start.17 = (f32[128,128]{1,0:T(8,128)S(1)}, f32[128,128]{1,0:T(8,128)}, u32[]{:S(2)}) copy-start(f32[128,128]{1,0:T(8,128)} %get-tuple-element.9) | copy-start | bytes 196612
  133.6 4.7 %copy-start.22 = (f32[1,128]{1,0:T(1,128)S(1)}, f32[1,128]{1,0:T(1,128)}, u32[]{:S(2)}) copy-start(f32[1,128]{1,0:T(1,128)} %param.32) | copy-start | bytes 1540
  140.5 13.2 %slice-start = ((f32[8,33792]{1,0:T(8,128)}), f32[8,128]{1,0:T(8,128)S(1)}, s32[]{:S(2)}) async-start(f32[8,33792]{1,0:T(8,128)} %copy-done.9), calls=%async_computation.4 | async-start | bytes 8192 | tf_op jit(solution)/shard_map/slice | solution.py:123
  170.0 22.4 %all-to-all-start.3 = ((f32[32,2,128]{2,1,0:T(2,128)}), f32[32,2,128]{2,1,0:T(2,128)S(1)}, u32[]{:S(2)}, u32[]{:S(2)}) async-start(f32[32,2,128]{2,1,0:T(2,128)} %broadcast_in_dim.101), calls=%async_computation.3 | async-start | bytes 65536 | tf_op jit(solution)/shard_map/all_to_all | solution.py:157
  186.3 1.2 copy-start.5
  187.5 5.0 %copy-start.14 = (f32[128,128]{1,0:T(8,128)S(1)}, f32[128,128]{1,0:T(8,128)}, u32[]{:S(2)}) copy-start(f32[128,128]{1,0:T(8,128)} %get-tuple-element.12) | copy-start | bytes 196612
  187.6 5.0 %copy-start.15 = (f32[128,128]{1,0:T(8,128)S(1)}, f32[128,128]{1,0:T(8,128)}, u32[]{:S(2)}) copy-start(f32[128,128]{1,0:T(8,128)} %get-tuple-element.11) | copy-start | bytes 196612

commit v5 on v4

--- a/solution.py
+++ b/solution.py
@@ -51,6 +51,31 @@
 def window_scan(kept, charge):
     shape = jax.ShapeDtypeStruct(kept.shape, jnp.float32)
     return pl.pallas_call(scan_kernel, out_shape=(shape, shape))(kept, charge)
+
+
+def spread_kernel(rows_ref, flow_ref, out_ref):
+    block = out_ref.shape[0]
+    first = pl.program_id(0) * block
+    bus = first + lax.broadcasted_iota(jnp.int32, (block, rows_ref.shape[1]), 0)
+    pick = (bus == rows_ref[...]).astype(jnp.float32)
+    out_ref[...] = jnp.dot(
+        pick, flow_ref[...], precision=lax.Precision.HIGHEST, preferred_element_type=jnp.float32
+    )
+
+
+def spread_rows(rows, flow, bus_count):
+    block = bus_count // 8
+    lines, hours = flow.shape
+    return pl.pallas_call(
+        spread_kernel,
+        grid=(bus_count // block,),
+        in_specs=[
+            pl.BlockSpec((1, lines), lambda i: (0, 0)),
+            pl.BlockSpec((lines, hours), lambda i: (0, 0)),
+        ],
+        out_specs=pl.BlockSpec((block, hours), lambda i: (i, 0)),
+        out_shape=jax.ShapeDtypeStruct((bus_count, hours), jnp.float32),
+    )(rows.reshape(1, lines), flow)
 
 
 def carried_state(kept_last, state_last, position):
@@ -144,7 +169,7 @@
             price_far = price_far - penalty_far * mismatch
         mismatch = own_edge - far_edge
         tie_flow = tie_gain * mismatch + 0.5 * (price_now - price_far)
-        spread = jnp.zeros((bus_count, hour_count), jnp.float32).at[edge_rows].add(tie_flow)
+        spread = spread_rows(edge_rows, tie_flow.reshape(rounds * lines, hour_count), bus_count)
         fixed_part = demand_local - dispatch - injection + spread
         balance = jnp.dot(matrix, rounded, preferred_element_type=jnp.float32) + fixed_part
         padded = padded_2(dispatch, (("tm", 1),), 1)

time: 194 us -> 214 us (1.10)
  Pallas kernels: 4.55 us -> 26 us
  other arithmetic: 40 us -> 21.9 us
  waiting for transfers between devices: 39.4 us -> 50.8 us
  matrix products: 15.1 us -> 17.9 us
    pallas_call x0 -> x2, Pallas kernels: none -> 21.5 us  [spread_rows(): pl.pallas_call(spread_kernel, grid=(bus_count // block,), in_specs=[pl.Bl...]
    scatter-add x2 -> x0, other arithmetic: 13.7 us -> none  [local(): jnp.zeros((bus_count, hour_count), jnp.float32).at[edge_rows].add(tie_flow)]
    all_to_all x2, waiting for transfers between devices: 33.9 us -> 44.3 us  [exchanged(): got = lax.all_to_all(sent, 'area', split_axis=0, concat_axis=0, tiled=True)]
    add x1 -> x0, other arithmetic: 3.75 us -> none  [local(): dispatch + dispatch_step * (balance - slope * dispatch) + ramp_local * bend]
    dot_general x2, matrix products: 13.7 us -> 16.5 us  [local(): jnp.dot(matrix, rounded, preferred_element_type=jnp.float32) + fixed_part]
  transfers between devices with their start and end apart: 8 -> 8, of which waited for: 4 -> 6; matrix products, arithmetic and copies ran while one was open for 24% -> 14% of each run, Pallas kernels for 0% -> 0%
where the time goes in v5:
time: 214 us; the launch traced here: 213 us
  starting transfers between devices  53.8 us (25%)
  waiting for transfers between devices  50.8 us (24%)
  local copies, waits for them, and re-layouts  41.2 us (19%)
  Pallas kernels  26 us (12%)
  other arithmetic  21.9 us (10%)
  matrix products  17.9 us (8%)
    all_to_all x2, waiting for transfers between devices, exchanged(): got = lax.all_to_all(sent, 'area', split_axis=0, concat_axis=0, tiled=True)  44.3 us
    all_to_all x2, starting transfers between devices, local(): ends = lax.all_to_all(copies, 'tm', split_axis=0, concat_axis=0, tiled=True)  28.5 us
    pallas_call x2, Pallas kernels, spread_rows(): pl.pallas_call(spread_kernel, grid=(bus_count // block,), in_specs=[pl.Bl...  21.5 us
    dot_general x2, matrix products, local(): jnp.dot(matrix, rounded, preferred_element_type=jnp.float32) + fixed_part  16.5 us
    all_to_all x2, starting transfers between devices, exchanged(): got = lax.all_to_all(sent, 'area', split_axis=0, concat_axis=0, tiled=True)  14.1 us
    gather x2, local copies, waits for them, and re-layouts, local(): own_edge = lax.optimization_barrier(rounded[edge_rows].astype(jnp.float32))  7.25 us
    ppermute x2, starting transfers between devices, padded_2(): before = lax.ppermute(last, axis, up)  5.61 us
    ppermute x2, starting transfers between devices, padded_2(): after = lax.ppermute(leading, axis, down)  5.57 us
  transfers between devices with their start and end apart: 8, of which 6 were waited for; matrix products, arithmetic and copies ran while one was open for 14% of the time, Pallas kernels for 0%

profile of v5, /device:TPU:1, one launch (start us, length us, event | category | flops | bytes accessed | tf_op | source)
XLA Modules:
  0.0 212.8 jit_solution(2333112672398079245)
XLA Ops:
  2.5 4.0 %gather_fusion = bf16[1024,128]{1,0:T(8,128)(2,1)S(1)} fusion(bf16[2176,128]{1,0:T(8,128)(2,1)} %bitcast.1259, s32[1024]{0:T(1024)S(1)} %fusion.47), kind=kCustom, calls=%fused_computation.3 | custom fusion | bytes 528384 | tf_op jit(solution)/shard_map/gather | solution.py:158
  7.3 1.6 gather_fusion.7
  9.5 1.5 broadcast_select_fusion.2
  11.0 1.5 select_maximum_fusion
  12.5 9.7 %all-to-all-start = ((f32[16,264,128]{2,1,0:T(8,128)}), f32[16,264,128]{2,1,0:T(8,128)}, u32[]{:S(2)}, u32[]{:S(2)}) async-start(f32[16,264,128]{2,1,0:T(8,128)} %select_maximum_fusion), calls=%async_computation | async-start | bytes 4325376 | tf_op jit(solution)/shard_map/all_to_all | solution.py:143
  22.3 1.3 fusion.180
  23.7 1.6 copy.42
  25.3 3.6 %collective-permute-start.1 = (f32[2176,1]{0,1:T(1,128)S(1)}, f32[2176,1]{0,1:T(1,128)S(1)}, u32[]{:S(2)}, u32[]{:S(2)}) collective-permute-start(f32[2176,1]{0,1:T(1,128)S(1)} %copy.42), channel_id=1, source_target_pairs={{1,0},{2,1},{3,2},{4,3},{5,4},{6,5},{7,6},{8,7},{9,8},{10,9},{11,1... | collective-permute-start | bytes 26120 | tf_op jit(solution)/shard_map/ppermute | solution.py:24
  29.3 2.3 %collective-permute-start = (f32[2176,1]{0,1:T(1,128)S(1)}, f32[2176,1]{0,1:T(1,128)S(1)}, u32[]{:S(2)}, u32[]{:S(2)}) collective-permute-start(f32[2176,1]{0,1:T(1,128)S(1)} %copy.40), channel_id=1, source_target_pairs={{0,1},{1,2},{2,3},{3,4},{4,5},{5,6},{6,7},{7,8},{8,9},{9,10},{10,1... | collective-permute-start | bytes 26120 | tf_op jit(solution)/shard_map/ppermute | solution.py:23
  32.4 1.4 copy.41
  33.8 1.4 copy.43
  35.2 36.5 %all-to-all-done = f32[16,264,128]{2,1,0:T(8,128)} async-done(((f32[16,264,128]{2,1,0:T(8,128)}), f32[16,264,128]{2,1,0:T(8,128)}, u32[]{:S(2)}, u32[]{:S(2)}) %all-to-all-start) | async-done | bytes 2162720 | tf_op jit(solution)/shard_map/all_to_all | solution.py:143
  71.7 2.2 %gather_fusion.2 = f32[8,264,128]{2,1,0:T(8,128)S(1)} fusion(f32[16,264,128]{2,1,0:T(8,128)} %all-to-all-done, s32[1024]{0:T(1024)S(1)} %pad_clamp_fusion.1), kind=kCustom, calls=%fused_computation.5 | custom fusion | bytes 2162720 | tf_op jit(solution)/shard_map/jit(_take)/gather | solution.py:144
  74.2 1.0 copy-done.8
  76.2 1.1 fusion.37
  77.2 10.8 %shard_map.183 = f32[2176,128]{1,0:T(8,128)} custom-call(s32[1,1024]{1,0:T(1,128)} %bitcast.1273, f32[1024,128]{1,0:T(8,128)} %bitcast.1266), custom_call_target="tpu_custom_call" | custom-call | tf_op jit(solution)/shard_map/pallas_call | solution.py:69
  88.0 9.1 %fusion.23 = (f32[2176,128]{1,0:T(8,128)S(1)}, bf16[2176,128]{1,0:T(8,128)(2,1)}, f32[2176,128]{1,0:T(8,128)}) fusion(f32[2176,1]{1,0:T(8,128)} %copy.43, f32[2176,128]{1,0:T(8,128)S(1)} %bitcast_convert_fusion, f32[2176,1]{1,0:T(8,128)} %copy.41, bf16[1,2176,128]{2,1,0:T(8,128)(2,1)} %param.19, f32[2176]{0:T(1024)S(1)} %reduce.3, f32[2176]{0:T(1024)S(1)} %reduce.2, ...), kind=kOutput, calls=%fused_computation.36 | convolution fusion | flops 1216888832 | bytes 16189440 | tf_op jit(solution)/shard_map/dot_general | solution.py:174
  97.1 2.0 gather_fusion.3
  99.8 2.3 %shard_map.184 = (f32[128,128]{1,0:T(8,128)}, f32[128,128]{1,0:T(8,128)}) custom-call(f32[128,128]{1,0:T(8,128)} %bitcast.1271, f32[128,128]{1,0:T(8,128)} %multiply_multiply_fusion.1.charge_ref), custom_call_target="tpu_custom_call" | custom-call | tf_op jit(solution)/shard_map/pallas_call | solution.py:53
  102.0 1.0 slice_reduce_fusion.2
  103.7 15.5 %all-to-all-start.1 = ((f32[32,2,128]{2,1,0:T(2,128)}), f32[32,2,128]{2,1,0:T(2,128)S(1)}, u32[]{:S(2)}, u32[]{:S(2)}) async-start(f32[32,2,128]{2,1,0:T(2,128)} %broadcast_in_dim.98), calls=%async_computation.1 | async-start | bytes 65536 | tf_op jit(solution)/shard_map/all_to_all | solution.py:182
  119.2 1.1 fusion.28
  120.3 1.0 copy-done.4
  121.5 3.2 %gather_fusion.4 = bf16[1024,128]{1,0:T(8,128)(2,1)S(1)} fusion(bf16[2176,128]{1,0:T(8,128)(2,1)S(1)} %fusion.25, s32[1024]{0:T(1024)S(1)} %fusion.47), kind=kCustom, calls=%fused_computation.7 | custom fusion | bytes 528384 | tf_op jit(solution)/shard_map/gather | solution.py:158
  124.7 1.6 gather_fusion.9
  126.3 2.4 %broadcast_select_fusion = f32[16,128,128]{2,1,0:T(8,128)} fusion(f32[16,128,128]{2,1,0:T(8,128)} %gather_fusion.9, pred[16]{0:T(512)(128)(4,1)S(1)} %compare_and_fusion), kind=kLoop, calls=%fused_computation.69 | loop fusion | flops 262144 | bytes 2097168 | tf_op jit(solution)/shard_map/jit(_take)/select_n | solution.py:159
  128.9 4.3 %all-to-all-start.2 = ((f32[16,128,128]{2,1,0:T(8,128)}), f32[16,128,128]{2,1,0:T(8,128)}, u32[]{:S(2)}, u32[]{:S(2)}) async-start(f32[16,128,128]{2,1,0:T(8,128)} %broadcast_select_fusion), calls=%async_computation.2 | async-start | bytes 2097152 | tf_op jit(solution)/shard_map/all_to_all | solution.py:143
  133.3 1.7 fusion.179
  135.0 1.6 copy.44
  136.6 3.3 %collective-permute-start.2 = (f32[2176,1]{0,1:T(1,128)S(1)}, f32[2176,1]{0,1:T(1,128)S(1)}, u32[]{:S(2)}, u32[]{:S(2)}) collective-permute-start(f32[2176,1]{0,1:T(1,128)S(1)} %copy.44), channel_id=1, source_target_pairs={{0,1},{1,2},{2,3},{3,4},{4,5},{5,6},{6,7},{7,8},{8,9},{9,10},{10,1... | collective-permute-start | bytes 26120 | tf_op jit(solution)/shard_map/ppermute | solution.py:23
  139.9 1.6 copy.46
  141.5 1.9 collective-permute-start.3
  143.5 1.4 copy.45
  144.9 2.0 collective-permute-done.3
  146.9 1.4 copy.47
  148.9 2.5 %scatter_custom_fusion = f32[2176,128]{1,0:T(8,128)} fusion(s32[128]{0:T(128)} %copy-done.28, f32[]{:T(128)} %constant.40.clone.1, f32[128,128]{1,0:T(8,128)} %get-tuple-element.9, f32[128,128]{1,0:T(8,128)} %get-tuple-element.10, f32[128]{0:T(128)} %broadcast_select_fusion.66, f32[128]{0:T(128)} %bitcast.1282), kind=kCustom, calls=%fused_computation.56 | custom fusion | flops 65536 | bytes 1246720 | tf_op jit(solution)/shard_map/scatter-add | solution.py:188
  151.4 7.8 %all-to-all-done.2 = f32[16,128,128]{2,1,0:T(8,128)} async-done(((f32[16,128,128]{2,1,0:T(8,128)}), f32[16,128,128]{2,1,0:T(8,128)}, u32[]{:S(2)}, u32[]{:S(2)}) %all-to-all-start.2) | async-done | bytes 1048608 | tf_op jit(solution)/shard_map/all_to_all | solution.py:143
  159.2 2.6 %gather_fusion.5 = f32[8,128,128]{2,1,0:T(8,128)} fusion(f32[16,128,128]{2,1,0:T(8,128)} %all-to-all-done.2, s32[1024]{0:T(1024)S(1)} %pad_clamp_fusion.1), kind=kCustom, calls=%fused_computation.8 | custom fusion | bytes 1048608 | tf_op jit(solution)/shard_map/jit(_take)/gather | solution.py:144
  161.8 2.8 %add_bitcast_fusion = (f32[1,8,128,128]{3,2,1,0:T(8,128)}, f32[8,128,128]{2,1,0:T(8,128)}) fusion(bf16[1,8,128,128]{3,2,1,0:T(8,128)(2,1)S(1)} %copy-done.13, f32[8,128]{1,0:T(8,128)S(1)} %bitcast.1268, f32[8,128,128]{2,1,0:T(8,128)S(1)} %convert.8, f32[8,128,128]{2,1,0:T(8,128)} %gather_fusion.5, pred[8]{0:T(512)(128)(4,1)} %copy-done.27, ...), kind=kLoop, calls=%fused_computation.72 | loop fusion | flops 1835008 | bytes 3944456 | tf_op jit(solution)/shard_map/broadcast_in_dim | solution.py:200
  164.7 10.7 %shard_map.185 = f32[2176,128]{1,0:T(8,128)} custom-call(s32[1,1024]{1,0:T(1,128)} %bitcast.1274, f32[1024,128]{1,0:T(8,128)} %bitcast.1265), custom_call_target="tpu_custom_call" | custom-call | tf_op jit(solution)/shard_map/pallas_call | solution.py:69
  175.4 7.4 %fusion.7 = f32[2176,128]{1,0:T(8,128)S(1)} fusion(bf16[2176,128]{1,0:T(8,128)(2,1)} %bitcast.1263, bf16[1,2176,2176]{2,1,0:T(8,128)(2,1)} %param.22, f32[2176,128]{1,0:T(8,128)} %shard_map.185, f32[2176,128]{1,0:T(8,128)} %scatter_custom_fusion, f32[2176,128]{1,0:T(8,128)S(1)} %get-tuple-element.32, bf16[1,2176,128]{2,1,0:T(8,128)(2,1)} %param.20), kind=kOutput, calls=%fused_computation.16 | convolution fusion | flops 1213546496 | bytes 15040512 | tf_op jit(solution)/shard_map/dot_general | solution.py:174
  184.3 2.3 %shard_map.186 = (f32[128,128]{1,0:T(8,128)}, f32[128,128]{1,0:T(8,128)}) custom-call(f32[128,128]{1,0:T(8,128)} %bitcast.1272, f32[128,128]{1,0:T(8,128)} %multiply_multiply_fusion.charge_ref), custom_call_target="tpu_custom_call" | custom-call | tf_op jit(solution)/shard_map/pallas_call | solution.py:53
  186.5 1.0 slice_reduce_fusion
  187.5 1.0 slice_reduce_fusion.1
  189.2 13.0 %all-to-all-start.3 = ((f32[32,2,128]{2,1,0:T(2,128)}), f32[32,2,128]{2,1,0:T(2,128)S(1)}, u32[]{:S(2)}, u32[]{:S(2)}) async-start(f32[32,2,128]{2,1,0:T(2,128)} %broadcast_in_dim.103), calls=%async_computation.3 | async-start | bytes 65536 | tf_op jit(solution)/shard_map/all_to_all | solution.py:182
  202.3 3.6 %fusion.35 = (bf16[1,2176,128]{2,1,0:T(8,128)(2,1)}, bf16[2176,128]{1,0:T(8,128)(2,1)S(1)}) fusion(f32[2176,1]{1,0:T(8,128)} %copy.47, f32[2176,128]{1,0:T(8,128)S(1)} %get-tuple-element.32, f32[2176,1]{1,0:T(8,128)} %copy.45, f32[2176]{0:T(1024)S(1)} %copy-done.20, f32[2176,128]{1,0:T(8,128)S(1)} %fusion.7, f32[2176]{0:T(1024)S(1)} %copy-done.18), kind=kLoop, calls=%fused_computation.58 | loop fusion | flops 3620864 | bytes 3377152 | tf_op jit(solution)/shard_map/broadcast_in_dim | solution.py:199
  207.1 1.1 bitcast_subtract_fusion
  208.2 3.7 %all-to-all-done.3 = f32[32,2,128]{2,1,0:T(2,128)S(1)} async-done(((f32[32,2,128]{2,1,0:T(2,128)}), f32[32,2,128]{2,1,0:T(2,128)S(1)}, u32[]{:S(2)}, u32[]{:S(2)}) %all-to-all-start.3) | async-done | bytes 32800 | tf_op jit(solution)/shard_map/all_to_all | solution.py:182
  (103 shorter events, 12.0 us)
Async XLA Ops:
  0.6 118.6 %copy-start = (bf16[1,34,64,64]{3,2,1,0:T(8,128)(2,1)S(1)}, bf16[1,34,64,64]{3,2,1,0:T(8,128)(2,1)}, u32[]{:S(2)}) copy-start(bf16[1,34,64,64]{3,2,1,0:T(8,128)(2,1)} %param.23) | copy-start | bytes 835588
  2.5 4.1 %copy-start.11 = (bf16[1,8,128,128]{3,2,1,0:T(8,128)(2,1)S(1)}, bf16[1,8,128,128]{3,2,1,0:T(8,128)(2,1)}, u32[]{:S(2)}) copy-start(bf16[1,8,128,128]{3,2,1,0:T(8,128)(2,1)} %param.21) | copy-start | bytes 786436
  6.6 68.7 %copy-start.2 = (f32[8,128,128]{2,1,0:T(8,128)}, f32[8,128,128]{2,1,0:T(8,128)S(1)}, u32[]{:S(2)}) copy-start(f32[8,128,128]{2,1,0:T(8,128)S(1)} %convert.7) | copy-start | bytes 1572868
  7.2 1.6 copy-start.14
  12.5 9.8 %copy-start.10 = (bf16[1,2176,128]{2,1,0:T(8,128)(2,1)S(1)}, bf16[1,2176,128]{2,1,0:T(8,128)(2,1)}, u32[]{:S(2)}) copy-start(bf16[1,2176,128]{2,1,0:T(8,128)(2,1)} %param.19) | copy-start | bytes 1671172
  12.5 59.2 %all-to-all-start = ((f32[16,264,128]{2,1,0:T(8,128)}), f32[16,264,128]{2,1,0:T(8,128)}, u32[]{:S(2)}, u32[]{:S(2)}) async-start(f32[16,264,128]{2,1,0:T(8,128)} %select_maximum_fusion), calls=%async_computation | async-start | bytes 4325376 | tf_op jit(solution)/shard_map/all_to_all | solution.py:143
  23.7 8.0 %copy-start.29 = (s32[1,128]{1,0:T(1,128)S(1)}, s32[1,128]{1,0:T(1,128)}, u32[]{:S(2)}) copy-start(s32[1,128]{1,0:T(1,128)} %param.30) | copy-start | bytes 1540
  23.7 8.0 %copy-start.30 = (f32[1,128]{1,0:T(1,128)S(1)}, f32[1,128]{1,0:T(1,128)}, u32[]{:S(2)}) copy-start(f32[1,128]{1,0:T(1,128)} %param.31) | copy-start | bytes 1540
  23.7 8.0 %copy-start.22 = (f32[1,2176]{1,0:T(1,128)S(1)}, f32[1,2176]{1,0:T(1,128)}, u32[]{:S(2)}) copy-start(f32[1,2176]{1,0:T(1,128)} %param.24) | copy-start | bytes 26116
  23.7 8.1 %copy-start.23 = (f32[1,2176]{1,0:T(1,128)S(1)}, f32[1,2176]{1,0:T(1,128)}, u32[]{:S(2)}) copy-start(f32[1,2176]{1,0:T(1,128)} %param.25) | copy-start | bytes 26116
  25.3 8.5 %collective-permute-start.1 = (f32[2176,1]{0,1:T(1,128)S(1)}, f32[2176,1]{0,1:T(1,128)S(1)}, u32[]{:S(2)}, u32[]{:S(2)}) collective-permute-start(f32[2176,1]{0,1:T(1,128)S(1)} %copy.42), channel_id=1, source_target_pairs={{1,0},{2,1},{3,2},{4,3},{5,4},{6,5},{7,6},{8,7},{9,8},{10,9},{11,1... | collective-permute-start | bytes 26120 | tf_op jit(solution)/shard_map/ppermute | solution.py:24
  29.3 3.1 %collective-permute-start = (f32[2176,1]{0,1:T(1,128)S(1)}, f32[2176,1]{0,1:T(1,128)S(1)}, u32[]{:S(2)}, u32[]{:S(2)}) collective-permute-start(f32[2176,1]{0,1:T(1,128)S(1)} %copy.40), channel_id=1, source_target_pairs={{0,1},{1,2},{2,3},{3,4},{4,5},{5,6},{6,7},{7,8},{8,9},{9,10},{10,1... | collective-permute-start | bytes 26120 | tf_op jit(solution)/shard_map/ppermute | solution.py:23
  31.6 42.3 %copy-start.27 = (pred[8]{0:T(512)(128)(4,1)}, pred[8]{0:T(512)(128)(4,1)S(1)}, u32[]{:S(2)}) copy-start(pred[8]{0:T(512)(128)(4,1)S(1)} %compare_and_fusion.1) | copy-start | bytes 28
  31.7 3.6 %copy-start.28 = (s32[128]{0:T(128)}, s32[128]{0:T(128)S(1)}, u32[]{:S(2)}) copy-start(s32[128]{0:T(128)S(1)} %fusion.53) | copy-start | bytes 1540
  31.7 67.4 %copy-start.25 = (f32[128]{0:T(128)}, f32[128]{0:T(128)S(1)}, u32[]{:S(2)}) copy-start(f32[128]{0:T(128)S(1)} %negate_bitcast_fusion) | copy-start | bytes 1540
  31.7 65.4 %copy-start.24 = (s32[1024]{0:T(1024)}, s32[1024]{0:T(1024)S(1)}, u32[]{:S(2)}) copy-start(s32[1024]{0:T(1024)S(1)} %pad_clamp_fusion) | copy-start | bytes 12292
  31.8 56.3 %copy-start.17 = (f32[2176]{0:T(1024)}, f32[2176]{0:T(1024)S(1)}, u32[]{:S(2)}) copy-start(f32[2176]{0:T(1024)S(1)} %reduce.2) | copy-start | bytes 26116
  31.8 56.2 %copy-start.19 = (f32[2176]{0:T(1024)}, f32[2176]{0:T(1024)S(1)}, u32[]{:S(2)}) copy-start(f32[2176]{0:T(1024)S(1)} %reduce.3) | copy-start | bytes 26116
  74.2 1.0 copy-start.8
  75.2 0.9 copy-start.12
  75.2 1.0 copy-start.21
  75.3 0.8 copy-start.6
  75.3 1.9 copy-start.7
  77.2 10.8 %copy-start.1 = (bf16[1,2176,128]{2,1,0:T(8,128)(2,1)S(1)}, bf16[1,2176,128]{2,1,0:T(8,128)(2,1)}, u32[]{:S(2)}) copy-start(bf16[1,2176,128]{2,1,0:T(8,128)(2,1)} %param.18) | copy-start | bytes 1671172
  97.1 22.1 %copy-start.9 = (bf16[2176,128]{1,0:T(8,128)(2,1)S(1)}, bf16[2176,128]{1,0:T(8,128)(2,1)}, u32[]{:S(2)}) copy-start(bf16[2176,128]{1,0:T(8,128)(2,1)} %get-tuple-element.33) | copy-start | bytes 1671172
  103.7 25.2 %all-to-all-start.1 = ((f32[32,2,128]{2,1,0:T(2,128)}), f32[32,2,128]{2,1,0:T(2,128)S(1)}, u32[]{:S(2)}, u32[]{:S(2)}) async-start(f32[32,2,128]{2,1,0:T(2,128)} %broadcast_in_dim.98), calls=%async_computation.1 | async-start | bytes 65536 | tf_op jit(solution)/shard_map/all_to_all | solution.py:182
  120.3 1.0 copy-start.4
  128.9 30.3 %all-to-all-start.2 = ((f32[16,128,128]{2,1,0:T(8,128)}), f32[16,128,128]{2,1,0:T(8,128)}, u32[]{:S(2)}, u32[]{:S(2)}) async-start(f32[16,128,128]{2,1,0:T(8,128)} %broadcast_select_fusion), calls=%async_computation.2 | async-start | bytes 2097152 | tf_op jit(solution)/shard_map/all_to_all | solution.py:143
  136.6 6.9 %collective-permute-start.2 = (f32[2176,1]{0,1:T(1,128)S(1)}, f32[2176,1]{0,1:T(1,128)S(1)}, u32[]{:S(2)}, u32[]{:S(2)}) collective-permute-start(f32[2176,1]{0,1:T(1,128)S(1)} %copy.44), channel_id=1, source_target_pairs={{0,1},{1,2},{2,3},{3,4},{4,5},{5,6},{6,7},{7,8},{8,9},{9,10},{10,1... | collective-permute-start | bytes 26120 | tf_op jit(solution)/shard_map/ppermute | solution.py:23
  141.5 5.4 %collective-permute-start.3 = (f32[2176,1]{0,1:T(1,128)S(1)}, f32[2176,1]{0,1:T(1,128)S(1)}, u32[]{:S(2)}, u32[]{:S(2)}) collective-permute-start(f32[2176,1]{0,1:T(1,128)S(1)} %copy.46), channel_id=1, source_target_pairs={{1,0},{2,1},{3,2},{4,3},{5,4},{6,5},{7,6},{8,7},{9,8},{10,9},{11,1... | collective-permute-start | bytes 26120 | tf_op jit(solution)/shard_map/ppermute | solution.py:24
  148.9 12.9 %copy-start.3 = (f32[8,128,128]{2,1,0:T(8,128)S(1)}, f32[8,128,128]{2,1,0:T(8,128)}, u32[]{:S(2)}) copy-start(f32[8,128,128]{2,1,0:T(8,128)} %copy-done.2) | copy-start | bytes 1572868
  148.9 12.9 %slice-start = ((f32[8,33792]{1,0:T(8,128)}), f32[8,128]{1,0:T(8,128)S(1)}, s32[]{:S(2)}) async-start(f32[8,33792]{1,0:T(8,128)} %copy-done.8), calls=%async_computation.4 | async-start | bytes 8192 | tf_op jit(solution)/shard_map/slice | solution.py:148
  148.9 12.9 %copy-start.13 = (bf16[1,8,128,128]{3,2,1,0:T(8,128)(2,1)S(1)}, bf16[1,8,128,128]{3,2,1,0:T(8,128)(2,1)}, u32[]{:S(2)}) copy-start(bf16[1,8,128,128]{3,2,1,0:T(8,128)(2,1)} %param.21) | copy-start | bytes 786436
  175.4 8.2 %copy-start.26 = (f32[128]{0:T(128)S(1)}, f32[128]{0:T(128)}, u32[]{:S(2)}) copy-start(f32[128]{0:T(128)} %copy-done.25) | copy-start | bytes 1540
  175.4 26.9 %copy-start.18 = (f32[2176]{0:T(1024)S(1)}, f32[2176]{0:T(1024)}, u32[]{:S(2)}) copy-start(f32[2176]{0:T(1024)} %copy-done.17) | copy-start | bytes 26116
  175.4 26.9 %copy-start.20 = (f32[2176]{0:T(1024)S(1)}, f32[2176]{0:T(1024)}, u32[]{:S(2)}) copy-start(f32[2176]{0:T(1024)} %copy-done.19) | copy-start | bytes 26116
  189.2 22.7 %all-to-all-start.3 = ((f32[32,2,128]{2,1,0:T(2,128)}), f32[32,2,128]{2,1,0:T(2,128)S(1)}, u32[]{:S(2)}, u32[]{:S(2)}) async-start(f32[32,2,128]{2,1,0:T(2,128)} %broadcast_in_dim.103), calls=%async_computation.3 | async-start | bytes 65536 | tf_op jit(solution)/shard_map/all_to_all | solution.py:182
  205.8 1.2 copy-start.5
  207.1 5.0 %copy-start.15 = (f32[128,128]{1,0:T(8,128)S(1)}, f32[128,128]{1,0:T(8,128)}, u32[]{:S(2)}) copy-start(f32[128,128]{1,0:T(8,128)} %get-tuple-element.12) | copy-start | bytes 196612
  207.1 5.0 %copy-start.16 = (f32[128,128]{1,0:T(8,128)S(1)}, f32[128,128]{1,0:T(8,128)}, u32[]{:S(2)}) copy-start(f32[128,128]{1,0:T(8,128)} %get-tuple-element.11) | copy-start | bytes 196612

commit v6 on v4

--- a/solution.py
+++ b/solution.py
@@ -124,13 +124,28 @@
             at += width
         return found
 
+    bus_ids = lax.broadcasted_iota(jnp.int32, (1, bus_count), 1)
+    edge_pick = (edge_rows.reshape(-1, 1) == bus_ids).astype(jnp.bfloat16)
+
+    def spread_rows(pick, flow):
+        high = lax.reduce_precision(flow, exponent_bits=8, mantissa_bits=7)
+        middle = lax.reduce_precision(flow - high, exponent_bits=8, mantissa_bits=7)
+        low = flow - high - middle
+        parts = jnp.concatenate([high, middle, low], axis=1).astype(jnp.bfloat16)
+        summed = lax.dot_general(
+            pick, parts, (((0,), (0,)), ((), ())), preferred_element_type=jnp.float32
+        )
+        width = flow.shape[1]
+        return summed[:, :width] + summed[:, width : 2 * width] + summed[:, 2 * width :]
+
     kept_total = None
     price_far = None
     penalty_far = None
     mismatch = None
     for iteration in range(ITERS):
         rounded = angle_now.astype(jnp.bfloat16)
-        own_edge = lax.optimization_barrier(rounded[edge_rows].astype(jnp.float32))
+        own_edge = jnp.dot(edge_pick, rounded, preferred_element_type=jnp.float32)
+        own_edge = lax.optimization_barrier(own_edge.reshape(rounds, lines, hour_count))
         edge_out = jnp.take(own_edge, round_of, axis=0)
         if iteration == 0:
             far_edge, price_far, penalty_far = exchanged(
@@ -144,7 +159,7 @@
             price_far = price_far - penalty_far * mismatch
         mismatch = own_edge - far_edge
         tie_flow = tie_gain * mismatch + 0.5 * (price_now - price_far)
-        spread = jnp.zeros((bus_count, hour_count), jnp.float32).at[edge_rows].add(tie_flow)
+        spread = spread_rows(edge_pick, tie_flow.reshape(rounds * lines, hour_count))
         fixed_part = demand_local - dispatch - injection + spread
         balance = jnp.dot(matrix, rounded, preferred_element_type=jnp.float32) + fixed_part
         padded = padded_2(dispatch, (("tm", 1),), 1)

time: 194 us -> 197 us (1.015)
  other arithmetic: 40 us -> 22.5 us
  waiting for transfers between devices: 39.4 us -> 53.2 us
  matrix products: 15.1 us -> 23.7 us
  starting transfers between devices: 53.8 us -> 51.8 us
    all_to_all x2, waiting for transfers between devices: 33.9 us -> 49.3 us  [exchanged(): got = lax.all_to_all(sent, 'area', split_axis=0, concat_axis=0, tiled=True)]
    scatter-add x2 -> x0, other arithmetic: 13.7 us -> none  [local(): jnp.zeros((bus_count, hour_count), jnp.float32).at[edge_rows].add(tie_flow)]
    dot_general x0 -> x4, matrix products: none -> 10.9 us  [the longest x2 6.53 us: spread_rows(): lax.dot_general(pick, parts, (((0,), (0,)), ((), ())), preferred_element_...]
    gather x2 -> x0, local copies, waits for them, and re-layouts: 7.25 us -> none  [local(): own_edge = lax.optimization_barrier(rounded[edge_rows].astype(jnp.float32))]
    unnamed x51 -> x96, local copies, waits for them, and re-layouts: 3.92 us -> 11.2 us
    ppermute x4 -> x0, local copies, waits for them, and re-layouts: 5.6 us -> none  [the longest x2 2.82 us: padded_2(): before = lax.ppermute(last, axis, up)]
    add x1 -> x0, other arithmetic: 3.75 us -> none  [local(): dispatch + dispatch_step * (balance - slope * dispatch) + ramp_local * bend]
    dot_general x2, matrix products: 13.7 us -> 10 us  [local(): jnp.dot(matrix, rounded, preferred_element_type=jnp.float32) + fixed_part]
  transfers between devices with their start and end apart: 8 -> 8, of which waited for: 4 -> 4; matrix products, arithmetic and copies ran while one was open for 24% -> 27% of each run, Pallas kernels for 0% -> 1%
where the time goes in v6:
time: 197 us; the launch traced here: 196 us
  waiting for transfers between devices  53.2 us (27%)
  starting transfers between devices  51.8 us (26%)
  local copies, waits for them, and re-layouts  38.8 us (20%)
  matrix products  23.7 us (12%)
  other arithmetic  22.5 us (11%)
  Pallas kernels  4.57 us (2%)
    all_to_all x2, waiting for transfers between devices, exchanged(): got = lax.all_to_all(sent, 'area', split_axis=0, concat_axis=0, tiled=True)  49.3 us
    all_to_all x2, starting transfers between devices, local(): ends = lax.all_to_all(copies, 'tm', split_axis=0, concat_axis=0, tiled=True)  27.1 us
    all_to_all x2, starting transfers between devices, exchanged(): got = lax.all_to_all(sent, 'area', split_axis=0, concat_axis=0, tiled=True)  13.9 us
    unnamed x96, local copies, waits for them, and re-layouts  11.2 us
    dot_general x2, matrix products, local(): jnp.dot(matrix, rounded, preferred_element_type=jnp.float32) + fixed_part  10 us
    dot_general x2, matrix products, spread_rows(): lax.dot_general(pick, parts, (((0,), (0,)), ((), ())), preferred_element_...  6.53 us
    ppermute x2, starting transfers between devices, padded_2(): before = lax.ppermute(last, axis, up)  6.4 us
    pallas_call x2, Pallas kernels, window_scan(): return pl.pallas_call(scan_kernel, out_shape=(shape, shape))(kept, charge)  4.57 us
  transfers between devices with their start and end apart: 8, of which 4 were waited for; matrix products, arithmetic and copies ran while one was open for 27% of the time, Pallas kernels for 1%

profile of v6, /device:TPU:1, one launch (start us, length us, event | category | flops | bytes accessed | tf_op | source)
XLA Modules:
  0.0 196.0 jit_solution(551600541807532418)
XLA Ops:
  1.8 2.7 %fusion.9 = f32[8,128,128]{2,1,0:T(8,128)S(1)} fusion(s32[8,128]{1,0:T(8,128)} %bitcast.1286, bf16[1,2176,128]{2,1,0:T(8,128)(2,1)} %param.18), kind=kOutput, calls=%fused_computation.19 | convolution fusion | flops 572653568 | bytes 1085440 | tf_op jit(solution)/shard_map/dot_general | solution.py:147
  5.2 1.6 gather_fusion.5
  7.5 1.5 broadcast_select_fusion.2
  9.0 1.5 select_maximum_fusion
  10.5 9.6 %all-to-all-start = ((f32[16,264,128]{2,1,0:T(8,128)}), f32[16,264,128]{2,1,0:T(8,128)S(1)}, u32[]{:S(2)}, u32[]{:S(2)}) async-start(f32[16,264,128]{2,1,0:T(8,128)} %select_maximum_fusion), calls=%async_computation | async-start | bytes 4325376 | tf_op jit(solution)/shard_map/all_to_all | solution.py:118
  20.1 2.1 %copy.42 = bf16[1,2176,128]{1,2,0:T(8,128)(2,1)} copy(bf16[1,2176,128]{2,1,0:T(8,128)(2,1)} %param.19) | data formatting | bytes 1114112 | tf_op args[1]
  22.2 1.2 bitcast_convert_fusion
  24.9 3.9 %collective-permute-start = (f32[2176,1]{0,1:T(1,128)}, f32[2176,1]{0,1:T(1,128)}, u32[]{:S(2)}, u32[]{:S(2)}) collective-permute-start(f32[2176,1]{0,1:T(1,128)} %get-tuple-element.46), channel_id=1, source_target_pairs={{0,1},{1,2},{2,3},{3,4},{4,5},{5,6},{6,7},{7,8},{8,9},{9,10},{10,1... | collective-permute-start | bytes 26120 | tf_op jit(solution)/shard_map/ppermute | solution.py:23
  28.9 1.9 collective-permute-start.1
  30.9 2.1 %copy.41 = bf16[1,2176,128]{1,2,0:T(8,128)(2,1)} copy(bf16[1,2176,128]{2,1,0:T(8,128)(2,1)} %param.20) | data formatting | bytes 1114112 | tf_op args[2]
  34.9 34.9 %all-to-all-done = f32[16,264,128]{2,1,0:T(8,128)S(1)} async-done(((f32[16,264,128]{2,1,0:T(8,128)}), f32[16,264,128]{2,1,0:T(8,128)S(1)}, u32[]{:S(2)}, u32[]{:S(2)}) %all-to-all-start) | async-done | bytes 2162720 | tf_op jit(solution)/shard_map/all_to_all | solution.py:118
  69.8 1.6 gather_fusion.1
  71.5 1.5 bitcast_select_fusion
  74.6 4.1 %fusion.5 = f32[2176,384]{0,1:T(8,128)} fusion(s32[1024]{0:T(1024)S(1)} %bitcast.1287, bf16[1024,128]{1,0:T(8,128)(2,1)S(1)} %get-tuple-element.54, bf16[1024,128]{1,0:T(8,128)(2,1)S(1)} %get-tuple-element.55, bf16[1024,128]{1,0:T(8,128)(2,1)S(1)} %get-tuple-element.53), kind=kOutput, calls=%fused_computation.16 | convolution fusion | flops 1715863552 | bytes 4132864 | tf_op jit(solution)/shard_map/dot_general | solution.py:135
  79.9 7.0 %fusion.34 = (f32[2176,128]{0,1:T(8,128)}, bf16[2176,128]{0,1:T(8,128)(2,1)}, f32[2176,128]{0,1:T(8,128)}) fusion(f32[2176,1]{0,1:T(1,128)} %collective-permute-done.1, f32[2176,128]{0,1:T(8,128)S(1)} %copy-done.16, f32[2176,1]{0,1:T(1,128)} %collective-permute-done, bf16[1,2176,128]{1,2,0:T(8,128)(2,1)S(1)} %copy-done.12, f32[2176]{0:T(1024)S(1)} %reduce.3, ...), kind=kOutput, calls=%fused_computation.47 | convolution fusion | flops 1217445888 | bytes 18417664 | tf_op jit(solution)/shard_map/dot_general | solution.py:164
  86.9 2.1 %copy.43 = bf16[2176,128]{1,0:T(8,128)(2,1)} copy(bf16[2176,128]{0,1:T(8,128)(2,1)} %get-tuple-element.45) | data formatting | bytes 1114112 | tf_op jit(solution)/shard_map/convert_element_type | solution.py:180
  89.0 1.6 copy.44
  90.6 1.2 gather_fusion.2
  91.9 1.6 multiply_multiply_fusion.1.charge_ref
  93.4 2.3 %shard_map.183 = (f32[128,128]{1,0:T(8,128)}, f32[128,128]{1,0:T(8,128)}) custom-call(f32[128,128]{1,0:T(8,128)} %bitcast.1276, f32[128,128]{1,0:T(8,128)} %multiply_multiply_fusion.1.charge_ref), custom_call_target="tpu_custom_call" | custom-call | tf_op jit(solution)/shard_map/pallas_call | solution.py:53
  95.7 1.0 slice_reduce_fusion.2
  97.4 15.1 %all-to-all-start.1 = ((f32[32,2,128]{2,1,0:T(2,128)}), f32[32,2,128]{2,1,0:T(2,128)S(1)}, u32[]{:S(2)}, u32[]{:S(2)}) async-start(f32[32,2,128]{2,1,0:T(2,128)} %broadcast_in_dim.96), calls=%async_computation.1 | async-start | bytes 65536 | tf_op jit(solution)/shard_map/all_to_all | solution.py:172
  112.5 2.5 %fusion.38 = (bf16[34,64,128]{2,1,0:T(8,128)(2,1)S(1)}, f32[34,128,64]{1,2,0:T(8,128)}) fusion(bf16[34,64,128]{2,1,0:T(8,128)(2,1)} %bitcast.1271, bf16[1,34,64,64]{3,2,1,0:T(8,128)(2,1)S(1)} %copy-done, bf16[34,64,128]{2,1,0:T(8,128)(2,1)} %bitcast.1272), kind=kOutput, calls=%fused_computation.60 | convolution fusion | flops 36487168 | bytes 3063808 | tf_op jit(solution)/shard_map/tij,tjh->tih/dot_general | solution.py:181
  115.0 1.6 fusion.7
  116.7 1.7 gather_fusion.7
  118.4 2.4 %broadcast_select_fusion = f32[16,128,128]{2,1,0:T(8,128)} fusion(f32[16,128,128]{2,1,0:T(8,128)} %gather_fusion.7, pred[16]{0:T(512)(128)(4,1)S(1)} %copy-done.31), kind=kLoop, calls=%fused_computation.102 | loop fusion | flops 262144 | bytes 2097168 | tf_op jit(solution)/shard_map/jit(_take)/select_n | solution.py:149
  120.8 1.4 all-to-all-done.1
  122.2 4.4 %all-to-all-start.2 = ((f32[16,128,128]{2,1,0:T(8,128)}), f32[16,128,128]{2,1,0:T(8,128)}, u32[]{:S(2)}, u32[]{:S(2)}) async-start(f32[16,128,128]{2,1,0:T(8,128)} %broadcast_select_fusion), calls=%async_computation.2 | async-start | bytes 2097152 | tf_op jit(solution)/shard_map/all_to_all | solution.py:118
  126.6 1.5 fusion.202
  128.1 2.5 %collective-permute-start.2 = (f32[2176,1]{0,1:T(1,128)}, f32[2176,1]{0,1:T(1,128)}, u32[]{:S(2)}, u32[]{:S(2)}) collective-permute-start(f32[2176,1]{0,1:T(1,128)} %get-tuple-element.42), channel_id=1, source_target_pairs={{0,1},{1,2},{2,3},{3,4},{4,5},{5,6},{6,7},{7,8},{8,9},{9,10},{10,1... | collective-permute-start | bytes 26120 | tf_op jit(solution)/shard_map/ppermute | solution.py:23
  130.6 2.4 %collective-permute-start.3 = (f32[2176,1]{0,1:T(1,128)}, f32[2176,1]{0,1:T(1,128)}, u32[]{:S(2)}, u32[]{:S(2)}) collective-permute-start(f32[2176,1]{0,1:T(1,128)} %get-tuple-element.43), channel_id=1, source_target_pairs={{1,0},{2,1},{3,2},{4,3},{5,4},{6,5},{7,6},{8,7},{9,8},{10,9},{11,1... | collective-permute-start | bytes 26120 | tf_op jit(solution)/shard_map/ppermute | solution.py:24
  133.2 2.2 %scatter_custom_fusion = f32[2176,128]{1,0:T(8,128)} fusion(s32[128]{0:T(128)} %copy-done.37, f32[]{:T(128)} %constant.39.clone.1, f32[128,128]{1,0:T(8,128)S(1)} %copy-done.20, f32[128,128]{1,0:T(8,128)S(1)} %copy-done.19, f32[128]{0:T(128)S(1)} %broadcast_select_fusion.67, f32[128]{0:T(128)S(1)} %bitcast.1285), kind=kCustom, calls=%fused_computation.87 | custom fusion | flops 65536 | bytes 1246720 | tf_op jit(solution)/shard_map/scatter-add | solution.py:178
  135.4 2.6 %copy.45 = f32[2176,128]{0,1:T(8,128)} copy(f32[2176,128]{1,0:T(8,128)} %scatter_custom_fusion) | data formatting | bytes 2228224 | tf_op jit(solution)/shard_map/scatter-add | solution.py:178
  138.1 14.4 %all-to-all-done.2 = f32[16,128,128]{2,1,0:T(8,128)} async-done(((f32[16,128,128]{2,1,0:T(8,128)}), f32[16,128,128]{2,1,0:T(8,128)}, u32[]{:S(2)}, u32[]{:S(2)}) %all-to-all-start.2) | async-done | bytes 1048608 | tf_op jit(solution)/shard_map/all_to_all | solution.py:118
  152.5 2.7 %gather_fusion.3 = f32[8,128,128]{2,1,0:T(8,128)} fusion(f32[16,128,128]{2,1,0:T(8,128)} %all-to-all-done.2, s32[1024]{0:T(1024)} %copy-done.28), kind=kCustom, calls=%fused_computation.6 | custom fusion | bytes 1048608 | tf_op jit(solution)/shard_map/jit(_take)/gather | solution.py:119
  155.2 2.5 %add_bitcast_fusion = (f32[1,8,128,128]{3,2,1,0:T(8,128)}, f32[8,128,128]{2,1,0:T(8,128)S(1)}) fusion(bf16[1,8,128,128]{3,2,1,0:T(8,128)(2,1)S(1)} %copy-done.5, f32[8,128]{1,0:T(8,128)S(1)} %bitcast.1275, f32[8,128,128]{2,1,0:T(8,128)S(1)} %fusion.7, f32[8,128,128]{2,1,0:T(8,128)} %gather_fusion.3, pred[8]{0:T(512)(128)(4,1)S(1)} %copy-done.35, ...), kind=kLoop, calls=%fused_computation.105 | loop fusion | flops 1835008 | bytes 3944456 | tf_op jit(solution)/shard_map/broadcast_in_dim | solution.py:190
  157.9 2.5 %fusion.4 = f32[2176,384]{0,1:T(8,128)S(1)} fusion(s32[1024]{0:T(1024)S(1)} %bitcast.1289, bf16[1024,128]{1,0:T(8,128)(2,1)S(1)} %get-tuple-element.51, bf16[1024,128]{1,0:T(8,128)(2,1)S(1)} %get-tuple-element.52, bf16[1024,128]{1,0:T(8,128)(2,1)S(1)} %get-tuple-element.50), kind=kOutput, calls=%fused_computation.15 | convolution fusion | flops 1715863552 | bytes 4132864 | tf_op jit(solution)/shard_map/dot_general | solution.py:135
  161.3 3.0 %fusion.18 = f32[2176,128]{0,1:T(8,128)S(1)} fusion(bf16[2176,128]{1,0:T(8,128)(2,1)S(1)} %bitcast.1270, bf16[1,2176,2176]{2,1,0:T(8,128)(2,1)S(1)} %bitcast.1267, f32[2176,128]{0,1:T(8,128)S(1)} %copy-done.2, f32[2176,128]{0,1:T(8,128)S(1)} %copy-done.1, f32[2176,384]{0,1:T(8,128)S(1)} %fusion.4, bf16[1,2176,128]{1,2,0:T(8,128)(2,1)S(1)} %copy-done.9), kind=kOutput, calls=%fused_computation.25 | convolution fusion | flops 1214103552 | bytes 17268736 | tf_op jit(solution)/shard_map/dot_general | solution.py:164
  164.4 1.4 copy.50
  165.7 2.0 %gather_fusion.4 = f32[128,128]{1,0:T(8,128)S(1)} fusion(f32[2176,128]{1,0:T(8,128)} %copy.50, s32[1024]{0:T(1024)} %copy-done.29), kind=kCustom, calls=%fused_computation.7 | custom fusion | bytes 131584 | tf_op jit(solution)/shard_map/gather | solution.py:168
  168.5 2.3 %shard_map.184 = (f32[128,128]{1,0:T(8,128)}, f32[128,128]{1,0:T(8,128)}) custom-call(f32[128,128]{1,0:T(8,128)} %bitcast.1277, f32[128,128]{1,0:T(8,128)} %multiply_multiply_fusion.charge_ref), custom_call_target="tpu_custom_call" | custom-call | tf_op jit(solution)/shard_map/pallas_call | solution.py:53
  171.8 1.0 slice_reduce_fusion.1
  173.4 12.0 %all-to-all-start.3 = ((f32[32,2,128]{2,1,0:T(2,128)}), f32[32,2,128]{2,1,0:T(2,128)S(1)}, u32[]{:S(2)}, u32[]{:S(2)}) async-start(f32[32,2,128]{2,1,0:T(2,128)} %broadcast_in_dim.101), calls=%async_computation.3 | async-start | bytes 65536 | tf_op jit(solution)/shard_map/all_to_all | solution.py:172
  185.5 2.2 %fusion.57 = (bf16[1,2176,128]{1,2,0:T(8,128)(2,1)}, bf16[2176,128]{0,1:T(8,128)(2,1)}) fusion(f32[2176,1]{0,1:T(1,128)} %collective-permute-done.3, f32[2176,128]{0,1:T(8,128)S(1)} %copy-done.1, f32[2176,1]{0,1:T(1,128)} %collective-permute-done.2, f32[2176]{0:T(1024)S(1)} %copy-done.22, f32[2176,128]{0,1:T(8,128)S(1)} %fusion.18, f32[2176]{0:T(1024)S(1)} %reduce.2), kind=kLoop, calls=%fused_computation.89 | loop fusion | flops 3620864 | bytes 3377152 | tf_op jit(solution)/shard_map/broadcast_in_dim | solution.py:189
  187.7 1.4 copy.49
  190.5 1.1 bitcast_subtract_fusion
  191.6 1.0 copy.51
  192.6 2.5 %all-to-all-done.3 = f32[32,2,128]{2,1,0:T(2,128)S(1)} async-done(((f32[32,2,128]{2,1,0:T(2,128)}), f32[32,2,128]{2,1,0:T(2,128)S(1)}, u32[]{:S(2)}, u32[]{:S(2)}) %all-to-all-start.3) | async-done | bytes 32800 | tf_op jit(solution)/shard_map/all_to_all | solution.py:172
  (133 shorter events, 15.1 us)
Async XLA Ops:
  0.6 111.9 %copy-start = (bf16[1,34,64,64]{3,2,1,0:T(8,128)(2,1)S(1)}, bf16[1,34,64,64]{3,2,1,0:T(8,128)(2,1)}, u32[]{:S(2)}) copy-start(bf16[1,34,64,64]{3,2,1,0:T(8,128)(2,1)} %param.23) | copy-start | bytes 835588
  1.7 5.8 %copy-start.30 = (pred[16]{0:T(512)(128)(4,1)}, pred[16]{0:T(512)(128)(4,1)S(1)}, u32[]{:S(2)}) copy-start(pred[16]{0:T(512)(128)(4,1)S(1)} %compare_and_fusion) | copy-start | bytes 52
  1.8 3.5 %copy-start.27 = (s32[1024]{0:T(1024)}, s32[1024]{0:T(1024)S(1)}, u32[]{:S(2)}) copy-start(s32[1024]{0:T(1024)S(1)} %pad_clamp_fusion.3) | copy-start | bytes 12292
  1.8 2.8 %copy-start.5 = (bf16[1,8,128,128]{3,2,1,0:T(8,128)(2,1)S(1)}, bf16[1,8,128,128]{3,2,1,0:T(8,128)(2,1)}, u32[]{:S(2)}) copy-start(bf16[1,8,128,128]{3,2,1,0:T(8,128)(2,1)} %param.21) | copy-start | bytes 786436
  5.2 1.6 copy-start.14
  10.5 59.3 %all-to-all-start = ((f32[16,264,128]{2,1,0:T(8,128)}), f32[16,264,128]{2,1,0:T(8,128)S(1)}, u32[]{:S(2)}, u32[]{:S(2)}) async-start(f32[16,264,128]{2,1,0:T(8,128)} %select_maximum_fusion), calls=%async_computation | async-start | bytes 4325376 | tf_op jit(solution)/shard_map/all_to_all | solution.py:118
  22.2 8.7 %copy-start.25 = (f32[1,2176]{1,0:T(1,128)S(1)}, f32[1,2176]{1,0:T(1,128)}, u32[]{:S(2)}) copy-start(f32[1,2176]{1,0:T(1,128)} %param.24) | copy-start | bytes 26116
  22.2 8.7 %copy-start.26 = (f32[1,2176]{1,0:T(1,128)S(1)}, f32[1,2176]{1,0:T(1,128)}, u32[]{:S(2)}) copy-start(f32[1,2176]{1,0:T(1,128)} %param.25) | copy-start | bytes 26116
  24.9 53.7 %collective-permute-start = (f32[2176,1]{0,1:T(1,128)}, f32[2176,1]{0,1:T(1,128)}, u32[]{:S(2)}, u32[]{:S(2)}) collective-permute-start(f32[2176,1]{0,1:T(1,128)} %get-tuple-element.46), channel_id=1, source_target_pairs={{0,1},{1,2},{2,3},{3,4},{4,5},{5,6},{6,7},{7,8},{8,9},{9,10},{10,1... | collective-permute-start | bytes 26120 | tf_op jit(solution)/shard_map/ppermute | solution.py:23
  28.9 49.7 %collective-permute-start.1 = (f32[2176,1]{0,1:T(1,128)}, f32[2176,1]{0,1:T(1,128)}, u32[]{:S(2)}, u32[]{:S(2)}) collective-permute-start(f32[2176,1]{0,1:T(1,128)} %get-tuple-element.47), channel_id=1, source_target_pairs={{1,0},{2,1},{3,2},{4,3},{5,4},{6,5},{7,6},{8,7},{9,8},{10,9},{11,1... | collective-permute-start | bytes 26120 | tf_op jit(solution)/shard_map/ppermute | solution.py:24
  30.9 47.7 %copy-start.21 = (f32[2176]{0:T(1024)}, f32[2176]{0:T(1024)S(1)}, u32[]{:S(2)}) copy-start(f32[2176]{0:T(1024)S(1)} %reduce.3) | copy-start | bytes 26116
  33.0 38.5 %copy-start.28 = (s32[1024]{0:T(1024)}, s32[1024]{0:T(1024)S(1)}, u32[]{:S(2)}) copy-start(s32[1024]{0:T(1024)S(1)} %pad_clamp_fusion.1) | copy-start | bytes 12292
  34.3 56.4 %copy-start.29 = (s32[1024]{0:T(1024)}, s32[1024]{0:T(1024)S(1)}, u32[]{:S(2)}) copy-start(s32[1024]{0:T(1024)S(1)} %pad_clamp_fusion) | copy-start | bytes 12292
  34.3 38.7 %copy-start.34 = (pred[8]{0:T(512)(128)(4,1)}, pred[8]{0:T(512)(128)(4,1)S(1)}, u32[]{:S(2)}) copy-start(pred[8]{0:T(512)(128)(4,1)S(1)} %compare_and_fusion.1) | copy-start | bytes 28
  34.9 56.9 %copy-start.32 = (f32[128]{0:T(128)}, f32[128]{0:T(128)S(1)}, u32[]{:S(2)}) copy-start(f32[128]{0:T(128)S(1)} %negate_bitcast_fusion) | copy-start | bytes 1540
  73.0 1.4 copy-start.38
  74.0 4.6 %slice-start = ((s8[9469952]{0:T(1024)(128)(4,1)}), s8[4194304]{0:T(1024)(128)(4,1)S(1)}, s32[]{:S(2)}) async-start(s8[9469952]{0:T(1024)(128)(4,1)} %bitcast.1264), calls=%async_computation.4 | async-start | bytes 8388608
  74.5 4.9 %slice-start.1 = ((s8[9469952]{0:T(1024)(128)(4,1)}), s8[4194304]{0:T(1024)(128)(4,1)S(1)}, s32[]{:S(2)}) async-start(s8[9469952]{0:T(1024)(128)(4,1)} %bitcast.1264), calls=%async_computation.5 | async-start | bytes 8388608
  74.5 5.4 %slice-start.2 = ((s8[9469952]{0:T(1024)(128)(4,1)}), s8[1081344]{0:T(1024)(128)(4,1)S(1)}, s32[]{:S(2)}) async-start(s8[9469952]{0:T(1024)(128)(4,1)} %bitcast.1264), calls=%async_computation.6 | async-start | bytes 2162688
  74.5 5.4 %copy-start.8 = (bf16[1,2176,128]{1,2,0:T(8,128)(2,1)S(1)}, bf16[1,2176,128]{1,2,0:T(8,128)(2,1)}, u32[]{:S(2)}) copy-start(bf16[1,2176,128]{1,2,0:T(8,128)(2,1)} %copy.41) | copy-start | bytes 1671172
  74.5 5.4 %copy-start.10 = (bf16[1,2176,128]{2,1,0:T(8,128)(2,1)S(1)}, bf16[1,2176,128]{2,1,0:T(8,128)(2,1)}, u32[]{:S(2)}) copy-start(bf16[1,2176,128]{2,1,0:T(8,128)(2,1)} %param.18) | copy-start | bytes 1671172
  74.5 5.4 %copy-start.12 = (bf16[1,2176,128]{1,2,0:T(8,128)(2,1)S(1)}, bf16[1,2176,128]{1,2,0:T(8,128)(2,1)}, u32[]{:S(2)}) copy-start(bf16[1,2176,128]{1,2,0:T(8,128)(2,1)} %copy.42) | copy-start | bytes 1671172
  74.5 5.4 %copy-start.16 = (f32[2176,128]{0,1:T(8,128)S(1)}, f32[2176,128]{0,1:T(8,128)}, u32[]{:S(2)}) copy-start(f32[2176,128]{0,1:T(8,128)} %copy-done.15) | copy-start | bytes 3342340
  97.4 24.8 %all-to-all-start.1 = ((f32[32,2,128]{2,1,0:T(2,128)}), f32[32,2,128]{2,1,0:T(2,128)S(1)}, u32[]{:S(2)}, u32[]{:S(2)}) async-start(f32[32,2,128]{2,1,0:T(2,128)} %broadcast_in_dim.96), calls=%async_computation.1 | async-start | bytes 65536 | tf_op jit(solution)/shard_map/all_to_all | solution.py:172
  112.5 2.5 %copy-start.39 = (s32[1,8,128]{2,1,0:T(8,128)S(1)}, s32[1,8,128]{2,1,0:T(8,128)}, u32[]{:S(2)}) copy-start(s32[1,8,128]{2,1,0:T(8,128)} %param.27) | copy-start | bytes 12292
  115.0 1.6 copy-start.6
  116.7 1.7 copy-start.31
  120.8 12.4 %copy-start.19 = (f32[128,128]{1,0:T(8,128)S(1)}, f32[128,128]{1,0:T(8,128)}, u32[]{:S(2)}) copy-start(f32[128,128]{1,0:T(8,128)} %get-tuple-element.10) | copy-start | bytes 196612
  120.8 12.4 %copy-start.20 = (f32[128,128]{1,0:T(8,128)S(1)}, f32[128,128]{1,0:T(8,128)}, u32[]{:S(2)}) copy-start(f32[128,128]{1,0:T(8,128)} %get-tuple-element.9) | copy-start | bytes 196612
  120.8 12.4 %copy-start.36 = (f32[1,128]{1,0:T(1,128)S(1)}, f32[1,128]{1,0:T(1,128)}, u32[]{:S(2)}) copy-start(f32[1,128]{1,0:T(1,128)} %param.32) | copy-start | bytes 1540
  122.2 30.3 %all-to-all-start.2 = ((f32[16,128,128]{2,1,0:T(8,128)}), f32[16,128,128]{2,1,0:T(8,128)}, u32[]{:S(2)}, u32[]{:S(2)}) async-start(f32[16,128,128]{2,1,0:T(8,128)} %broadcast_select_fusion), calls=%async_computation.2 | async-start | bytes 2097152 | tf_op jit(solution)/shard_map/all_to_all | solution.py:118
  128.1 57.3 %collective-permute-start.2 = (f32[2176,1]{0,1:T(1,128)}, f32[2176,1]{0,1:T(1,128)}, u32[]{:S(2)}, u32[]{:S(2)}) collective-permute-start(f32[2176,1]{0,1:T(1,128)} %get-tuple-element.42), channel_id=1, source_target_pairs={{0,1},{1,2},{2,3},{3,4},{4,5},{5,6},{6,7},{7,8},{8,9},{9,10},{10,1... | collective-permute-start | bytes 26120 | tf_op jit(solution)/shard_map/ppermute | solution.py:23
  130.6 54.9 %collective-permute-start.3 = (f32[2176,1]{0,1:T(1,128)}, f32[2176,1]{0,1:T(1,128)}, u32[]{:S(2)}, u32[]{:S(2)}) collective-permute-start(f32[2176,1]{0,1:T(1,128)} %get-tuple-element.43), channel_id=1, source_target_pairs={{1,0},{2,1},{3,2},{4,3},{5,4},{6,5},{7,6},{8,7},{9,8},{10,9},{11,1... | collective-permute-start | bytes 26120 | tf_op jit(solution)/shard_map/ppermute | solution.py:24
  135.4 19.8 %slice-start.6 = ((f32[8,33792]{1,0:T(8,128)}), f32[8,128]{1,0:T(8,128)S(1)}, s32[]{:S(2)}) async-start(f32[8,33792]{1,0:T(8,128)} %copy-done.4), calls=%async_computation.10 | async-start | bytes 8192 | tf_op jit(solution)/shard_map/slice | solution.py:123
  135.4 19.8 %copy-start.24 = (f32[1,8,128]{2,1,0:T(8,128)S(1)}, f32[1,8,128]{2,1,0:T(8,128)}, u32[]{:S(2)}) copy-start(f32[1,8,128]{2,1,0:T(8,128)} %param.28) | copy-start | bytes 12292
  135.4 19.8 %copy-start.35 = (pred[8]{0:T(512)(128)(4,1)S(1)}, pred[8]{0:T(512)(128)(4,1)}, u32[]{:S(2)}) copy-start(pred[8]{0:T(512)(128)(4,1)} %copy-done.34) | copy-start | bytes 28
  155.2 5.2 %slice-start.3 = ((s8[9469952]{0:T(1024)(128)(4,1)}), s8[4194304]{0:T(1024)(128)(4,1)S(1)}, s32[]{:S(2)}) async-start(s8[9469952]{0:T(1024)(128)(4,1)} %bitcast.1266), calls=%async_computation.7 | async-start | bytes 8388608
  157.8 2.5 %slice-start.4 = ((s8[9469952]{0:T(1024)(128)(4,1)}), s8[4194304]{0:T(1024)(128)(4,1)S(1)}, s32[]{:S(2)}) async-start(s8[9469952]{0:T(1024)(128)(4,1)} %bitcast.1266), calls=%async_computation.8 | async-start | bytes 8388608
  157.9 2.5 %slice-start.5 = ((s8[9469952]{0:T(1024)(128)(4,1)}), s8[1081344]{0:T(1024)(128)(4,1)S(1)}, s32[]{:S(2)}) async-start(s8[9469952]{0:T(1024)(128)(4,1)} %bitcast.1266), calls=%async_computation.9 | async-start | bytes 2162688
  157.9 2.8 %copy-start.1 = (f32[2176,128]{0,1:T(8,128)S(1)}, f32[2176,128]{0,1:T(8,128)}, u32[]{:S(2)}) copy-start(f32[2176,128]{0,1:T(8,128)} %get-tuple-element.44) | copy-start | bytes 3342340
  157.9 3.1 %copy-start.2 = (f32[2176,128]{0,1:T(8,128)S(1)}, f32[2176,128]{0,1:T(8,128)}, u32[]{:S(2)}) copy-start(f32[2176,128]{0,1:T(8,128)} %copy.45) | copy-start | bytes 3342340
  157.9 3.2 %copy-start.7 = (bf16[34,64,128]{2,1,0:T(8,128)(2,1)S(1)}, bf16[34,64,128]{2,1,0:T(8,128)(2,1)}, u32[]{:S(2)}) copy-start(bf16[34,64,128]{2,1,0:T(8,128)(2,1)} %copy-done.6) | copy-start | bytes 1671172
  157.9 3.4 %copy-start.9 = (bf16[1,2176,128]{1,2,0:T(8,128)(2,1)S(1)}, bf16[1,2176,128]{1,2,0:T(8,128)(2,1)}, u32[]{:S(2)}) copy-start(bf16[1,2176,128]{1,2,0:T(8,128)(2,1)} %copy.41) | copy-start | bytes 1671172
  164.3 3.4 %copy-start.33 = (f32[128]{0:T(128)S(1)}, f32[128]{0:T(128)}, u32[]{:S(2)}) copy-start(f32[128]{0:T(128)} %copy-done.32) | copy-start | bytes 1540
  164.3 21.1 %copy-start.22 = (f32[2176]{0:T(1024)S(1)}, f32[2176]{0:T(1024)}, u32[]{:S(2)}) copy-start(f32[2176]{0:T(1024)} %copy-done.21) | copy-start | bytes 26116
  173.4 21.7 %all-to-all-start.3 = ((f32[32,2,128]{2,1,0:T(2,128)}), f32[32,2,128]{2,1,0:T(2,128)S(1)}, u32[]{:S(2)}, u32[]{:S(2)}) async-start(f32[32,2,128]{2,1,0:T(2,128)} %broadcast_in_dim.101), calls=%async_computation.3 | async-start | bytes 65536 | tf_op jit(solution)/shard_map/all_to_all | solution.py:172
  191.6 3.7 %copy-start.17 = (f32[128,128]{1,0:T(8,128)S(1)}, f32[128,128]{1,0:T(8,128)}, u32[]{:S(2)}) copy-start(f32[128,128]{1,0:T(8,128)} %get-tuple-element.12) | copy-start | bytes 196612
  191.6 3.7 %copy-start.18 = (f32[128,128]{1,0:T(8,128)S(1)}, f32[128,128]{1,0:T(8,128)}, u32[]{:S(2)}) copy-start(f32[128,128]{1,0:T(8,128)} %get-tuple-element.11) | copy-start | bytes 196612
  (7 other events, 7.4 us)

commit v7 on v4

--- a/solution.py
+++ b/solution.py
@@ -82,7 +82,7 @@
     area_count = lax.axis_size("area")
     area_here = lax.axis_index("area")
     position = lax.axis_index("tm")
-    partners = jnp.take(partner, area_here, axis=1)
+    partners = jnp.take(partner, area_here, axis=1, mode="clip")
     edge_rows = boundary[0]
     store_rows = store_bus[0]
     matrix = susceptance[0]
@@ -113,10 +113,11 @@
 
     def exchanged(parts, shapes):
         lanes = 128
-        sent = jnp.concatenate([part.reshape(area_count, -1, lanes) for part in parts], axis=1)
-        sent = jnp.pad(sent, ((0, 0), (0, -sent.shape[1] % 8), (0, 0)))
+        blocks = [part.reshape(rounds, -1, lanes) for part in parts]
+        blocks = [jnp.pad(b, ((0, 0), (0, -b.shape[1] % 8), (0, 0))) for b in blocks]
+        sent = jnp.take(jnp.concatenate(blocks, axis=1), round_of, axis=0, mode="clip")
         got = lax.all_to_all(sent, "area", split_axis=0, concat_axis=0, tiled=True)
-        got = jnp.take(got, partners, axis=0).reshape(rounds, -1)
+        got = jnp.take(got, partners, axis=0, mode="clip").reshape(rounds, -1)
         found, at = [], 0
         for shape in shapes:
             width = math.prod(shape[1:])
@@ -131,16 +132,14 @@
     for iteration in range(ITERS):
         rounded = angle_now.astype(jnp.bfloat16)
         own_edge = lax.optimization_barrier(rounded[edge_rows].astype(jnp.float32))
-        edge_out = jnp.take(own_edge, round_of, axis=0)
         if iteration == 0:
             far_edge, price_far, penalty_far = exchanged(
-                (edge_out, jnp.take(price_now, round_of, axis=0),
-                 jnp.take(tie_penalty[0], round_of, axis=0)),
+                (own_edge, price_now, tie_penalty[0]),
                 (own_edge.shape, price_now.shape, tie_penalty[0].shape),
             )
             penalty_far = penalty_far[:, :, None]
         else:
-            (far_edge,) = exchanged((edge_out,), (own_edge.shape,))
+            (far_edge,) = exchanged((own_edge,), (own_edge.shape,))
             price_far = price_far - penalty_far * mismatch
         mismatch = own_edge - far_edge
         tie_flow = tie_gain * mismatch + 0.5 * (price_now - price_far)

time: 194 us -> 185 us (0.954)
  other arithmetic: 40 us -> 30.9 us
    select_n x7 -> x0, other arithmetic: 6.42 us -> none  [the longest x3 3.86 us: local(): edge_out = jnp.take(own_edge, round_of, axis=0)]
    gather x6 -> x4, local copies, waits for them, and re-layouts: 10.1 us -> 8.51 us  [the longest x2 4.82 us: exchanged(): got = jnp.take(got, partners, axis=0, mode='clip').reshape(rounds, -1)]
    unnamed x51 -> x54, local copies, waits for them, and re-layouts: 3.92 us -> 5.23 us
  transfers between devices with their start and end apart: 8 -> 8, of which waited for: 4 -> 4; matrix products, arithmetic and copies ran while one was open for 24% -> 22% of each run, Pallas kernels for 0% -> 0%
where the time goes in v7:
time: 185 us; the launch traced here: 184 us
  starting transfers between devices  53.8 us (29%)
  waiting for transfers between devices  40.6 us (22%)
  local copies, waits for them, and re-layouts  38.1 us (21%)
  other arithmetic  30.9 us (17%)
  matrix products  14.9 us (8%)
  Pallas kernels  4.55 us (2%)
    all_to_all x2, waiting for transfers between devices, exchanged(): got = lax.all_to_all(sent, 'area', split_axis=0, concat_axis=0, tiled=True)  35.7 us
    all_to_all x2, starting transfers between devices, local(): ends = lax.all_to_all(copies, 'tm', split_axis=0, concat_axis=0, tiled=True)  28.2 us
    all_to_all x2, starting transfers between devices, exchanged(): got = lax.all_to_all(sent, 'area', split_axis=0, concat_axis=0, tiled=True)  14.1 us
    dot_general x2, matrix products, local(): jnp.dot(matrix, rounded, preferred_element_type=jnp.float32) + fixed_part  13.6 us
    scatter-add x2, other arithmetic, local(): jnp.zeros((bus_count, hour_count), jnp.float32).at[edge_rows].add(tie_flow)  13.3 us
    gather x2, local copies, waits for them, and re-layouts, local(): own_edge = lax.optimization_barrier(rounded[edge_rows].astype(jnp.float32))  7.26 us
    ppermute x2, starting transfers between devices, padded_2(): before = lax.ppermute(last, axis, up)  5.84 us
    ppermute x2, starting transfers between devices, padded_2(): after = lax.ppermute(leading, axis, down)  5.75 us
  transfers between devices with their start and end apart: 8, of which 4 were waited for; matrix products, arithmetic and copies ran while one was open for 22% of the time, Pallas kernels for 0%

profile of v7, /device:TPU:1, one launch (start us, length us, event | category | flops | bytes accessed | tf_op | source)
XLA Modules:
  0.0 184.2 jit_solution(8675269928339820569)
XLA Ops:
  0.7 0.9 dynamic-slice_reduce_fusion
  1.7 0.7 broadcast_clamp_fusion
  2.4 4.0 %gather_fusion = bf16[1024,128]{1,0:T(8,128)(2,1)S(1)} fusion(bf16[2176,128]{1,0:T(8,128)(2,1)} %bitcast.1251, s32[1024]{0:T(1024)S(1)} %broadcast_clamp_fusion), kind=kCustom, calls=%fused_computation | custom fusion | bytes 528384 | tf_op jit(solution)/shard_map/gather | solution.py:134
  7.3 2.1 %gather_fusion.1 = f32[16,264,128]{2,1,0:T(8,128)} fusion(f32[8,264,128]{2,1,0:T(8,128)S(1)} %select_maximum_fusion, s32[1024]{0:T(1024)S(1)} %pad_clamp_fusion.2), kind=kCustom, calls=%fused_computation.1 | custom fusion | bytes 4325440 | tf_op jit(solution)/shard_map/jit(_take)/gather | solution.py:118
  9.4 9.7 %all-to-all-start = ((f32[16,264,128]{2,1,0:T(8,128)}), f32[16,264,128]{2,1,0:T(8,128)}, u32[]{:S(2)}, u32[]{:S(2)}) async-start(f32[16,264,128]{2,1,0:T(8,128)} %gather_fusion.1), calls=%async_computation | async-start | bytes 4325376 | tf_op jit(solution)/shard_map/all_to_all | solution.py:119
  20.5 3.6 %collective-permute-start.1 = (f32[2176,1]{0,1:T(1,128)S(1)}, f32[2176,1]{0,1:T(1,128)S(1)}, u32[]{:S(2)}, u32[]{:S(2)}) collective-permute-start(f32[2176,1]{0,1:T(1,128)S(1)} %copy.34), channel_id=1, source_target_pairs={{1,0},{2,1},{3,2},{4,3},{5,4},{6,5},{7,6},{8,7},{9,8},{10,9},{11,1... | collective-permute-start | bytes 26120 | tf_op jit(solution)/shard_map/ppermute | solution.py:24
  24.5 2.3 %collective-permute-start = (f32[2176,1]{0,1:T(1,128)S(1)}, f32[2176,1]{0,1:T(1,128)S(1)}, u32[]{:S(2)}, u32[]{:S(2)}) collective-permute-start(f32[2176,1]{0,1:T(1,128)S(1)} %copy.32), channel_id=1, source_target_pairs={{0,1},{1,2},{2,3},{3,4},{4,5},{5,6},{6,7},{7,8},{8,9},{9,10},{10,1... | collective-permute-start | bytes 26120 | tf_op jit(solution)/shard_map/ppermute | solution.py:23
  26.9 6.6 %fusion.10 = f32[2176,128]{1,0:T(8,128)S(1)} fusion(bf16[1,2176,2176]{2,1,0:T(8,128)(2,1)} %param.20, bf16[1,2176,128]{2,1,0:T(8,128)(2,1)} %param.17, bf16[1,2176,128]{2,1,0:T(8,128)(2,1)} %param.18, bf16[1,2176,128]{2,1,0:T(8,128)(2,1)S(1)} %copy-done.1), kind=kOutput, calls=%fused_computation.17 | convolution fusion | flops 1213267968 | bytes 12255232 | tf_op jit(solution)/shard_map/dot_general | solution.py:148
  33.6 1.4 copy.33
  35.0 1.4 copy.35
  36.4 32.1 %all-to-all-done = f32[16,264,128]{2,1,0:T(8,128)} async-done(((f32[16,264,128]{2,1,0:T(8,128)}), f32[16,264,128]{2,1,0:T(8,128)}, u32[]{:S(2)}, u32[]{:S(2)}) %all-to-all-start) | async-done | bytes 2162720 | tf_op jit(solution)/shard_map/all_to_all | solution.py:119
  68.5 2.2 %gather_fusion.2 = f32[8,264,128]{2,1,0:T(8,128)S(1)} fusion(f32[16,264,128]{2,1,0:T(8,128)} %all-to-all-done, s32[1024]{0:T(1024)S(1)} %pad_clamp_fusion.1), kind=kCustom, calls=%fused_computation.2 | custom fusion | bytes 2162720 | tf_op jit(solution)/shard_map/jit(_take)/gather | solution.py:120
  71.0 0.9 copy-done.10
  73.0 6.4 %scatter_fusion = f32[2176,128]{1,0:T(8,128)S(1)} fusion(f32[2176,128]{1,0:T(8,128)S(1)} %fusion.10, s32[1024]{0:T(1024)S(1)} %fusion.44, f32[1024,128]{1,0:T(8,128)S(1)} %bitcast.1260), kind=kCustom, calls=%fused_computation.8 | custom fusion | flops 131072 | bytes 1576960 | tf_op jit(solution)/shard_map/scatter-add | solution.py:146
  80.1 0.7 multiply_multiply_fusion.1.charge_ref
  80.8 2.3 %shard_map.183 = (f32[128,128]{1,0:T(8,128)}, f32[128,128]{1,0:T(8,128)}) custom-call(f32[128,128]{1,0:T(8,128)} %bitcast.1263, f32[128,128]{1,0:T(8,128)} %multiply_multiply_fusion.1.charge_ref), custom_call_target="tpu_custom_call" | custom-call | tf_op jit(solution)/shard_map/pallas_call | solution.py:53
  83.1 1.0 slice_reduce_fusion.2
  84.8 15.5 %all-to-all-start.1 = ((f32[32,2,128]{2,1,0:T(2,128)}), f32[32,2,128]{2,1,0:T(2,128)S(1)}, u32[]{:S(2)}, u32[]{:S(2)}) async-start(f32[32,2,128]{2,1,0:T(2,128)} %broadcast_in_dim.62), calls=%async_computation.1 | async-start | bytes 65536 | tf_op jit(solution)/shard_map/all_to_all | solution.py:156
  100.3 3.7 %fusion.21 = (f32[2176,128]{1,0:T(8,128)S(1)}, bf16[2176,128]{1,0:T(8,128)(2,1)S(1)}) fusion(f32[2176,1]{1,0:T(8,128)} %copy.35, f32[2176,128]{1,0:T(8,128)} %copy-done.2, f32[2176,1]{1,0:T(8,128)} %copy.33, f32[2176,128]{1,0:T(8,128)S(1)} %scatter_fusion, bf16[1,2176,128]{2,1,0:T(8,128)(2,1)} %param.17, f32[2176]{0:T(1024)S(1)} %reduce.2, f32[2176]{0:T(1024)S(1)} %reduce.1), kind=kLoop, calls=%fused_computation.31 | loop fusion | flops 3620864 | bytes 4491264 | tf_op jit(solution)/shard_map/add | solution.py:151
  104.0 1.1 fusion.26
  105.1 1.0 copy-done.3
  106.2 3.2 %gather_fusion.4 = bf16[1024,128]{1,0:T(8,128)(2,1)S(1)} fusion(bf16[2176,128]{1,0:T(8,128)(2,1)S(1)} %fusion.23, s32[1024]{0:T(1024)S(1)} %broadcast_clamp_fusion), kind=kCustom, calls=%fused_computation.4 | custom fusion | bytes 528384 | tf_op jit(solution)/shard_map/gather | solution.py:134
  109.5 1.6 gather_fusion.5
  111.2 4.4 %all-to-all-start.2 = ((f32[16,128,128]{2,1,0:T(8,128)}), f32[16,128,128]{2,1,0:T(8,128)}, u32[]{:S(2)}, u32[]{:S(2)}) async-start(f32[16,128,128]{2,1,0:T(8,128)} %gather_fusion.5), calls=%async_computation.2 | async-start | bytes 2097152 | tf_op jit(solution)/shard_map/all_to_all | solution.py:119
  115.5 1.3 fusion.173
  116.9 1.6 copy.36
  118.4 3.6 %collective-permute-start.2 = (f32[2176,1]{0,1:T(1,128)S(1)}, f32[2176,1]{0,1:T(1,128)S(1)}, u32[]{:S(2)}, u32[]{:S(2)}) collective-permute-start(f32[2176,1]{0,1:T(1,128)S(1)} %copy.36), channel_id=1, source_target_pairs={{0,1},{1,2},{2,3},{3,4},{4,5},{5,6},{6,7},{7,8},{8,9},{9,10},{10,1... | collective-permute-start | bytes 26120 | tf_op jit(solution)/shard_map/ppermute | solution.py:23
  122.4 2.1 %collective-permute-start.3 = (f32[2176,1]{0,1:T(1,128)S(1)}, f32[2176,1]{0,1:T(1,128)S(1)}, u32[]{:S(2)}, u32[]{:S(2)}) collective-permute-start(f32[2176,1]{0,1:T(1,128)S(1)} %copy.38), channel_id=1, source_target_pairs={{1,0},{2,1},{3,2},{4,3},{5,4},{6,5},{7,6},{8,7},{9,8},{10,9},{11,1... | collective-permute-start | bytes 26120 | tf_op jit(solution)/shard_map/ppermute | solution.py:24
  124.5 0.7 slice.927
  125.2 1.4 copy.37
  126.6 1.1 collective-permute-done.3
  127.7 1.4 copy.39
  129.3 2.1 %scatter_custom_fusion.1 = f32[2176,128]{1,0:T(8,128)} fusion(s32[128]{0:T(128)S(1)} %fusion.47, f32[]{:T(128)} %constant.42.clone.1, f32[128,128]{1,0:T(8,128)S(1)} %copy-done.17, f32[128,128]{1,0:T(8,128)S(1)} %copy-done.16, f32[128]{0:T(128)S(1)} %broadcast_select_fusion.63, f32[128]{0:T(128)S(1)} %bitcast.1273), kind=kCustom, calls=%fused_computation.53 | custom fusion | flops 65536 | bytes 1246212 | tf_op jit(solution)/shard_map/scatter-add | solution.py:162
  131.4 7.0 %fusion.7 = f32[2176,128]{1,0:T(8,128)S(1)} fusion(bf16[2176,128]{1,0:T(8,128)(2,1)} %bitcast.1256, bf16[1,2176,2176]{2,1,0:T(8,128)(2,1)} %param.20, f32[2176,128]{1,0:T(8,128)} %scatter_custom_fusion.1, f32[2176,128]{1,0:T(8,128)S(1)} %get-tuple-element.29, bf16[1,2176,128]{2,1,0:T(8,128)(2,1)} %param.18), kind=kOutput, calls=%fused_computation.16 | convolution fusion | flops 1213267968 | bytes 13926400 | tf_op jit(solution)/shard_map/dot_general | solution.py:148
  138.4 3.6 %all-to-all-done.2 = f32[16,128,128]{2,1,0:T(8,128)} async-done(((f32[16,128,128]{2,1,0:T(8,128)}), f32[16,128,128]{2,1,0:T(8,128)}, u32[]{:S(2)}, u32[]{:S(2)}) %all-to-all-start.2) | async-done | bytes 1048608 | tf_op jit(solution)/shard_map/all_to_all | solution.py:119
  142.0 2.6 %gather_fusion.6 = f32[8,128,128]{2,1,0:T(8,128)} fusion(f32[16,128,128]{2,1,0:T(8,128)} %all-to-all-done.2, s32[1024]{0:T(1024)S(1)} %pad_clamp_fusion.1), kind=kCustom, calls=%fused_computation.6 | custom fusion | bytes 1048608 | tf_op jit(solution)/shard_map/jit(_take)/gather | solution.py:120
  144.6 3.2 %add_bitcast_fusion = (f32[1,8,128,128]{3,2,1,0:T(8,128)}, f32[8,128,128]{2,1,0:T(8,128)}) fusion(bf16[1,8,128,128]{3,2,1,0:T(8,128)(2,1)} %param.19, f32[8,128]{1,0:T(8,128)S(1)} %bitcast.1266, f32[8,128,128]{2,1,0:T(8,128)} %copy-done.5, f32[8,128,128]{2,1,0:T(8,128)} %gather_fusion.6, f32[8,128,128]{2,1,0:T(8,128)} %copy-done.6, ...), kind=kLoop, calls=%fused_computation.66 | loop fusion | flops 1703936 | bytes 3944448 | tf_op jit(solution)/shard_map/broadcast_in_dim | solution.py:174
  147.8 6.8 %scatter_fusion.1 = f32[2176,128]{1,0:T(8,128)S(1)} fusion(f32[2176,128]{1,0:T(8,128)S(1)} %fusion.7, s32[1024]{0:T(1024)S(1)} %fusion.44, f32[1024,128]{1,0:T(8,128)} %bitcast.1259), kind=kCustom, calls=%fused_computation.10 | custom fusion | flops 131072 | bytes 1576960 | tf_op jit(solution)/shard_map/scatter-add | solution.py:146
  155.3 0.7 multiply_multiply_fusion.charge_ref
  156.0 2.3 %shard_map.184 = (f32[128,128]{1,0:T(8,128)}, f32[128,128]{1,0:T(8,128)}) custom-call(f32[128,128]{1,0:T(8,128)} %bitcast.1264, f32[128,128]{1,0:T(8,128)} %multiply_multiply_fusion.charge_ref), custom_call_target="tpu_custom_call" | custom-call | tf_op jit(solution)/shard_map/pallas_call | solution.py:53
  158.3 1.0 slice_reduce_fusion
  159.3 1.0 slice_reduce_fusion.1
  161.0 12.7 %all-to-all-start.3 = ((f32[32,2,128]{2,1,0:T(2,128)}), f32[32,2,128]{2,1,0:T(2,128)S(1)}, u32[]{:S(2)}, u32[]{:S(2)}) async-start(f32[32,2,128]{2,1,0:T(2,128)} %broadcast_in_dim.65), calls=%async_computation.3 | async-start | bytes 65536 | tf_op jit(solution)/shard_map/all_to_all | solution.py:156
  173.7 3.6 %fusion.33 = (bf16[1,2176,128]{2,1,0:T(8,128)(2,1)}, bf16[2176,128]{1,0:T(8,128)(2,1)S(1)}) fusion(f32[2176,1]{1,0:T(8,128)} %copy.39, f32[2176,128]{1,0:T(8,128)S(1)} %get-tuple-element.29, f32[2176,1]{1,0:T(8,128)} %copy.37, f32[2176]{0:T(1024)S(1)} %reduce.2, f32[2176,128]{1,0:T(8,128)S(1)} %scatter_fusion.1, f32[2176]{0:T(1024)S(1)} %reduce.1), kind=kLoop, calls=%fused_computation.55 | loop fusion | flops 3620864 | bytes 3377152 | tf_op jit(solution)/shard_map/broadcast_in_dim | solution.py:173
  177.5 1.0 copy-done.4
  178.5 1.1 bitcast_subtract_fusion
  179.6 3.7 %all-to-all-done.3 = f32[32,2,128]{2,1,0:T(2,128)S(1)} async-done(((f32[32,2,128]{2,1,0:T(2,128)}), f32[32,2,128]{2,1,0:T(2,128)S(1)}, u32[]{:S(2)}, u32[]{:S(2)}) %all-to-all-start.3) | async-done | bytes 32800 | tf_op jit(solution)/shard_map/all_to_all | solution.py:156
  183.5 0.7 add_bitcast_fusion.1
  (84 shorter events, 7.6 us)
Async XLA Ops:
  0.6 103.4 %copy-start = (bf16[1,34,64,64]{3,2,1,0:T(8,128)(2,1)S(1)}, bf16[1,34,64,64]{3,2,1,0:T(8,128)(2,1)}, u32[]{:S(2)}) copy-start(bf16[1,34,64,64]{3,2,1,0:T(8,128)(2,1)} %param.21) | copy-start | bytes 835588
  2.4 4.1 %copy-start.11 = (bf16[1,8,128,128]{3,2,1,0:T(8,128)(2,1)S(1)}, bf16[1,8,128,128]{3,2,1,0:T(8,128)(2,1)}, u32[]{:S(2)}) copy-start(bf16[1,8,128,128]{3,2,1,0:T(8,128)(2,1)} %param.19) | copy-start | bytes 786436
  6.4 0.7 copy-start.18
  6.5 0.8 copy-start.6
  9.4 9.8 %copy-start.13 = (bf16[1,2176,128]{2,1,0:T(8,128)(2,1)S(1)}, bf16[1,2176,128]{2,1,0:T(8,128)(2,1)}, u32[]{:S(2)}) copy-start(bf16[1,2176,128]{2,1,0:T(8,128)(2,1)} %param.17) | copy-start | bytes 1671172
  9.4 59.2 %all-to-all-start = ((f32[16,264,128]{2,1,0:T(8,128)}), f32[16,264,128]{2,1,0:T(8,128)}, u32[]{:S(2)}, u32[]{:S(2)}) async-start(f32[16,264,128]{2,1,0:T(8,128)} %gather_fusion.1), calls=%async_computation | async-start | bytes 4325376 | tf_op jit(solution)/shard_map/all_to_all | solution.py:119
  19.2 1.0 copy-start.2
  20.2 6.6 %copy-start.24 = (s32[1,128]{1,0:T(1,128)S(1)}, s32[1,128]{1,0:T(1,128)}, u32[]{:S(2)}) copy-start(s32[1,128]{1,0:T(1,128)} %param.28) | copy-start | bytes 1540
  20.2 6.7 %copy-start.25 = (f32[1,128]{1,0:T(1,128)S(1)}, f32[1,128]{1,0:T(1,128)}, u32[]{:S(2)}) copy-start(f32[1,128]{1,0:T(1,128)} %param.29) | copy-start | bytes 1540
  20.2 6.7 %copy-start.20 = (s32[1,8,128]{2,1,0:T(8,128)S(1)}, s32[1,8,128]{2,1,0:T(8,128)}, u32[]{:S(2)}) copy-start(s32[1,8,128]{2,1,0:T(8,128)} %param.25) | copy-start | bytes 12292
  20.2 6.7 %copy-start.1 = (bf16[1,2176,128]{2,1,0:T(8,128)(2,1)S(1)}, bf16[1,2176,128]{2,1,0:T(8,128)(2,1)}, u32[]{:S(2)}) copy-start(bf16[1,2176,128]{2,1,0:T(8,128)(2,1)} %param.16) | copy-start | bytes 1671172
  20.5 14.5 %collective-permute-start.1 = (f32[2176,1]{0,1:T(1,128)S(1)}, f32[2176,1]{0,1:T(1,128)S(1)}, u32[]{:S(2)}, u32[]{:S(2)}) collective-permute-start(f32[2176,1]{0,1:T(1,128)S(1)} %copy.34), channel_id=1, source_target_pairs={{1,0},{2,1},{3,2},{4,3},{5,4},{6,5},{7,6},{8,7},{9,8},{10,9},{11,1... | collective-permute-start | bytes 26120 | tf_op jit(solution)/shard_map/ppermute | solution.py:24
  24.5 9.1 %collective-permute-start = (f32[2176,1]{0,1:T(1,128)S(1)}, f32[2176,1]{0,1:T(1,128)S(1)}, u32[]{:S(2)}, u32[]{:S(2)}) collective-permute-start(f32[2176,1]{0,1:T(1,128)S(1)} %copy.32), channel_id=1, source_target_pairs={{0,1},{1,2},{2,3},{3,4},{4,5},{5,6},{6,7},{7,8},{8,9},{9,10},{10,1... | collective-permute-start | bytes 26120 | tf_op jit(solution)/shard_map/ppermute | solution.py:23
  26.9 6.6 %copy-start.21 = (f32[1,2176]{1,0:T(1,128)S(1)}, f32[1,2176]{1,0:T(1,128)}, u32[]{:S(2)}) copy-start(f32[1,2176]{1,0:T(1,128)} %param.22) | copy-start | bytes 26116
  26.9 6.7 %copy-start.22 = (f32[1,2176]{1,0:T(1,128)S(1)}, f32[1,2176]{1,0:T(1,128)}, u32[]{:S(2)}) copy-start(f32[1,2176]{1,0:T(1,128)} %param.23) | copy-start | bytes 26116
  71.0 1.0 copy-start.10
  71.0 1.4 copy-start.7
  71.0 1.5 copy-start.12
  71.0 1.5 copy-start.19
  72.0 0.8 copy-start.8
  72.1 1.0 copy-start.9
  84.8 26.3 %all-to-all-start.1 = ((f32[32,2,128]{2,1,0:T(2,128)}), f32[32,2,128]{2,1,0:T(2,128)S(1)}, u32[]{:S(2)}, u32[]{:S(2)}) async-start(f32[32,2,128]{2,1,0:T(2,128)} %broadcast_in_dim.62), calls=%async_computation.1 | async-start | bytes 65536 | tf_op jit(solution)/shard_map/all_to_all | solution.py:156
  105.1 1.0 copy-start.3
  109.5 1.6 copy-start.5
  111.2 30.8 %all-to-all-start.2 = ((f32[16,128,128]{2,1,0:T(8,128)}), f32[16,128,128]{2,1,0:T(8,128)}, u32[]{:S(2)}, u32[]{:S(2)}) async-start(f32[16,128,128]{2,1,0:T(8,128)} %gather_fusion.5), calls=%async_computation.2 | async-start | bytes 2097152 | tf_op jit(solution)/shard_map/all_to_all | solution.py:119
  118.4 6.8 %collective-permute-start.2 = (f32[2176,1]{0,1:T(1,128)S(1)}, f32[2176,1]{0,1:T(1,128)S(1)}, u32[]{:S(2)}, u32[]{:S(2)}) collective-permute-start(f32[2176,1]{0,1:T(1,128)S(1)} %copy.36), channel_id=1, source_target_pairs={{0,1},{1,2},{2,3},{3,4},{4,5},{5,6},{6,7},{7,8},{8,9},{9,10},{10,1... | collective-permute-start | bytes 26120 | tf_op jit(solution)/shard_map/ppermute | solution.py:23
  122.4 5.4 %collective-permute-start.3 = (f32[2176,1]{0,1:T(1,128)S(1)}, f32[2176,1]{0,1:T(1,128)S(1)}, u32[]{:S(2)}, u32[]{:S(2)}) collective-permute-start(f32[2176,1]{0,1:T(1,128)S(1)} %copy.38), channel_id=1, source_target_pairs={{1,0},{2,1},{3,2},{4,3},{5,4},{6,5},{7,6},{8,7},{9,8},{10,9},{11,1... | collective-permute-start | bytes 26120 | tf_op jit(solution)/shard_map/ppermute | solution.py:24
  125.2 4.0 %copy-start.16 = (f32[128,128]{1,0:T(8,128)S(1)}, f32[128,128]{1,0:T(8,128)}, u32[]{:S(2)}) copy-start(f32[128,128]{1,0:T(8,128)} %get-tuple-element.9) | copy-start | bytes 196612
  125.2 4.0 %copy-start.17 = (f32[128,128]{1,0:T(8,128)S(1)}, f32[128,128]{1,0:T(8,128)}, u32[]{:S(2)}) copy-start(f32[128,128]{1,0:T(8,128)} %get-tuple-element.8) | copy-start | bytes 196612
  125.2 4.0 %copy-start.23 = (f32[1,128]{1,0:T(1,128)S(1)}, f32[1,128]{1,0:T(1,128)}, u32[]{:S(2)}) copy-start(f32[1,128]{1,0:T(1,128)} %param.30) | copy-start | bytes 1540
  161.0 22.4 %all-to-all-start.3 = ((f32[32,2,128]{2,1,0:T(2,128)}), f32[32,2,128]{2,1,0:T(2,128)S(1)}, u32[]{:S(2)}, u32[]{:S(2)}) async-start(f32[32,2,128]{2,1,0:T(2,128)} %broadcast_in_dim.65), calls=%async_computation.3 | async-start | bytes 65536 | tf_op jit(solution)/shard_map/all_to_all | solution.py:156
  177.2 1.2 copy-start.4
  178.5 5.0 %copy-start.14 = (f32[128,128]{1,0:T(8,128)S(1)}, f32[128,128]{1,0:T(8,128)}, u32[]{:S(2)}) copy-start(f32[128,128]{1,0:T(8,128)} %get-tuple-element.11) | copy-start | bytes 196612
  178.5 5.0 %copy-start.15 = (f32[128,128]{1,0:T(8,128)S(1)}, f32[128,128]{1,0:T(8,128)}, u32[]{:S(2)}) copy-start(f32[128,128]{1,0:T(8,128)} %get-tuple-element.10) | copy-start | bytes 196612

commit v8 on v7

--- a/solution.py
+++ b/solution.py
@@ -35,7 +35,7 @@
     return jnp.where(lane >= step, moved, fill)
 
 
-def scan_kernel(kept_ref, charge_ref, total_ref, state_ref):
+def scan_kernel(kept_ref, charge_ref, total_ref, state_ref, ends_ref):
     kept = kept_ref[...]
     state = charge_ref[...]
     lane = lax.broadcasted_iota(jnp.int32, kept.shape, 1)
@@ -46,11 +46,16 @@
         step *= 2
     total_ref[...] = kept
     state_ref[...] = state
-
-
-def window_scan(kept, charge):
+    row = lax.broadcasted_iota(jnp.int32, ends_ref.shape, 1)
+    kept_end = jnp.broadcast_to(jnp.transpose(kept)[-1:, :][None], ends_ref.shape)
+    state_end = jnp.broadcast_to(jnp.transpose(state)[-1:, :][None], ends_ref.shape)
+    ends_ref[...] = jnp.where(row == 0, kept_end, jnp.where(row == 1, state_end, 0.0))
+
+
+def window_scan(kept, charge, copies):
     shape = jax.ShapeDtypeStruct(kept.shape, jnp.float32)
-    return pl.pallas_call(scan_kernel, out_shape=(shape, shape))(kept, charge)
+    ends = jax.ShapeDtypeStruct((copies, 8, kept.shape[0]), jnp.float32)
+    return pl.pallas_call(scan_kernel, out_shape=(shape, shape, ends))(kept, charge)
 
 
 def carried_state(kept_last, state_last, position):
@@ -150,9 +155,7 @@
         bend = padded[:, :-2] - 2.0 * dispatch + padded[:, 2:]
         dispatch_next = dispatch + dispatch_step * (balance - slope * dispatch) + ramp_local * bend
         charge = -gain_local * balance[store_rows] / math.sqrt(year_hours)
-        kept_total, local_state = window_scan(kept_local, charge)
-        ends = jnp.stack([kept_total[:, -1], local_state[:, -1]])
-        copies = jnp.broadcast_to(ends, (lax.axis_size("tm"),) + ends.shape)
+        kept_total, local_state, copies = window_scan(kept_local, charge, lax.axis_size("tm"))
         ends = lax.all_to_all(copies, "tm", split_axis=0, concat_axis=0, tiled=True)
         state_in = carried_state(ends[:, 0], ends[:, 1], position)
         charge_state = local_state + kept_total * state_in[:, None]

time: 185 us -> 182 us (0.984)
  local copies, waits for them, and re-layouts: 38.1 us -> 33.8 us
    slice x3 -> x0, local copies, waits for them, and re-layouts: 3.07 us -> none  [local(): ends = jnp.stack([kept_total[:, -1], local_state[:, -1]])]
    unnamed x54 -> x62, local copies, waits for them, and re-layouts: 5.23 us -> 5.23 us
  transfers between devices with their start and end apart: 8 -> 8, of which waited for: 4 -> 4; matrix products, arithmetic and copies ran while one was open for 22% -> 23% of each run, Pallas kernels for 0% -> 0%
where the time goes in v8:
time: 182 us; the launch traced here: 181 us
  starting transfers between devices  53.9 us (30%)
  waiting for transfers between devices  41.4 us (23%)
  local copies, waits for them, and re-layouts  33.8 us (19%)
  other arithmetic  31 us (17%)
  matrix products  15 us (8%)
  Pallas kernels  4.71 us (3%)
    all_to_all x2, waiting for transfers between devices, exchanged(): got = lax.all_to_all(sent, 'area', split_axis=0, concat_axis=0, tiled=True)  35.6 us
    all_to_all x2, starting transfers between devices, local(): ends = lax.all_to_all(copies, 'tm', split_axis=0, concat_axis=0, tiled=True)  28.2 us
    all_to_all x2, starting transfers between devices, exchanged(): got = lax.all_to_all(sent, 'area', split_axis=0, concat_axis=0, tiled=True)  14.1 us
    dot_general x2, matrix products, local(): jnp.dot(matrix, rounded, preferred_element_type=jnp.float32) + fixed_part  13.6 us
    scatter-add x2, other arithmetic, local(): jnp.zeros((bus_count, hour_count), jnp.float32).at[edge_rows].add(tie_flow)  13.3 us
    gather x2, local copies, waits for them, and re-layouts, local(): own_edge = lax.optimization_barrier(rounded[edge_rows].astype(jnp.float32))  7.25 us
    ppermute x2, starting transfers between devices, padded_2(): before = lax.ppermute(last, axis, up)  5.84 us
    ppermute x2, starting transfers between devices, padded_2(): after = lax.ppermute(leading, axis, down)  5.76 us
  transfers between devices with their start and end apart: 8, of which 4 were waited for; matrix products, arithmetic and copies ran while one was open for 23% of the time, Pallas kernels for 0%

profile of v8, /device:TPU:1, one launch (start us, length us, event | category | flops | bytes accessed | tf_op | source)
XLA Modules:
  0.0 181.0 jit_solution(5407094884551237060)
XLA Ops:
  0.7 0.9 dynamic-slice_reduce_fusion
  1.7 0.7 broadcast_clamp_fusion
  2.4 4.0 %gather_fusion = bf16[1024,128]{1,0:T(8,128)(2,1)S(1)} fusion(bf16[2176,128]{1,0:T(8,128)(2,1)} %bitcast.1247, s32[1024]{0:T(1024)S(1)} %broadcast_clamp_fusion), kind=kCustom, calls=%fused_computation | custom fusion | bytes 528384 | tf_op jit(solution)/shard_map/gather | solution.py:139
  7.3 2.0 %gather_fusion.1 = f32[16,264,128]{2,1,0:T(8,128)} fusion(f32[8,264,128]{2,1,0:T(8,128)S(1)} %select_maximum_fusion, s32[1024]{0:T(1024)S(1)} %pad_clamp_fusion.2), kind=kCustom, calls=%fused_computation.1 | custom fusion | bytes 4325440 | tf_op jit(solution)/shard_map/jit(_take)/gather | solution.py:123
  9.3 9.7 %all-to-all-start = ((f32[16,264,128]{2,1,0:T(8,128)}), f32[16,264,128]{2,1,0:T(8,128)}, u32[]{:S(2)}, u32[]{:S(2)}) async-start(f32[16,264,128]{2,1,0:T(8,128)} %gather_fusion.1), calls=%async_computation | async-start | bytes 4325376 | tf_op jit(solution)/shard_map/all_to_all | solution.py:124
  19.5 0.6 copy-done.2
  20.5 3.6 %collective-permute-start.1 = (f32[2176,1]{0,1:T(1,128)S(1)}, f32[2176,1]{0,1:T(1,128)S(1)}, u32[]{:S(2)}, u32[]{:S(2)}) collective-permute-start(f32[2176,1]{0,1:T(1,128)S(1)} %copy.33), channel_id=1, source_target_pairs={{1,0},{2,1},{3,2},{4,3},{5,4},{6,5},{7,6},{8,7},{9,8},{10,9},{11,1... | collective-permute-start | bytes 26120 | tf_op jit(solution)/shard_map/ppermute | solution.py:24
  24.5 2.3 %collective-permute-start = (f32[2176,1]{0,1:T(1,128)S(1)}, f32[2176,1]{0,1:T(1,128)S(1)}, u32[]{:S(2)}, u32[]{:S(2)}) collective-permute-start(f32[2176,1]{0,1:T(1,128)S(1)} %copy.31), channel_id=1, source_target_pairs={{0,1},{1,2},{2,3},{3,4},{4,5},{5,6},{6,7},{7,8},{8,9},{9,10},{10,1... | collective-permute-start | bytes 26120 | tf_op jit(solution)/shard_map/ppermute | solution.py:23
  26.9 6.6 %fusion.10 = f32[2176,128]{1,0:T(8,128)S(1)} fusion(bf16[1,2176,2176]{2,1,0:T(8,128)(2,1)} %param.20, bf16[1,2176,128]{2,1,0:T(8,128)(2,1)} %param.17, bf16[1,2176,128]{2,1,0:T(8,128)(2,1)} %param.18, bf16[1,2176,128]{2,1,0:T(8,128)(2,1)S(1)} %copy-done.1), kind=kOutput, calls=%fused_computation.17 | convolution fusion | flops 1213267968 | bytes 12255232 | tf_op jit(solution)/shard_map/dot_general | solution.py:153
  33.6 1.4 copy.32
  35.0 1.4 copy.34
  36.4 32.1 %all-to-all-done = f32[16,264,128]{2,1,0:T(8,128)} async-done(((f32[16,264,128]{2,1,0:T(8,128)}), f32[16,264,128]{2,1,0:T(8,128)}, u32[]{:S(2)}, u32[]{:S(2)}) %all-to-all-start) | async-done | bytes 2162720 | tf_op jit(solution)/shard_map/all_to_all | solution.py:124
  68.5 2.2 %gather_fusion.2 = f32[8,264,128]{2,1,0:T(8,128)S(1)} fusion(f32[16,264,128]{2,1,0:T(8,128)} %all-to-all-done, s32[1024]{0:T(1024)S(1)} %pad_clamp_fusion.1), kind=kCustom, calls=%fused_computation.2 | custom fusion | bytes 2162720 | tf_op jit(solution)/shard_map/jit(_take)/gather | solution.py:125
  71.0 0.9 copy-done.10
  73.0 6.4 %scatter_fusion = f32[2176,128]{1,0:T(8,128)S(1)} fusion(f32[2176,128]{1,0:T(8,128)S(1)} %fusion.10, s32[1024]{0:T(1024)S(1)} %fusion.44, f32[1024,128]{1,0:T(8,128)S(1)} %bitcast.1256), kind=kCustom, calls=%fused_computation.8 | custom fusion | flops 131072 | bytes 1576960 | tf_op jit(solution)/shard_map/scatter-add | solution.py:151
  79.5 0.6 gather_fusion.3
  80.1 0.7 multiply_multiply_fusion.1.charge_ref
  80.8 2.4 %shard_map.183 = (f32[128,128]{1,0:T(8,128)}, f32[128,128]{1,0:T(8,128)}, f32[32,8,128]{2,1,0:T(8,128)}) custom-call(f32[128,128]{1,0:T(8,128)} %bitcast.1259, f32[128,128]{1,0:T(8,128)} %multiply_multiply_fusion.1.charge_ref), custom_call_target="tpu_custom_call" | custom-call | tf_op jit(solution)/shard_map/pallas_call | solution.py:58
  83.2 15.5 %all-to-all-start.1 = ((f32[32,8,128]{2,1,0:T(8,128)}), f32[32,8,128]{2,1,0:T(8,128)S(1)}, u32[]{:S(2)}, u32[]{:S(2)}) async-start(f32[32,8,128]{2,1,0:T(8,128)} %get-tuple-element.12), calls=%async_computation.1 | async-start | bytes 262144 | tf_op jit(solution)/shard_map/all_to_all | solution.py:159
  98.7 3.7 %fusion.21 = (f32[2176,128]{1,0:T(8,128)S(1)}, bf16[2176,128]{1,0:T(8,128)(2,1)S(1)}) fusion(f32[2176,1]{1,0:T(8,128)} %copy.34, f32[2176,128]{1,0:T(8,128)} %copy-done.2, f32[2176,1]{1,0:T(8,128)} %copy.32, f32[2176,128]{1,0:T(8,128)S(1)} %scatter_fusion, bf16[1,2176,128]{2,1,0:T(8,128)(2,1)} %param.17, f32[2176]{0:T(1024)S(1)} %reduce.2, f32[2176]{0:T(1024)S(1)} %reduce.1), kind=kLoop, calls=%fused_computation.31 | loop fusion | flops 3620864 | bytes 4491264 | tf_op jit(solution)/shard_map/add | solution.py:156
  102.4 1.1 fusion.26
  103.5 1.0 copy-done.3
  104.6 3.2 %gather_fusion.4 = bf16[1024,128]{1,0:T(8,128)(2,1)S(1)} fusion(bf16[2176,128]{1,0:T(8,128)(2,1)S(1)} %fusion.23, s32[1024]{0:T(1024)S(1)} %broadcast_clamp_fusion), kind=kCustom, calls=%fused_computation.4 | custom fusion | bytes 528384 | tf_op jit(solution)/shard_map/gather | solution.py:139
  107.9 1.6 gather_fusion.5
  109.5 4.4 %all-to-all-start.2 = ((f32[16,128,128]{2,1,0:T(8,128)}), f32[16,128,128]{2,1,0:T(8,128)}, u32[]{:S(2)}, u32[]{:S(2)}) async-start(f32[16,128,128]{2,1,0:T(8,128)} %gather_fusion.5), calls=%async_computation.2 | async-start | bytes 2097152 | tf_op jit(solution)/shard_map/all_to_all | solution.py:124
  113.8 1.3 fusion.173
  115.2 1.6 copy.35
  116.8 3.6 %collective-permute-start.2 = (f32[2176,1]{0,1:T(1,128)S(1)}, f32[2176,1]{0,1:T(1,128)S(1)}, u32[]{:S(2)}, u32[]{:S(2)}) collective-permute-start(f32[2176,1]{0,1:T(1,128)S(1)} %copy.35), channel_id=1, source_target_pairs={{0,1},{1,2},{2,3},{3,4},{4,5},{5,6},{6,7},{7,8},{8,9},{9,10},{10,1... | collective-permute-start | bytes 26120 | tf_op jit(solution)/shard_map/ppermute | solution.py:23
  120.7 2.1 %collective-permute-start.3 = (f32[2176,1]{0,1:T(1,128)S(1)}, f32[2176,1]{0,1:T(1,128)S(1)}, u32[]{:S(2)}, u32[]{:S(2)}) collective-permute-start(f32[2176,1]{0,1:T(1,128)S(1)} %copy.37), channel_id=1, source_target_pairs={{1,0},{2,1},{3,2},{4,3},{5,4},{6,5},{7,6},{8,7},{9,8},{10,9},{11,1... | collective-permute-start | bytes 26120 | tf_op jit(solution)/shard_map/ppermute | solution.py:24
  122.9 0.7 slice.911
  123.6 1.4 copy.36
  125.0 1.1 collective-permute-done.3
  126.1 1.4 copy.38
  127.6 2.2 %scatter_custom_fusion.1 = f32[2176,128]{1,0:T(8,128)} fusion(s32[128]{0:T(128)} %copy-done.27, f32[]{:T(128)} %constant.42.clone.1, f32[128,128]{1,0:T(8,128)S(1)} %copy-done.17, f32[128,128]{1,0:T(8,128)S(1)} %copy-done.16, f32[128]{0:T(128)S(1)} %broadcast_select_fusion.63, f32[128]{0:T(128)S(1)} %bitcast.1265), kind=kCustom, calls=%fused_computation.53 | custom fusion | flops 65536 | bytes 1246720 | tf_op jit(solution)/shard_map/scatter-add | solution.py:165
  129.8 7.0 %fusion.7 = f32[2176,128]{1,0:T(8,128)S(1)} fusion(bf16[2176,128]{1,0:T(8,128)(2,1)} %bitcast.1252, bf16[1,2176,2176]{2,1,0:T(8,128)(2,1)} %param.20, f32[2176,128]{1,0:T(8,128)} %scatter_custom_fusion.1, f32[2176,128]{1,0:T(8,128)S(1)} %get-tuple-element.33, bf16[1,2176,128]{2,1,0:T(8,128)(2,1)} %param.18), kind=kOutput, calls=%fused_computation.16 | convolution fusion | flops 1213267968 | bytes 13926400 | tf_op jit(solution)/shard_map/dot_general | solution.py:153
  136.8 3.5 %all-to-all-done.2 = f32[16,128,128]{2,1,0:T(8,128)} async-done(((f32[16,128,128]{2,1,0:T(8,128)}), f32[16,128,128]{2,1,0:T(8,128)}, u32[]{:S(2)}, u32[]{:S(2)}) %all-to-all-start.2) | async-done | bytes 1048608 | tf_op jit(solution)/shard_map/all_to_all | solution.py:124
  140.3 2.6 %gather_fusion.6 = f32[8,128,128]{2,1,0:T(8,128)} fusion(f32[16,128,128]{2,1,0:T(8,128)} %all-to-all-done.2, s32[1024]{0:T(1024)S(1)} %pad_clamp_fusion.1), kind=kCustom, calls=%fused_computation.6 | custom fusion | bytes 1048608 | tf_op jit(solution)/shard_map/jit(_take)/gather | solution.py:125
  142.9 3.2 %add_bitcast_fusion = (f32[1,8,128,128]{3,2,1,0:T(8,128)}, f32[8,128,128]{2,1,0:T(8,128)}) fusion(bf16[1,8,128,128]{3,2,1,0:T(8,128)(2,1)} %param.19, f32[8,128]{1,0:T(8,128)S(1)} %bitcast.1262, f32[8,128,128]{2,1,0:T(8,128)} %copy-done.5, f32[8,128,128]{2,1,0:T(8,128)} %gather_fusion.6, f32[8,128,128]{2,1,0:T(8,128)} %copy-done.6, ...), kind=kLoop, calls=%fused_computation.66 | loop fusion | flops 1703936 | bytes 3944448 | tf_op jit(solution)/shard_map/broadcast_in_dim | solution.py:177
  146.1 6.8 %scatter_fusion.1 = f32[2176,128]{1,0:T(8,128)S(1)} fusion(f32[2176,128]{1,0:T(8,128)S(1)} %fusion.7, s32[1024]{0:T(1024)S(1)} %fusion.44, f32[1024,128]{1,0:T(8,128)} %bitcast.1255), kind=kCustom, calls=%fused_computation.10 | custom fusion | flops 131072 | bytes 1576960 | tf_op jit(solution)/shard_map/scatter-add | solution.py:151
  153.0 0.8 gather_fusion.7
  153.7 0.7 multiply_multiply_fusion.charge_ref
  154.4 2.4 %shard_map.184 = (f32[128,128]{1,0:T(8,128)}, f32[128,128]{1,0:T(8,128)}, f32[32,8,128]{2,1,0:T(8,128)}) custom-call(f32[128,128]{1,0:T(8,128)} %bitcast.1260, f32[128,128]{1,0:T(8,128)} %multiply_multiply_fusion.charge_ref), custom_call_target="tpu_custom_call" | custom-call | tf_op jit(solution)/shard_map/pallas_call | solution.py:58
  156.8 12.7 %all-to-all-start.3 = ((f32[32,8,128]{2,1,0:T(8,128)}), f32[32,8,128]{2,1,0:T(8,128)S(1)}, u32[]{:S(2)}, u32[]{:S(2)}) async-start(f32[32,8,128]{2,1,0:T(8,128)} %get-tuple-element.15), calls=%async_computation.3 | async-start | bytes 262144 | tf_op jit(solution)/shard_map/all_to_all | solution.py:159
  169.5 3.6 %fusion.33 = (bf16[1,2176,128]{2,1,0:T(8,128)(2,1)}, bf16[2176,128]{1,0:T(8,128)(2,1)S(1)}) fusion(f32[2176,1]{1,0:T(8,128)} %copy.38, f32[2176,128]{1,0:T(8,128)S(1)} %get-tuple-element.33, f32[2176,1]{1,0:T(8,128)} %copy.36, f32[2176]{0:T(1024)S(1)} %reduce.2, f32[2176,128]{1,0:T(8,128)S(1)} %scatter_fusion.1, f32[2176]{0:T(1024)S(1)} %reduce.1), kind=kLoop, calls=%fused_computation.55 | loop fusion | flops 3620864 | bytes 3377152 | tf_op jit(solution)/shard_map/broadcast_in_dim | solution.py:176
  173.4 0.9 copy-done.4
  174.3 1.1 bitcast_subtract_fusion
  175.5 4.7 %all-to-all-done.3 = f32[32,8,128]{2,1,0:T(8,128)S(1)} async-done(((f32[32,8,128]{2,1,0:T(8,128)}), f32[32,8,128]{2,1,0:T(8,128)S(1)}, u32[]{:S(2)}, u32[]{:S(2)}) %all-to-all-start.3) | async-done | bytes 131104 | tf_op jit(solution)/shard_map/all_to_all | solution.py:159
  180.3 0.7 add_bitcast_fusion.1
  (85 shorter events, 4.4 us)
Async XLA Ops:
  0.6 101.7 %copy-start = (bf16[1,34,64,64]{3,2,1,0:T(8,128)(2,1)S(1)}, bf16[1,34,64,64]{3,2,1,0:T(8,128)(2,1)}, u32[]{:S(2)}) copy-start(bf16[1,34,64,64]{3,2,1,0:T(8,128)(2,1)} %param.21) | copy-start | bytes 835588
  2.4 4.1 %copy-start.11 = (bf16[1,8,128,128]{3,2,1,0:T(8,128)(2,1)S(1)}, bf16[1,8,128,128]{3,2,1,0:T(8,128)(2,1)}, u32[]{:S(2)}) copy-start(bf16[1,8,128,128]{3,2,1,0:T(8,128)(2,1)} %param.19) | copy-start | bytes 786436
  6.4 0.7 copy-start.18
  6.5 0.8 copy-start.6
  9.3 9.8 %copy-start.13 = (bf16[1,2176,128]{2,1,0:T(8,128)(2,1)S(1)}, bf16[1,2176,128]{2,1,0:T(8,128)(2,1)}, u32[]{:S(2)}) copy-start(bf16[1,2176,128]{2,1,0:T(8,128)(2,1)} %param.17) | copy-start | bytes 1671172
  9.3 59.2 %all-to-all-start = ((f32[16,264,128]{2,1,0:T(8,128)}), f32[16,264,128]{2,1,0:T(8,128)}, u32[]{:S(2)}, u32[]{:S(2)}) async-start(f32[16,264,128]{2,1,0:T(8,128)} %gather_fusion.1), calls=%async_computation | async-start | bytes 4325376 | tf_op jit(solution)/shard_map/all_to_all | solution.py:124
  19.2 1.0 copy-start.2
  20.2 6.6 %copy-start.28 = (s32[1,128]{1,0:T(1,128)S(1)}, s32[1,128]{1,0:T(1,128)}, u32[]{:S(2)}) copy-start(s32[1,128]{1,0:T(1,128)} %param.28) | copy-start | bytes 1540
  20.2 6.7 %copy-start.29 = (f32[1,128]{1,0:T(1,128)S(1)}, f32[1,128]{1,0:T(1,128)}, u32[]{:S(2)}) copy-start(f32[1,128]{1,0:T(1,128)} %param.29) | copy-start | bytes 1540
  20.2 6.7 %copy-start.20 = (s32[1,8,128]{2,1,0:T(8,128)S(1)}, s32[1,8,128]{2,1,0:T(8,128)}, u32[]{:S(2)}) copy-start(s32[1,8,128]{2,1,0:T(8,128)} %param.25) | copy-start | bytes 12292
  20.2 6.7 %copy-start.1 = (bf16[1,2176,128]{2,1,0:T(8,128)(2,1)S(1)}, bf16[1,2176,128]{2,1,0:T(8,128)(2,1)}, u32[]{:S(2)}) copy-start(bf16[1,2176,128]{2,1,0:T(8,128)(2,1)} %param.16) | copy-start | bytes 1671172
  20.5 14.5 %collective-permute-start.1 = (f32[2176,1]{0,1:T(1,128)S(1)}, f32[2176,1]{0,1:T(1,128)S(1)}, u32[]{:S(2)}, u32[]{:S(2)}) collective-permute-start(f32[2176,1]{0,1:T(1,128)S(1)} %copy.33), channel_id=1, source_target_pairs={{1,0},{2,1},{3,2},{4,3},{5,4},{6,5},{7,6},{8,7},{9,8},{10,9},{11,1... | collective-permute-start | bytes 26120 | tf_op jit(solution)/shard_map/ppermute | solution.py:24
  24.5 9.1 %collective-permute-start = (f32[2176,1]{0,1:T(1,128)S(1)}, f32[2176,1]{0,1:T(1,128)S(1)}, u32[]{:S(2)}, u32[]{:S(2)}) collective-permute-start(f32[2176,1]{0,1:T(1,128)S(1)} %copy.31), channel_id=1, source_target_pairs={{0,1},{1,2},{2,3},{3,4},{4,5},{5,6},{6,7},{7,8},{8,9},{9,10},{10,1... | collective-permute-start | bytes 26120 | tf_op jit(solution)/shard_map/ppermute | solution.py:23
  26.8 6.7 %copy-start.27 = (s32[128]{0:T(128)}, s32[128]{0:T(128)S(1)}, u32[]{:S(2)}) copy-start(s32[128]{0:T(128)S(1)} %fusion.47) | copy-start | bytes 1540
  26.9 53.2 %copy-start.24 = (f32[128]{0:T(128)}, f32[128]{0:T(128)S(1)}, u32[]{:S(2)}) copy-start(f32[128]{0:T(128)S(1)} %negate_bitcast_fusion) | copy-start | bytes 1540
  26.9 6.6 %copy-start.21 = (f32[1,2176]{1,0:T(1,128)S(1)}, f32[1,2176]{1,0:T(1,128)}, u32[]{:S(2)}) copy-start(f32[1,2176]{1,0:T(1,128)} %param.22) | copy-start | bytes 26116
  26.9 6.7 %copy-start.22 = (f32[1,2176]{1,0:T(1,128)S(1)}, f32[1,2176]{1,0:T(1,128)}, u32[]{:S(2)}) copy-start(f32[1,2176]{1,0:T(1,128)} %param.23) | copy-start | bytes 26116
  33.5 45.9 %copy-start.23 = (s32[1024]{0:T(1024)}, s32[1024]{0:T(1024)S(1)}, u32[]{:S(2)}) copy-start(s32[1024]{0:T(1024)S(1)} %pad_clamp_fusion) | copy-start | bytes 12292
  71.0 1.0 copy-start.10
  71.0 1.4 copy-start.7
  71.0 1.5 copy-start.12
  71.0 1.5 copy-start.19
  72.0 0.8 copy-start.8
  72.0 1.0 copy-start.9
  83.2 26.3 %all-to-all-start.1 = ((f32[32,8,128]{2,1,0:T(8,128)}), f32[32,8,128]{2,1,0:T(8,128)S(1)}, u32[]{:S(2)}, u32[]{:S(2)}) async-start(f32[32,8,128]{2,1,0:T(8,128)} %get-tuple-element.12), calls=%async_computation.1 | async-start | bytes 262144 | tf_op jit(solution)/shard_map/all_to_all | solution.py:159
  103.5 1.0 copy-start.3
  107.9 1.6 copy-start.5
  109.5 30.9 %all-to-all-start.2 = ((f32[16,128,128]{2,1,0:T(8,128)}), f32[16,128,128]{2,1,0:T(8,128)}, u32[]{:S(2)}, u32[]{:S(2)}) async-start(f32[16,128,128]{2,1,0:T(8,128)} %gather_fusion.5), calls=%async_computation.2 | async-start | bytes 2097152 | tf_op jit(solution)/shard_map/all_to_all | solution.py:124
  116.8 6.8 %collective-permute-start.2 = (f32[2176,1]{0,1:T(1,128)S(1)}, f32[2176,1]{0,1:T(1,128)S(1)}, u32[]{:S(2)}, u32[]{:S(2)}) collective-permute-start(f32[2176,1]{0,1:T(1,128)S(1)} %copy.35), channel_id=1, source_target_pairs={{0,1},{1,2},{2,3},{3,4},{4,5},{5,6},{6,7},{7,8},{8,9},{9,10},{10,1... | collective-permute-start | bytes 26120 | tf_op jit(solution)/shard_map/ppermute | solution.py:23
  120.7 5.4 %collective-permute-start.3 = (f32[2176,1]{0,1:T(1,128)S(1)}, f32[2176,1]{0,1:T(1,128)S(1)}, u32[]{:S(2)}, u32[]{:S(2)}) collective-permute-start(f32[2176,1]{0,1:T(1,128)S(1)} %copy.37), channel_id=1, source_target_pairs={{1,0},{2,1},{3,2},{4,3},{5,4},{6,5},{7,6},{8,7},{9,8},{10,9},{11,1... | collective-permute-start | bytes 26120 | tf_op jit(solution)/shard_map/ppermute | solution.py:24
  123.5 4.0 %copy-start.16 = (f32[128,128]{1,0:T(8,128)S(1)}, f32[128,128]{1,0:T(8,128)}, u32[]{:S(2)}) copy-start(f32[128,128]{1,0:T(8,128)} %get-tuple-element.11) | copy-start | bytes 196612
  123.6 4.0 %copy-start.17 = (f32[128,128]{1,0:T(8,128)S(1)}, f32[128,128]{1,0:T(8,128)}, u32[]{:S(2)}) copy-start(f32[128,128]{1,0:T(8,128)} %get-tuple-element.10) | copy-start | bytes 196612
  123.6 4.0 %copy-start.26 = (f32[1,128]{1,0:T(1,128)S(1)}, f32[1,128]{1,0:T(1,128)}, u32[]{:S(2)}) copy-start(f32[1,128]{1,0:T(1,128)} %param.30) | copy-start | bytes 1540
  146.1 7.6 %copy-start.25 = (f32[128]{0:T(128)S(1)}, f32[128]{0:T(128)}, u32[]{:S(2)}) copy-start(f32[128]{0:T(128)} %copy-done.24) | copy-start | bytes 1540
  156.8 23.3 %all-to-all-start.3 = ((f32[32,8,128]{2,1,0:T(8,128)}), f32[32,8,128]{2,1,0:T(8,128)S(1)}, u32[]{:S(2)}, u32[]{:S(2)}) async-start(f32[32,8,128]{2,1,0:T(8,128)} %get-tuple-element.15), calls=%async_computation.3 | async-start | bytes 262144 | tf_op jit(solution)/shard_map/all_to_all | solution.py:159
  173.1 1.2 copy-start.4
  174.3 5.9 %copy-start.14 = (f32[128,128]{1,0:T(8,128)S(1)}, f32[128,128]{1,0:T(8,128)}, u32[]{:S(2)}) copy-start(f32[128,128]{1,0:T(8,128)} %get-tuple-element.14) | copy-start | bytes 196612
  174.3 5.9 %copy-start.15 = (f32[128,128]{1,0:T(8,128)S(1)}, f32[128,128]{1,0:T(8,128)}, u32[]{:S(2)}) copy-start(f32[128,128]{1,0:T(8,128)} %get-tuple-element.13) | copy-start | bytes 196612

commit v9 on v8

--- a/solution.py
+++ b/solution.py
@@ -136,7 +136,7 @@
     mismatch = None
     for iteration in range(ITERS):
         rounded = angle_now.astype(jnp.bfloat16)
-        own_edge = lax.optimization_barrier(rounded[edge_rows].astype(jnp.float32))
+        own_edge = lax.optimization_barrier(rounded.astype(jnp.float32)[edge_rows])
         if iteration == 0:
             far_edge, price_far, penalty_far = exchanged(
                 (own_edge, price_now, tie_penalty[0]),

time: 182 us -> 183 us (level)
    unnamed x62 -> x58, local copies, waits for them, and re-layouts: 5.23 us -> 4.61 us
  transfers between devices with their start and end apart: 8 -> 8, of which waited for: 4 -> 4; matrix products, arithmetic and copies ran while one was open for 23% -> 24% of each run, Pallas kernels for 0% -> 0%
where the time goes in v9:
time: 183 us; the launch traced here: 182 us
  starting transfers between devices  53.9 us (29%)
  waiting for transfers between devices  41.4 us (23%)
  local copies, waits for them, and re-layouts  33.9 us (19%)
  other arithmetic  32 us (17%)
  matrix products  15 us (8%)
  Pallas kernels  4.71 us (3%)
    all_to_all x2, waiting for transfers between devices, exchanged(): got = lax.all_to_all(sent, 'area', split_axis=0, concat_axis=0, tiled=True)  35.6 us
    all_to_all x2, starting transfers between devices, local(): ends = lax.all_to_all(copies, 'tm', split_axis=0, concat_axis=0, tiled=True)  28.2 us
    all_to_all x2, starting transfers between devices, exchanged(): got = lax.all_to_all(sent, 'area', split_axis=0, concat_axis=0, tiled=True)  14.1 us
    dot_general x2, matrix products, local(): jnp.dot(matrix, rounded, preferred_element_type=jnp.float32) + fixed_part  13.6 us
    scatter-add x2, other arithmetic, local(): jnp.zeros((bus_count, hour_count), jnp.float32).at[edge_rows].add(tie_flow)  13.3 us
    gather x2, local copies, waits for them, and re-layouts, local(): own_edge = lax.optimization_barrier(rounded.astype(jnp.float32)[edge_rows])  6.81 us
    ppermute x2, starting transfers between devices, padded_2(): before = lax.ppermute(last, axis, up)  5.83 us
    ppermute x2, starting transfers between devices, padded_2(): after = lax.ppermute(leading, axis, down)  5.76 us
  transfers between devices with their start and end apart: 8, of which 4 were waited for; matrix products, arithmetic and copies ran while one was open for 24% of the time, Pallas kernels for 0%

profile of v9, /device:TPU:1, one launch (start us, length us, event | category | flops | bytes accessed | tf_op | source)
XLA Modules:
  0.0 181.9 jit_solution(4888839470921807794)
XLA Ops:
  0.7 1.0 dynamic-slice_reduce_fusion
  1.7 0.7 broadcast_clamp_fusion
  2.4 1.0 bitcast_convert_fusion.2
  3.5 2.8 %gather_fusion = f32[1024,128]{1,0:T(8,128)S(1)} fusion(f32[2176,128]{1,0:T(8,128)S(1)} %bitcast_convert_fusion.1, s32[1024]{0:T(1024)S(1)} %broadcast_clamp_fusion), kind=kCustom, calls=%fused_computation | custom fusion | bytes 1052672 | tf_op jit(solution)/shard_map/gather | solution.py:139
  6.4 2.1 %gather_fusion.1 = f32[16,264,128]{2,1,0:T(8,128)} fusion(f32[8,264,128]{2,1,0:T(8,128)S(1)} %select_maximum_fusion, s32[1024]{0:T(1024)S(1)} %pad_clamp_fusion.2), kind=kCustom, calls=%fused_computation.1 | custom fusion | bytes 4325440 | tf_op jit(solution)/shard_map/jit(_take)/gather | solution.py:123
  8.5 9.7 %all-to-all-start = ((f32[16,264,128]{2,1,0:T(8,128)}), f32[16,264,128]{2,1,0:T(8,128)}, u32[]{:S(2)}, u32[]{:S(2)}) async-start(f32[16,264,128]{2,1,0:T(8,128)} %gather_fusion.1), calls=%async_computation | async-start | bytes 4325376 | tf_op jit(solution)/shard_map/all_to_all | solution.py:124
  18.7 0.6 copy-done.1
  19.7 3.6 %collective-permute-start.1 = (f32[2176,1]{0,1:T(1,128)S(1)}, f32[2176,1]{0,1:T(1,128)S(1)}, u32[]{:S(2)}, u32[]{:S(2)}) collective-permute-start(f32[2176,1]{0,1:T(1,128)S(1)} %copy.33), channel_id=1, source_target_pairs={{1,0},{2,1},{3,2},{4,3},{5,4},{6,5},{7,6},{8,7},{9,8},{10,9},{11,1... | collective-permute-start | bytes 26120 | tf_op jit(solution)/shard_map/ppermute | solution.py:24
  23.7 2.3 %collective-permute-start = (f32[2176,1]{0,1:T(1,128)S(1)}, f32[2176,1]{0,1:T(1,128)S(1)}, u32[]{:S(2)}, u32[]{:S(2)}) collective-permute-start(f32[2176,1]{0,1:T(1,128)S(1)} %copy.31), channel_id=1, source_target_pairs={{0,1},{1,2},{2,3},{3,4},{4,5},{5,6},{6,7},{7,8},{8,9},{9,10},{10,1... | collective-permute-start | bytes 26120 | tf_op jit(solution)/shard_map/ppermute | solution.py:23
  26.1 6.6 %fusion.10 = f32[2176,128]{1,0:T(8,128)S(1)} fusion(bf16[1,2176,2176]{2,1,0:T(8,128)(2,1)} %param.20, bf16[1,2176,128]{2,1,0:T(8,128)(2,1)} %param.17, bf16[1,2176,128]{2,1,0:T(8,128)(2,1)} %param.18, bf16[1,2176,128]{2,1,0:T(8,128)(2,1)S(1)} %copy-done.4), kind=kOutput, calls=%fused_computation.17 | convolution fusion | flops 1213267968 | bytes 12255232 | tf_op jit(solution)/shard_map/dot_general | solution.py:153
  32.8 1.4 copy.32
  34.2 1.4 copy.34
  35.6 32.1 %all-to-all-done = f32[16,264,128]{2,1,0:T(8,128)} async-done(((f32[16,264,128]{2,1,0:T(8,128)}), f32[16,264,128]{2,1,0:T(8,128)}, u32[]{:S(2)}, u32[]{:S(2)}) %all-to-all-start) | async-done | bytes 2162720 | tf_op jit(solution)/shard_map/all_to_all | solution.py:124
  67.7 2.2 %gather_fusion.2 = f32[8,264,128]{2,1,0:T(8,128)S(1)} fusion(f32[16,264,128]{2,1,0:T(8,128)} %all-to-all-done, s32[1024]{0:T(1024)S(1)} %pad_clamp_fusion.1), kind=kCustom, calls=%fused_computation.2 | custom fusion | bytes 2162720 | tf_op jit(solution)/shard_map/jit(_take)/gather | solution.py:125
  70.2 1.0 copy-done.9
  72.2 6.4 %scatter_fusion = f32[2176,128]{1,0:T(8,128)S(1)} fusion(f32[2176,128]{1,0:T(8,128)S(1)} %fusion.10, s32[1024]{0:T(1024)S(1)} %fusion.46, f32[1024,128]{1,0:T(8,128)S(1)} %bitcast.1262), kind=kCustom, calls=%fused_computation.8 | custom fusion | flops 131072 | bytes 1576960 | tf_op jit(solution)/shard_map/scatter-add | solution.py:151
  79.3 0.7 multiply_multiply_fusion.1.charge_ref
  80.0 2.4 %shard_map.183 = (f32[128,128]{1,0:T(8,128)}, f32[128,128]{1,0:T(8,128)}, f32[32,8,128]{2,1,0:T(8,128)}) custom-call(f32[128,128]{1,0:T(8,128)} %bitcast.1263, f32[128,128]{1,0:T(8,128)} %multiply_multiply_fusion.1.charge_ref), custom_call_target="tpu_custom_call" | custom-call | tf_op jit(solution)/shard_map/pallas_call | solution.py:58
  82.4 15.5 %all-to-all-start.1 = ((f32[32,8,128]{2,1,0:T(8,128)}), f32[32,8,128]{2,1,0:T(8,128)S(1)}, u32[]{:S(2)}, u32[]{:S(2)}) async-start(f32[32,8,128]{2,1,0:T(8,128)} %get-tuple-element.12), calls=%async_computation.1 | async-start | bytes 262144 | tf_op jit(solution)/shard_map/all_to_all | solution.py:159
  97.8 3.7 %fusion.21 = (f32[2176,128]{1,0:T(8,128)S(1)}, bf16[2176,128]{1,0:T(8,128)(2,1)S(1)}) fusion(f32[2176,1]{1,0:T(8,128)} %copy.34, f32[2176,128]{1,0:T(8,128)} %copy-done.1, f32[2176,1]{1,0:T(8,128)} %copy.32, f32[2176,128]{1,0:T(8,128)S(1)} %scatter_fusion, bf16[1,2176,128]{2,1,0:T(8,128)(2,1)} %param.17, f32[2176]{0:T(1024)S(1)} %reduce.2, f32[2176]{0:T(1024)S(1)} %reduce.1), kind=kLoop, calls=%fused_computation.31 | loop fusion | flops 3620864 | bytes 4491264 | tf_op jit(solution)/shard_map/add | solution.py:156
  101.6 1.1 fusion.26
  102.7 1.0 copy-done.2
  103.8 4.0 %gather_fusion.4 = f32[1024,128]{1,0:T(8,128)} fusion(f32[2176,128]{1,0:T(8,128)S(1)} %fusion.27, s32[1024]{0:T(1024)S(1)} %broadcast_clamp_fusion), kind=kCustom, calls=%fused_computation.4 | custom fusion | bytes 1052672 | tf_op jit(solution)/shard_map/gather | solution.py:139
  107.8 2.6 %gather_fusion.5 = f32[16,128,128]{2,1,0:T(8,128)} fusion(f32[8,128,128]{2,1,0:T(8,128)} %bitcast.1250, s32[1024]{0:T(1024)S(1)} %pad_clamp_fusion.2), kind=kCustom, calls=%fused_computation.5 | custom fusion | bytes 2097216 | tf_op jit(solution)/shard_map/jit(_take)/gather | solution.py:123
  110.4 4.3 %all-to-all-start.2 = ((f32[16,128,128]{2,1,0:T(8,128)}), f32[16,128,128]{2,1,0:T(8,128)}, u32[]{:S(2)}, u32[]{:S(2)}) async-start(f32[16,128,128]{2,1,0:T(8,128)} %gather_fusion.5), calls=%async_computation.2 | async-start | bytes 2097152 | tf_op jit(solution)/shard_map/all_to_all | solution.py:124
  114.8 1.3 fusion.174
  116.1 1.6 copy.35
  117.7 3.6 %collective-permute-start.2 = (f32[2176,1]{0,1:T(1,128)S(1)}, f32[2176,1]{0,1:T(1,128)S(1)}, u32[]{:S(2)}, u32[]{:S(2)}) collective-permute-start(f32[2176,1]{0,1:T(1,128)S(1)} %copy.35), channel_id=1, source_target_pairs={{0,1},{1,2},{2,3},{3,4},{4,5},{5,6},{6,7},{7,8},{8,9},{9,10},{10,1... | collective-permute-start | bytes 26120 | tf_op jit(solution)/shard_map/ppermute | solution.py:23
  121.6 2.1 %collective-permute-start.3 = (f32[2176,1]{0,1:T(1,128)S(1)}, f32[2176,1]{0,1:T(1,128)S(1)}, u32[]{:S(2)}, u32[]{:S(2)}) collective-permute-start(f32[2176,1]{0,1:T(1,128)S(1)} %copy.37), channel_id=1, source_target_pairs={{1,0},{2,1},{3,2},{4,3},{5,4},{6,5},{7,6},{8,7},{9,8},{10,9},{11,1... | collective-permute-start | bytes 26120 | tf_op jit(solution)/shard_map/ppermute | solution.py:24
  123.8 0.7 slice.911
  124.5 1.4 copy.36
  125.9 1.1 collective-permute-done.3
  127.0 1.4 copy.38
  128.5 2.3 %scatter_custom_fusion.1 = f32[2176,128]{1,0:T(8,128)} fusion(s32[128]{0:T(128)} %copy-done.25, f32[]{:T(128)} %constant.42.clone.1, f32[128,128]{1,0:T(8,128)S(1)} %copy-done.15, f32[128,128]{1,0:T(8,128)S(1)} %copy-done.14, f32[128]{0:T(128)S(1)} %broadcast_select_fusion.63, f32[128]{0:T(128)S(1)} %bitcast.1269), kind=kCustom, calls=%fused_computation.56 | custom fusion | flops 65536 | bytes 1246720 | tf_op jit(solution)/shard_map/scatter-add | solution.py:165
  130.8 7.0 %fusion.7 = f32[2176,128]{1,0:T(8,128)S(1)} fusion(bf16[2176,128]{1,0:T(8,128)(2,1)} %bitcast.1258, bf16[1,2176,2176]{2,1,0:T(8,128)(2,1)} %param.20, f32[2176,128]{1,0:T(8,128)} %scatter_custom_fusion.1, f32[2176,128]{1,0:T(8,128)S(1)} %get-tuple-element.33, bf16[1,2176,128]{2,1,0:T(8,128)(2,1)} %param.18), kind=kOutput, calls=%fused_computation.16 | convolution fusion | flops 1213267968 | bytes 13926400 | tf_op jit(solution)/shard_map/dot_general | solution.py:153
  137.8 3.5 %all-to-all-done.2 = f32[16,128,128]{2,1,0:T(8,128)} async-done(((f32[16,128,128]{2,1,0:T(8,128)}), f32[16,128,128]{2,1,0:T(8,128)}, u32[]{:S(2)}, u32[]{:S(2)}) %all-to-all-start.2) | async-done | bytes 1048608 | tf_op jit(solution)/shard_map/all_to_all | solution.py:124
  141.3 2.6 %gather_fusion.6 = f32[8,128,128]{2,1,0:T(8,128)} fusion(f32[16,128,128]{2,1,0:T(8,128)} %all-to-all-done.2, s32[1024]{0:T(1024)S(1)} %pad_clamp_fusion.1), kind=kCustom, calls=%fused_computation.6 | custom fusion | bytes 1048608 | tf_op jit(solution)/shard_map/jit(_take)/gather | solution.py:125
  143.8 3.2 %add_bitcast_fusion = (f32[1,8,128,128]{3,2,1,0:T(8,128)}, f32[8,128,128]{2,1,0:T(8,128)}) fusion(bf16[1,8,128,128]{3,2,1,0:T(8,128)(2,1)} %param.19, f32[8,128]{1,0:T(8,128)S(1)} %bitcast.1266, f32[8,128,128]{2,1,0:T(8,128)} %bitcast.1251, f32[8,128,128]{2,1,0:T(8,128)} %gather_fusion.6, f32[8,128,128]{2,1,0:T(8,128)} %bitcast.1253, ...), kind=kLoop, calls=%fused_computation.69 | loop fusion | flops 1703936 | bytes 3944448 | tf_op jit(solution)/shard_map/broadcast_in_dim | solution.py:177
  147.0 6.8 %scatter_fusion.1 = f32[2176,128]{1,0:T(8,128)S(1)} fusion(f32[2176,128]{1,0:T(8,128)S(1)} %fusion.7, s32[1024]{0:T(1024)S(1)} %fusion.46, f32[1024,128]{1,0:T(8,128)} %bitcast.1261), kind=kCustom, calls=%fused_computation.10 | custom fusion | flops 131072 | bytes 1576960 | tf_op jit(solution)/shard_map/scatter-add | solution.py:151
  153.9 0.8 gather_fusion.7
  154.7 0.7 multiply_multiply_fusion.charge_ref
  155.4 2.4 %shard_map.184 = (f32[128,128]{1,0:T(8,128)}, f32[128,128]{1,0:T(8,128)}, f32[32,8,128]{2,1,0:T(8,128)}) custom-call(f32[128,128]{1,0:T(8,128)} %bitcast.1264, f32[128,128]{1,0:T(8,128)} %multiply_multiply_fusion.charge_ref), custom_call_target="tpu_custom_call" | custom-call | tf_op jit(solution)/shard_map/pallas_call | solution.py:58
  157.7 12.7 %all-to-all-start.3 = ((f32[32,8,128]{2,1,0:T(8,128)}), f32[32,8,128]{2,1,0:T(8,128)S(1)}, u32[]{:S(2)}, u32[]{:S(2)}) async-start(f32[32,8,128]{2,1,0:T(8,128)} %get-tuple-element.15), calls=%async_computation.3 | async-start | bytes 262144 | tf_op jit(solution)/shard_map/all_to_all | solution.py:159
  170.5 3.6 %fusion.35 = (bf16[1,2176,128]{2,1,0:T(8,128)(2,1)}, bf16[2176,128]{1,0:T(8,128)(2,1)S(1)}) fusion(f32[2176,1]{1,0:T(8,128)} %copy.38, f32[2176,128]{1,0:T(8,128)S(1)} %get-tuple-element.33, f32[2176,1]{1,0:T(8,128)} %copy.36, f32[2176]{0:T(1024)S(1)} %reduce.2, f32[2176,128]{1,0:T(8,128)S(1)} %scatter_fusion.1, f32[2176]{0:T(1024)S(1)} %reduce.1), kind=kLoop, calls=%fused_computation.58 | loop fusion | flops 3620864 | bytes 3377152 | tf_op jit(solution)/shard_map/broadcast_in_dim | solution.py:176
  174.3 1.0 copy-done.3
  175.3 1.1 bitcast_subtract_fusion
  176.4 4.7 %all-to-all-done.3 = f32[32,8,128]{2,1,0:T(8,128)S(1)} async-done(((f32[32,8,128]{2,1,0:T(8,128)}), f32[32,8,128]{2,1,0:T(8,128)S(1)}, u32[]{:S(2)}, u32[]{:S(2)}) %all-to-all-start.3) | async-done | bytes 131104 | tf_op jit(solution)/shard_map/all_to_all | solution.py:159
  181.2 0.7 add_bitcast_fusion.1
  (80 shorter events, 4.3 us)
Async XLA Ops:
  0.6 101.0 %copy-start = (bf16[1,34,64,64]{3,2,1,0:T(8,128)(2,1)S(1)}, bf16[1,34,64,64]{3,2,1,0:T(8,128)(2,1)}, u32[]{:S(2)}) copy-start(bf16[1,34,64,64]{3,2,1,0:T(8,128)(2,1)} %param.21) | copy-start | bytes 835588
  0.6 2.8 %copy-start.4 = (bf16[1,2176,128]{2,1,0:T(8,128)(2,1)S(1)}, bf16[1,2176,128]{2,1,0:T(8,128)(2,1)}, u32[]{:S(2)}) copy-start(bf16[1,2176,128]{2,1,0:T(8,128)(2,1)} %param.16) | copy-start | bytes 1671172
  3.5 2.8 %copy-start.16 = (f32[1,8,128]{2,1,0:T(8,128)S(1)}, f32[1,8,128]{2,1,0:T(8,128)}, u32[]{:S(2)}) copy-start(f32[1,8,128]{2,1,0:T(8,128)} %param.27) | copy-start | bytes 12292
  6.3 2.2 %copy-start.5 = (f32[1024,128]{1,0:T(8,128)}, f32[1024,128]{1,0:T(8,128)S(1)}, u32[]{:S(2)}) copy-start(f32[1024,128]{1,0:T(8,128)S(1)} %gather_fusion) | copy-start | bytes 1572868
  8.5 9.8 %copy-start.11 = (bf16[1,2176,128]{2,1,0:T(8,128)(2,1)S(1)}, bf16[1,2176,128]{2,1,0:T(8,128)(2,1)}, u32[]{:S(2)}) copy-start(bf16[1,2176,128]{2,1,0:T(8,128)(2,1)} %param.17) | copy-start | bytes 1671172
  8.5 59.2 %all-to-all-start = ((f32[16,264,128]{2,1,0:T(8,128)}), f32[16,264,128]{2,1,0:T(8,128)}, u32[]{:S(2)}, u32[]{:S(2)}) async-start(f32[16,264,128]{2,1,0:T(8,128)} %gather_fusion.1), calls=%async_computation | async-start | bytes 4325376 | tf_op jit(solution)/shard_map/all_to_all | solution.py:124
  18.3 1.0 copy-start.1
  19.3 6.6 %copy-start.26 = (s32[1,128]{1,0:T(1,128)S(1)}, s32[1,128]{1,0:T(1,128)}, u32[]{:S(2)}) copy-start(s32[1,128]{1,0:T(1,128)} %param.28) | copy-start | bytes 1540
  19.3 6.7 %copy-start.27 = (f32[1,128]{1,0:T(1,128)S(1)}, f32[1,128]{1,0:T(1,128)}, u32[]{:S(2)}) copy-start(f32[1,128]{1,0:T(1,128)} %param.29) | copy-start | bytes 1540
  19.3 6.7 %copy-start.18 = (s32[1,8,128]{2,1,0:T(8,128)S(1)}, s32[1,8,128]{2,1,0:T(8,128)}, u32[]{:S(2)}) copy-start(s32[1,8,128]{2,1,0:T(8,128)} %param.25) | copy-start | bytes 12292
  19.7 14.5 %collective-permute-start.1 = (f32[2176,1]{0,1:T(1,128)S(1)}, f32[2176,1]{0,1:T(1,128)S(1)}, u32[]{:S(2)}, u32[]{:S(2)}) collective-permute-start(f32[2176,1]{0,1:T(1,128)S(1)} %copy.33), channel_id=1, source_target_pairs={{1,0},{2,1},{3,2},{4,3},{5,4},{6,5},{7,6},{8,7},{9,8},{10,9},{11,1... | collective-permute-start | bytes 26120 | tf_op jit(solution)/shard_map/ppermute | solution.py:24
  23.7 9.1 %collective-permute-start = (f32[2176,1]{0,1:T(1,128)S(1)}, f32[2176,1]{0,1:T(1,128)S(1)}, u32[]{:S(2)}, u32[]{:S(2)}) collective-permute-start(f32[2176,1]{0,1:T(1,128)S(1)} %copy.31), channel_id=1, source_target_pairs={{0,1},{1,2},{2,3},{3,4},{4,5},{5,6},{6,7},{7,8},{8,9},{9,10},{10,1... | collective-permute-start | bytes 26120 | tf_op jit(solution)/shard_map/ppermute | solution.py:23
  26.0 6.7 %copy-start.25 = (s32[128]{0:T(128)}, s32[128]{0:T(128)S(1)}, u32[]{:S(2)}) copy-start(s32[128]{0:T(128)S(1)} %fusion.49) | copy-start | bytes 1540
  26.0 53.2 %copy-start.22 = (f32[128]{0:T(128)}, f32[128]{0:T(128)S(1)}, u32[]{:S(2)}) copy-start(f32[128]{0:T(128)S(1)} %negate_bitcast_fusion) | copy-start | bytes 1540
  26.1 6.6 %copy-start.19 = (f32[1,2176]{1,0:T(1,128)S(1)}, f32[1,2176]{1,0:T(1,128)}, u32[]{:S(2)}) copy-start(f32[1,2176]{1,0:T(1,128)} %param.22) | copy-start | bytes 26116
  26.1 6.7 %copy-start.20 = (f32[1,2176]{1,0:T(1,128)S(1)}, f32[1,2176]{1,0:T(1,128)}, u32[]{:S(2)}) copy-start(f32[1,2176]{1,0:T(1,128)} %param.23) | copy-start | bytes 26116
  32.7 45.9 %copy-start.21 = (s32[1024]{0:T(1024)}, s32[1024]{0:T(1024)S(1)}, u32[]{:S(2)}) copy-start(s32[1024]{0:T(1024)S(1)} %pad_clamp_fusion) | copy-start | bytes 12292
  70.1 1.0 copy-start.9
  70.1 1.4 copy-start.6
  70.2 1.5 copy-start.10
  70.2 1.5 copy-start.17
  71.2 0.8 copy-start.7
  71.2 1.0 copy-start.8
  82.4 28.1 %all-to-all-start.1 = ((f32[32,8,128]{2,1,0:T(8,128)}), f32[32,8,128]{2,1,0:T(8,128)S(1)}, u32[]{:S(2)}, u32[]{:S(2)}) async-start(f32[32,8,128]{2,1,0:T(8,128)} %get-tuple-element.12), calls=%async_computation.1 | async-start | bytes 262144 | tf_op jit(solution)/shard_map/all_to_all | solution.py:159
  102.7 1.0 copy-start.2
  110.4 30.8 %all-to-all-start.2 = ((f32[16,128,128]{2,1,0:T(8,128)}), f32[16,128,128]{2,1,0:T(8,128)}, u32[]{:S(2)}, u32[]{:S(2)}) async-start(f32[16,128,128]{2,1,0:T(8,128)} %gather_fusion.5), calls=%async_computation.2 | async-start | bytes 2097152 | tf_op jit(solution)/shard_map/all_to_all | solution.py:124
  117.7 6.8 %collective-permute-start.2 = (f32[2176,1]{0,1:T(1,128)S(1)}, f32[2176,1]{0,1:T(1,128)S(1)}, u32[]{:S(2)}, u32[]{:S(2)}) collective-permute-start(f32[2176,1]{0,1:T(1,128)S(1)} %copy.35), channel_id=1, source_target_pairs={{0,1},{1,2},{2,3},{3,4},{4,5},{5,6},{6,7},{7,8},{8,9},{9,10},{10,1... | collective-permute-start | bytes 26120 | tf_op jit(solution)/shard_map/ppermute | solution.py:23
  121.6 5.4 %collective-permute-start.3 = (f32[2176,1]{0,1:T(1,128)S(1)}, f32[2176,1]{0,1:T(1,128)S(1)}, u32[]{:S(2)}, u32[]{:S(2)}) collective-permute-start(f32[2176,1]{0,1:T(1,128)S(1)} %copy.37), channel_id=1, source_target_pairs={{1,0},{2,1},{3,2},{4,3},{5,4},{6,5},{7,6},{8,7},{9,8},{10,9},{11,1... | collective-permute-start | bytes 26120 | tf_op jit(solution)/shard_map/ppermute | solution.py:24
  124.5 4.0 %copy-start.14 = (f32[128,128]{1,0:T(8,128)S(1)}, f32[128,128]{1,0:T(8,128)}, u32[]{:S(2)}) copy-start(f32[128,128]{1,0:T(8,128)} %get-tuple-element.11) | copy-start | bytes 196612
  124.5 4.0 %copy-start.15 = (f32[128,128]{1,0:T(8,128)S(1)}, f32[128,128]{1,0:T(8,128)}, u32[]{:S(2)}) copy-start(f32[128,128]{1,0:T(8,128)} %get-tuple-element.10) | copy-start | bytes 196612
  124.5 4.0 %copy-start.24 = (f32[1,128]{1,0:T(1,128)S(1)}, f32[1,128]{1,0:T(1,128)}, u32[]{:S(2)}) copy-start(f32[1,128]{1,0:T(1,128)} %param.30) | copy-start | bytes 1540
  147.0 7.6 %copy-start.23 = (f32[128]{0:T(128)S(1)}, f32[128]{0:T(128)}, u32[]{:S(2)}) copy-start(f32[128]{0:T(128)} %copy-done.22) | copy-start | bytes 1540
  157.7 23.4 %all-to-all-start.3 = ((f32[32,8,128]{2,1,0:T(8,128)}), f32[32,8,128]{2,1,0:T(8,128)S(1)}, u32[]{:S(2)}, u32[]{:S(2)}) async-start(f32[32,8,128]{2,1,0:T(8,128)} %get-tuple-element.15), calls=%async_computation.3 | async-start | bytes 262144 | tf_op jit(solution)/shard_map/all_to_all | solution.py:159
  174.0 1.2 copy-start.3
  175.3 5.9 %copy-start.12 = (f32[128,128]{1,0:T(8,128)S(1)}, f32[128,128]{1,0:T(8,128)}, u32[]{:S(2)}) copy-start(f32[128,128]{1,0:T(8,128)} %get-tuple-element.14) | copy-start | bytes 196612
  175.3 5.9 %copy-start.13 = (f32[128,128]{1,0:T(8,128)S(1)}, f32[128,128]{1,0:T(8,128)}, u32[]{:S(2)}) copy-start(f32[128,128]{1,0:T(8,128)} %get-tuple-element.13) | copy-start | bytes 196612

commit v10 on v8

--- a/solution.py
+++ b/solution.py
@@ -1,3 +1,4 @@
+import functools
 import math
 
 import jax
@@ -35,9 +36,9 @@
     return jnp.where(lane >= step, moved, fill)
 
 
-def scan_kernel(kept_ref, charge_ref, total_ref, state_ref, ends_ref):
+def scan_kernel(kept_ref, balance_ref, gain_ref, total_ref, state_ref, ends_ref, *, scale):
     kept = kept_ref[...]
-    state = charge_ref[...]
+    state = -gain_ref[...] * balance_ref[...] / scale
     lane = lax.broadcasted_iota(jnp.int32, kept.shape, 1)
     step = 1
     while step < kept.shape[1]:
@@ -52,10 +53,11 @@
     ends_ref[...] = jnp.where(row == 0, kept_end, jnp.where(row == 1, state_end, 0.0))
 
 
-def window_scan(kept, charge, copies):
+def window_scan(kept, balance, gain, scale, copies):
     shape = jax.ShapeDtypeStruct(kept.shape, jnp.float32)
     ends = jax.ShapeDtypeStruct((copies, 8, kept.shape[0]), jnp.float32)
-    return pl.pallas_call(scan_kernel, out_shape=(shape, shape, ends))(kept, charge)
+    kernel = functools.partial(scan_kernel, scale=scale)
+    return pl.pallas_call(kernel, out_shape=(shape, shape, ends))(kept, balance, gain)
 
 
 def carried_state(kept_last, state_last, position):
@@ -154,8 +156,9 @@
         padded = padded_2(dispatch, (("tm", 1),), 1)
         bend = padded[:, :-2] - 2.0 * dispatch + padded[:, 2:]
         dispatch_next = dispatch + dispatch_step * (balance - slope * dispatch) + ramp_local * bend
-        charge = -gain_local * balance[store_rows] / math.sqrt(year_hours)
-        kept_total, local_state, copies = window_scan(kept_local, charge, lax.axis_size("tm"))
+        kept_total, local_state, copies = window_scan(
+            kept_local, balance[store_rows], gain_local, math.sqrt(year_hours), lax.axis_size("tm")
+        )
         ends = lax.all_to_all(copies, "tm", split_axis=0, concat_axis=0, tiled=True)
         state_in = carried_state(ends[:, 0], ends[:, 1], position)
         charge_state = local_state + kept_total * state_in[:, None]

time: 182 us -> 182 us (level)
  local copies, waits for them, and re-layouts: 33.8 us -> 35.8 us
    unnamed x62 -> x58, local copies, waits for them, and re-layouts: 5.23 us -> 5.22 us
where the time goes in v10:
time: 182 us; the launch traced here: 181 us
  starting transfers between devices  53.9 us (30%)
  waiting for transfers between devices  40.6 us (22%)
  local copies, waits for them, and re-layouts  35.8 us (20%)
  other arithmetic  29.6 us (16%)
  matrix products  15 us (8%)
  Pallas kernels  5 us (3%)
    all_to_all x2, waiting for transfers between devices, exchanged(): got = lax.all_to_all(sent, 'area', split_axis=0, concat_axis=0, tiled=True)  34.8 us
    all_to_all x2, starting transfers between devices, local(): ends = lax.all_to_all(copies, 'tm', split_axis=0, concat_axis=0, tiled=True)  28.2 us
    all_to_all x2, starting transfers between devices, exchanged(): got = lax.all_to_all(sent, 'area', split_axis=0, concat_axis=0, tiled=True)  14.1 us
    dot_general x2, matrix products, local(): jnp.dot(matrix, rounded, preferred_element_type=jnp.float32) + fixed_part  13.6 us
    scatter-add x2, other arithmetic, local(): jnp.zeros((bus_count, hour_count), jnp.float32).at[edge_rows].add(tie_flow)  13.3 us
    gather x2, local copies, waits for them, and re-layouts, local(): own_edge = lax.optimization_barrier(rounded[edge_rows].astype(jnp.float32))  7.26 us
    ppermute x2, starting transfers between devices, padded_2(): before = lax.ppermute(last, axis, up)  5.84 us
    ppermute x2, starting transfers between devices, padded_2(): after = lax.ppermute(leading, axis, down)  5.75 us
  transfers between devices with their start and end apart: 8, of which 4 were waited for; matrix products, arithmetic and copies ran while one was open for 23% of the time, Pallas kernels for 0%

profile of v10, /device:TPU:1, one launch (start us, length us, event | category | flops | bytes accessed | tf_op | source)
XLA Modules:
  0.0 181.1 jit_solution(866864616210381291)
XLA Ops:
  0.7 0.9 dynamic-slice_reduce_fusion
  1.7 0.7 broadcast_clamp_fusion
  2.4 4.0 %gather_fusion = bf16[1024,128]{1,0:T(8,128)(2,1)S(1)} fusion(bf16[2176,128]{1,0:T(8,128)(2,1)} %bitcast.1246, s32[1024]{0:T(1024)S(1)} %broadcast_clamp_fusion), kind=kCustom, calls=%fused_computation | custom fusion | bytes 528384 | tf_op jit(solution)/shard_map/gather | solution.py:141
  6.6 0.6 copy-done.18
  7.3 2.0 %gather_fusion.1 = f32[16,264,128]{2,1,0:T(8,128)} fusion(f32[8,264,128]{2,1,0:T(8,128)S(1)} %select_maximum_fusion, s32[1024]{0:T(1024)S(1)} %pad_clamp_fusion.2), kind=kCustom, calls=%fused_computation.1 | custom fusion | bytes 4325440 | tf_op jit(solution)/shard_map/jit(_take)/gather | solution.py:125
  9.3 9.7 %all-to-all-start = ((f32[16,264,128]{2,1,0:T(8,128)}), f32[16,264,128]{2,1,0:T(8,128)}, u32[]{:S(2)}, u32[]{:S(2)}) async-start(f32[16,264,128]{2,1,0:T(8,128)} %gather_fusion.1), calls=%async_computation | async-start | bytes 4325376 | tf_op jit(solution)/shard_map/all_to_all | solution.py:126
  19.5 0.6 copy-done.2
  20.5 3.6 %collective-permute-start.1 = (f32[2176,1]{0,1:T(1,128)S(1)}, f32[2176,1]{0,1:T(1,128)S(1)}, u32[]{:S(2)}, u32[]{:S(2)}) collective-permute-start(f32[2176,1]{0,1:T(1,128)S(1)} %copy.37), channel_id=1, source_target_pairs={{1,0},{2,1},{3,2},{4,3},{5,4},{6,5},{7,6},{8,7},{9,8},{10,9},{11,1... | collective-permute-start | bytes 26120 | tf_op jit(solution)/shard_map/ppermute | solution.py:25
  24.5 2.3 %collective-permute-start = (f32[2176,1]{0,1:T(1,128)S(1)}, f32[2176,1]{0,1:T(1,128)S(1)}, u32[]{:S(2)}, u32[]{:S(2)}) collective-permute-start(f32[2176,1]{0,1:T(1,128)S(1)} %copy.35), channel_id=1, source_target_pairs={{0,1},{1,2},{2,3},{3,4},{4,5},{5,6},{6,7},{7,8},{8,9},{9,10},{10,1... | collective-permute-start | bytes 26120 | tf_op jit(solution)/shard_map/ppermute | solution.py:24
  26.9 6.6 %fusion.10 = f32[2176,128]{1,0:T(8,128)S(1)} fusion(bf16[1,2176,2176]{2,1,0:T(8,128)(2,1)} %param.20, bf16[1,2176,128]{2,1,0:T(8,128)(2,1)} %param.17, bf16[1,2176,128]{2,1,0:T(8,128)(2,1)} %param.18, bf16[1,2176,128]{2,1,0:T(8,128)(2,1)S(1)} %copy-done.1), kind=kOutput, calls=%fused_computation.17 | convolution fusion | flops 1213267968 | bytes 12255232 | tf_op jit(solution)/shard_map/dot_general | solution.py:155
  33.6 0.7 copy.39.gain_ref
  34.4 1.4 copy.36
  35.8 1.4 copy.38
  37.2 31.4 %all-to-all-done = f32[16,264,128]{2,1,0:T(8,128)} async-done(((f32[16,264,128]{2,1,0:T(8,128)}), f32[16,264,128]{2,1,0:T(8,128)}, u32[]{:S(2)}, u32[]{:S(2)}) %all-to-all-start) | async-done | bytes 2162720 | tf_op jit(solution)/shard_map/all_to_all | solution.py:126
  68.5 2.2 %gather_fusion.2 = f32[8,264,128]{2,1,0:T(8,128)S(1)} fusion(f32[16,264,128]{2,1,0:T(8,128)} %all-to-all-done, s32[1024]{0:T(1024)S(1)} %pad_clamp_fusion.1), kind=kCustom, calls=%fused_computation.2 | custom fusion | bytes 2162720 | tf_op jit(solution)/shard_map/jit(_take)/gather | solution.py:127
  71.0 0.9 copy-done.10
  73.0 6.4 %scatter_fusion = f32[2176,128]{1,0:T(8,128)S(1)} fusion(f32[2176,128]{1,0:T(8,128)S(1)} %fusion.10, s32[1024]{0:T(1024)S(1)} %fusion.44, f32[1024,128]{1,0:T(8,128)S(1)} %bitcast.1255), kind=kCustom, calls=%fused_computation.8 | custom fusion | flops 131072 | bytes 1576960 | tf_op jit(solution)/shard_map/scatter-add | solution.py:153
  79.5 1.2 gather_fusion.3
  80.7 2.5 %shard_map.183 = (f32[128,128]{1,0:T(8,128)}, f32[128,128]{1,0:T(8,128)}, f32[32,8,128]{2,1,0:T(8,128)}) custom-call(f32[128,128]{1,0:T(8,128)} %bitcast.1258, f32[128,128]{1,0:T(8,128)} %gather_fusion.3, f32[128,1]{1,0:T(8,128)} %copy.39.gain_ref), custom_call_target="tpu_custom_call" | custom-call | tf_op jit(solution)/shard_map/pallas_call | solution.py:60
  83.2 15.5 %all-to-all-start.1 = ((f32[32,8,128]{2,1,0:T(8,128)}), f32[32,8,128]{2,1,0:T(8,128)S(1)}, u32[]{:S(2)}, u32[]{:S(2)}) async-start(f32[32,8,128]{2,1,0:T(8,128)} %get-tuple-element.12), calls=%async_computation.1 | async-start | bytes 262144 | tf_op jit(solution)/shard_map/all_to_all | solution.py:162
  98.7 3.8 %fusion.21 = (f32[2176,128]{1,0:T(8,128)S(1)}, bf16[2176,128]{1,0:T(8,128)(2,1)S(1)}) fusion(f32[2176,1]{1,0:T(8,128)} %copy.38, f32[2176,128]{1,0:T(8,128)} %copy-done.2, f32[2176,1]{1,0:T(8,128)} %copy.36, f32[2176,128]{1,0:T(8,128)S(1)} %scatter_fusion, bf16[1,2176,128]{2,1,0:T(8,128)(2,1)} %param.17, f32[2176]{0:T(1024)S(1)} %reduce.2, f32[2176]{0:T(1024)S(1)} %reduce.1), kind=kLoop, calls=%fused_computation.31 | loop fusion | flops 3620864 | bytes 4491264 | tf_op jit(solution)/shard_map/add | solution.py:158
  102.5 1.1 fusion.26
  103.6 1.0 copy-done.3
  104.7 3.2 %gather_fusion.4 = bf16[1024,128]{1,0:T(8,128)(2,1)S(1)} fusion(bf16[2176,128]{1,0:T(8,128)(2,1)S(1)} %fusion.23, s32[1024]{0:T(1024)S(1)} %broadcast_clamp_fusion), kind=kCustom, calls=%fused_computation.4 | custom fusion | bytes 528384 | tf_op jit(solution)/shard_map/gather | solution.py:141
  108.0 1.6 gather_fusion.5
  109.6 4.4 %all-to-all-start.2 = ((f32[16,128,128]{2,1,0:T(8,128)}), f32[16,128,128]{2,1,0:T(8,128)}, u32[]{:S(2)}, u32[]{:S(2)}) async-start(f32[16,128,128]{2,1,0:T(8,128)} %gather_fusion.5), calls=%async_computation.2 | async-start | bytes 2097152 | tf_op jit(solution)/shard_map/all_to_all | solution.py:126
  114.0 1.3 fusion.173
  115.3 1.6 copy.40
  116.9 3.6 %collective-permute-start.2 = (f32[2176,1]{0,1:T(1,128)S(1)}, f32[2176,1]{0,1:T(1,128)S(1)}, u32[]{:S(2)}, u32[]{:S(2)}) collective-permute-start(f32[2176,1]{0,1:T(1,128)S(1)} %copy.40), channel_id=1, source_target_pairs={{0,1},{1,2},{2,3},{3,4},{4,5},{5,6},{6,7},{7,8},{8,9},{9,10},{10,1... | collective-permute-start | bytes 26120 | tf_op jit(solution)/shard_map/ppermute | solution.py:24
  120.8 2.1 %collective-permute-start.3 = (f32[2176,1]{0,1:T(1,128)S(1)}, f32[2176,1]{0,1:T(1,128)S(1)}, u32[]{:S(2)}, u32[]{:S(2)}) collective-permute-start(f32[2176,1]{0,1:T(1,128)S(1)} %copy.42), channel_id=1, source_target_pairs={{1,0},{2,1},{3,2},{4,3},{5,4},{6,5},{7,6},{8,7},{9,8},{10,9},{11,1... | collective-permute-start | bytes 26120 | tf_op jit(solution)/shard_map/ppermute | solution.py:25
  123.0 0.7 slice.911
  123.7 1.4 copy.41
  125.1 1.1 collective-permute-done.3
  126.2 1.4 copy.43
  127.7 2.3 %scatter_custom_fusion.1 = f32[2176,128]{1,0:T(8,128)} fusion(s32[128]{0:T(128)} %copy-done.26, f32[]{:T(128)} %constant.41.clone.1, f32[128,128]{1,0:T(8,128)S(1)} %copy-done.17, f32[128,128]{1,0:T(8,128)S(1)} %copy-done.16, f32[128]{0:T(128)S(1)} %broadcast_select_fusion.63, f32[128]{0:T(128)S(1)} %bitcast.1265), kind=kCustom, calls=%fused_computation.53 | custom fusion | flops 65536 | bytes 1246720 | tf_op jit(solution)/shard_map/scatter-add | solution.py:168
  130.0 7.0 %fusion.7 = f32[2176,128]{1,0:T(8,128)S(1)} fusion(bf16[2176,128]{1,0:T(8,128)(2,1)} %bitcast.1251, bf16[1,2176,2176]{2,1,0:T(8,128)(2,1)} %param.20, f32[2176,128]{1,0:T(8,128)} %scatter_custom_fusion.1, f32[2176,128]{1,0:T(8,128)S(1)} %get-tuple-element.33, bf16[1,2176,128]{2,1,0:T(8,128)(2,1)} %param.18), kind=kOutput, calls=%fused_computation.16 | convolution fusion | flops 1213267968 | bytes 13926400 | tf_op jit(solution)/shard_map/dot_general | solution.py:155
  136.9 3.5 %all-to-all-done.2 = f32[16,128,128]{2,1,0:T(8,128)} async-done(((f32[16,128,128]{2,1,0:T(8,128)}), f32[16,128,128]{2,1,0:T(8,128)}, u32[]{:S(2)}, u32[]{:S(2)}) %all-to-all-start.2) | async-done | bytes 1048608 | tf_op jit(solution)/shard_map/all_to_all | solution.py:126
  140.4 2.6 %gather_fusion.6 = f32[8,128,128]{2,1,0:T(8,128)} fusion(f32[16,128,128]{2,1,0:T(8,128)} %all-to-all-done.2, s32[1024]{0:T(1024)S(1)} %pad_clamp_fusion.1), kind=kCustom, calls=%fused_computation.6 | custom fusion | bytes 1048608 | tf_op jit(solution)/shard_map/jit(_take)/gather | solution.py:127
  143.0 3.2 %add_bitcast_fusion = (f32[1,8,128,128]{3,2,1,0:T(8,128)}, f32[8,128,128]{2,1,0:T(8,128)}) fusion(bf16[1,8,128,128]{3,2,1,0:T(8,128)(2,1)} %param.19, f32[8,128]{1,0:T(8,128)S(1)} %bitcast.1261, f32[8,128,128]{2,1,0:T(8,128)} %copy-done.5, f32[8,128,128]{2,1,0:T(8,128)} %gather_fusion.6, f32[8,128,128]{2,1,0:T(8,128)} %copy-done.6, ...), kind=kLoop, calls=%fused_computation.66 | loop fusion | flops 1703936 | bytes 3944448 | tf_op jit(solution)/shard_map/broadcast_in_dim | solution.py:180
  146.2 6.8 %scatter_fusion.1 = f32[2176,128]{1,0:T(8,128)S(1)} fusion(f32[2176,128]{1,0:T(8,128)S(1)} %fusion.7, s32[1024]{0:T(1024)S(1)} %fusion.44, f32[1024,128]{1,0:T(8,128)} %bitcast.1254), kind=kCustom, calls=%fused_computation.10 | custom fusion | flops 131072 | bytes 1576960 | tf_op jit(solution)/shard_map/scatter-add | solution.py:153
  153.1 1.4 gather_fusion.7
  154.4 2.5 %shard_map.184 = (f32[128,128]{1,0:T(8,128)}, f32[128,128]{1,0:T(8,128)}, f32[32,8,128]{2,1,0:T(8,128)}) custom-call(f32[128,128]{1,0:T(8,128)} %bitcast.1259, f32[128,128]{1,0:T(8,128)} %gather_fusion.7, f32[128,1]{1,0:T(8,128)} %copy.39.gain_ref), custom_call_target="tpu_custom_call" | custom-call | tf_op jit(solution)/shard_map/pallas_call | solution.py:60
  156.9 12.7 %all-to-all-start.3 = ((f32[32,8,128]{2,1,0:T(8,128)}), f32[32,8,128]{2,1,0:T(8,128)S(1)}, u32[]{:S(2)}, u32[]{:S(2)}) async-start(f32[32,8,128]{2,1,0:T(8,128)} %get-tuple-element.15), calls=%async_computation.3 | async-start | bytes 262144 | tf_op jit(solution)/shard_map/all_to_all | solution.py:162
  169.6 3.6 %fusion.33 = (bf16[1,2176,128]{2,1,0:T(8,128)(2,1)}, bf16[2176,128]{1,0:T(8,128)(2,1)S(1)}) fusion(f32[2176,1]{1,0:T(8,128)} %copy.43, f32[2176,128]{1,0:T(8,128)S(1)} %get-tuple-element.33, f32[2176,1]{1,0:T(8,128)} %copy.41, f32[2176]{0:T(1024)S(1)} %reduce.2, f32[2176,128]{1,0:T(8,128)S(1)} %scatter_fusion.1, f32[2176]{0:T(1024)S(1)} %reduce.1), kind=kLoop, calls=%fused_computation.55 | loop fusion | flops 3620864 | bytes 3377152 | tf_op jit(solution)/shard_map/broadcast_in_dim | solution.py:179
  173.5 1.0 copy-done.4
  174.5 1.1 bitcast_subtract_fusion
  175.6 4.7 %all-to-all-done.3 = f32[32,8,128]{2,1,0:T(8,128)S(1)} async-done(((f32[32,8,128]{2,1,0:T(8,128)}), f32[32,8,128]{2,1,0:T(8,128)S(1)}, u32[]{:S(2)}, u32[]{:S(2)}) %all-to-all-start.3) | async-done | bytes 131104 | tf_op jit(solution)/shard_map/all_to_all | solution.py:162
  180.4 0.7 add_bitcast_fusion.1
  (79 shorter events, 3.8 us)
Async XLA Ops:
  0.6 101.9 %copy-start = (bf16[1,34,64,64]{3,2,1,0:T(8,128)(2,1)S(1)}, bf16[1,34,64,64]{3,2,1,0:T(8,128)(2,1)}, u32[]{:S(2)}) copy-start(bf16[1,34,64,64]{3,2,1,0:T(8,128)(2,1)} %param.21) | copy-start | bytes 835588
  2.4 4.1 %copy-start.11 = (bf16[1,8,128,128]{3,2,1,0:T(8,128)(2,1)S(1)}, bf16[1,8,128,128]{3,2,1,0:T(8,128)(2,1)}, u32[]{:S(2)}) copy-start(bf16[1,8,128,128]{3,2,1,0:T(8,128)(2,1)} %param.19) | copy-start | bytes 786436
  6.4 0.7 copy-start.18
  6.5 0.8 copy-start.6
  9.3 9.8 %copy-start.13 = (bf16[1,2176,128]{2,1,0:T(8,128)(2,1)S(1)}, bf16[1,2176,128]{2,1,0:T(8,128)(2,1)}, u32[]{:S(2)}) copy-start(bf16[1,2176,128]{2,1,0:T(8,128)(2,1)} %param.17) | copy-start | bytes 1671172
  9.3 59.2 %all-to-all-start = ((f32[16,264,128]{2,1,0:T(8,128)}), f32[16,264,128]{2,1,0:T(8,128)}, u32[]{:S(2)}, u32[]{:S(2)}) async-start(f32[16,264,128]{2,1,0:T(8,128)} %gather_fusion.1), calls=%async_computation | async-start | bytes 4325376 | tf_op jit(solution)/shard_map/all_to_all | solution.py:126
  19.2 1.0 copy-start.2
  20.2 6.6 %copy-start.27 = (s32[1,128]{1,0:T(1,128)S(1)}, s32[1,128]{1,0:T(1,128)}, u32[]{:S(2)}) copy-start(s32[1,128]{1,0:T(1,128)} %param.28) | copy-start | bytes 1540
  20.2 6.7 %copy-start.20 = (s32[1,8,128]{2,1,0:T(8,128)S(1)}, s32[1,8,128]{2,1,0:T(8,128)}, u32[]{:S(2)}) copy-start(s32[1,8,128]{2,1,0:T(8,128)} %param.25) | copy-start | bytes 12292
  20.2 6.7 %copy-start.1 = (bf16[1,2176,128]{2,1,0:T(8,128)(2,1)S(1)}, bf16[1,2176,128]{2,1,0:T(8,128)(2,1)}, u32[]{:S(2)}) copy-start(bf16[1,2176,128]{2,1,0:T(8,128)(2,1)} %param.16) | copy-start | bytes 1671172
  20.5 15.3 %collective-permute-start.1 = (f32[2176,1]{0,1:T(1,128)S(1)}, f32[2176,1]{0,1:T(1,128)S(1)}, u32[]{:S(2)}, u32[]{:S(2)}) collective-permute-start(f32[2176,1]{0,1:T(1,128)S(1)} %copy.37), channel_id=1, source_target_pairs={{1,0},{2,1},{3,2},{4,3},{5,4},{6,5},{7,6},{8,7},{9,8},{10,9},{11,1... | collective-permute-start | bytes 26120 | tf_op jit(solution)/shard_map/ppermute | solution.py:25
  24.5 9.9 %collective-permute-start = (f32[2176,1]{0,1:T(1,128)S(1)}, f32[2176,1]{0,1:T(1,128)S(1)}, u32[]{:S(2)}, u32[]{:S(2)}) collective-permute-start(f32[2176,1]{0,1:T(1,128)S(1)} %copy.35), channel_id=1, source_target_pairs={{0,1},{1,2},{2,3},{3,4},{4,5},{5,6},{6,7},{7,8},{8,9},{9,10},{10,1... | collective-permute-start | bytes 26120 | tf_op jit(solution)/shard_map/ppermute | solution.py:24
  26.8 6.7 %copy-start.26 = (s32[128]{0:T(128)}, s32[128]{0:T(128)S(1)}, u32[]{:S(2)}) copy-start(s32[128]{0:T(128)S(1)} %fusion.47) | copy-start | bytes 1540
  26.9 6.7 %copy-start.21 = (f32[1,2176]{1,0:T(1,128)S(1)}, f32[1,2176]{1,0:T(1,128)}, u32[]{:S(2)}) copy-start(f32[1,2176]{1,0:T(1,128)} %param.22) | copy-start | bytes 26116
  26.9 6.7 %copy-start.22 = (f32[1,2176]{1,0:T(1,128)S(1)}, f32[1,2176]{1,0:T(1,128)}, u32[]{:S(2)}) copy-start(f32[1,2176]{1,0:T(1,128)} %param.23) | copy-start | bytes 26116
  26.9 6.7 %copy-start.24 = (f32[1,128]{1,0:T(1,128)S(1)}, f32[1,128]{1,0:T(1,128)}, u32[]{:S(2)}) copy-start(f32[1,128]{1,0:T(1,128)} %param.29) | copy-start | bytes 1540
  33.5 45.9 %copy-start.23 = (s32[1024]{0:T(1024)}, s32[1024]{0:T(1024)S(1)}, u32[]{:S(2)}) copy-start(s32[1024]{0:T(1024)S(1)} %pad_clamp_fusion) | copy-start | bytes 12292
  71.0 1.0 copy-start.10
  71.0 1.4 copy-start.7
  71.0 1.5 copy-start.12
  71.0 1.5 copy-start.19
  72.0 0.8 copy-start.8
  72.0 1.0 copy-start.9
  83.2 26.4 %all-to-all-start.1 = ((f32[32,8,128]{2,1,0:T(8,128)}), f32[32,8,128]{2,1,0:T(8,128)S(1)}, u32[]{:S(2)}, u32[]{:S(2)}) async-start(f32[32,8,128]{2,1,0:T(8,128)} %get-tuple-element.12), calls=%async_computation.1 | async-start | bytes 262144 | tf_op jit(solution)/shard_map/all_to_all | solution.py:162
  103.6 1.0 copy-start.3
  108.0 1.6 copy-start.5
  109.6 30.8 %all-to-all-start.2 = ((f32[16,128,128]{2,1,0:T(8,128)}), f32[16,128,128]{2,1,0:T(8,128)}, u32[]{:S(2)}, u32[]{:S(2)}) async-start(f32[16,128,128]{2,1,0:T(8,128)} %gather_fusion.5), calls=%async_computation.2 | async-start | bytes 2097152 | tf_op jit(solution)/shard_map/all_to_all | solution.py:126
  116.9 6.8 %collective-permute-start.2 = (f32[2176,1]{0,1:T(1,128)S(1)}, f32[2176,1]{0,1:T(1,128)S(1)}, u32[]{:S(2)}, u32[]{:S(2)}) collective-permute-start(f32[2176,1]{0,1:T(1,128)S(1)} %copy.40), channel_id=1, source_target_pairs={{0,1},{1,2},{2,3},{3,4},{4,5},{5,6},{6,7},{7,8},{8,9},{9,10},{10,1... | collective-permute-start | bytes 26120 | tf_op jit(solution)/shard_map/ppermute | solution.py:24
  120.8 5.4 %collective-permute-start.3 = (f32[2176,1]{0,1:T(1,128)S(1)}, f32[2176,1]{0,1:T(1,128)S(1)}, u32[]{:S(2)}, u32[]{:S(2)}) collective-permute-start(f32[2176,1]{0,1:T(1,128)S(1)} %copy.42), channel_id=1, source_target_pairs={{1,0},{2,1},{3,2},{4,3},{5,4},{6,5},{7,6},{8,7},{9,8},{10,9},{11,1... | collective-permute-start | bytes 26120 | tf_op jit(solution)/shard_map/ppermute | solution.py:25
  123.7 4.0 %copy-start.16 = (f32[128,128]{1,0:T(8,128)S(1)}, f32[128,128]{1,0:T(8,128)}, u32[]{:S(2)}) copy-start(f32[128,128]{1,0:T(8,128)} %get-tuple-element.11) | copy-start | bytes 196612
  123.7 4.0 %copy-start.17 = (f32[128,128]{1,0:T(8,128)S(1)}, f32[128,128]{1,0:T(8,128)}, u32[]{:S(2)}) copy-start(f32[128,128]{1,0:T(8,128)} %get-tuple-element.10) | copy-start | bytes 196612
  123.7 4.0 %copy-start.25 = (f32[1,128]{1,0:T(1,128)S(1)}, f32[1,128]{1,0:T(1,128)}, u32[]{:S(2)}) copy-start(f32[1,128]{1,0:T(1,128)} %param.30) | copy-start | bytes 1540
  156.9 23.4 %all-to-all-start.3 = ((f32[32,8,128]{2,1,0:T(8,128)}), f32[32,8,128]{2,1,0:T(8,128)S(1)}, u32[]{:S(2)}, u32[]{:S(2)}) async-start(f32[32,8,128]{2,1,0:T(8,128)} %get-tuple-element.15), calls=%async_computation.3 | async-start | bytes 262144 | tf_op jit(solution)/shard_map/all_to_all | solution.py:162
  173.2 1.2 copy-start.4
  174.5 5.9 %copy-start.14 = (f32[128,128]{1,0:T(8,128)S(1)}, f32[128,128]{1,0:T(8,128)}, u32[]{:S(2)}) copy-start(f32[128,128]{1,0:T(8,128)} %get-tuple-element.14) | copy-start | bytes 196612
  174.5 5.9 %copy-start.15 = (f32[128,128]{1,0:T(8,128)S(1)}, f32[128,128]{1,0:T(8,128)}, u32[]{:S(2)}) copy-start(f32[128,128]{1,0:T(8,128)} %get-tuple-element.13) | copy-start | bytes 196612
